TPU v7x, 32 devices: a whole 2x2x4 slice. The times are simulated.
32 devices in a mesh: section: 2 (over core), fsdp: 2 (over y), expert: 8 (over z, x).
Axes of the slice: x: 2, y: 2, z: 4, core: 2. Of those that a mesh axis runs over, the one named last changes fastest.
Arguments:
- tokens: bfloat16 [2048, 2048], P(('fsdp', 'expert')), may hold values from -40 to 40
- norm_gain: float32 [2, 2048], P('section'), may hold values from 0.5 to 1.5
- router: bfloat16 [2, 2048, 32], P('section'), may hold values from -0.3125 to 0.3125
- w_gate: bfloat16 [2, 32, 2048, 768], P('section', 'expert', 'fsdp'), may hold values from -0.125 to 0.125
- w_up: bfloat16 [2, 32, 2048, 768], P('section', 'expert', 'fsdp'), may hold values from -0.125 to 0.125
- w_down: bfloat16 [2, 32, 768, 2048], P('section', 'expert', None, 'fsdp'), may hold values from -0.21875 to 0.21875
- routes: int32 [2, 2048, 6], P('section', ('fsdp', 'expert')), may hold values from 0 to 31, all different within a row; in each aligned block of 64 rows (0 to 63, 64 to 127, ..., all dimensions but the last counted through in order) at most 14 rows name the same one
Outputs:
- final_out: bfloat16 [2048, 2048], P(('fsdp', 'expert'), 'section')
- layer_stats: float32 [2], P('section')
Inputs may be any that keep to these rules, and one draw needn't show every extreme that they name: `routes`: each row names 6 different experts; in every aligned block of 64 rows of one layer no expert is named by more than 14 rows, a bound that some block reaches.
All inputs are finite; a program needn't handle non-finite values.
Results may differ from a plain program's by a relative error of at most 0.0065.
Values may be sent and summed in bfloat16 or wider, within the bound.
No kernel may reach another device: no remote copies, remote signals or barrier semaphores. Data moves between devices by JAX's collectives and lax.ppermute only.
A program may use at most 192 MiB of HBM per device.

v0:
```python
import jax
import jax.numpy as jnp
from jax import lax
from jax.sharding import PartitionSpec as P

TOP = 6
BLOCK = 64


epsilon = 1e-06


def other_section(value):
    return lax.ppermute(value, "section", [(0, 1), (1, 0)])


def ring_pairs(count, shift):
    return [(source, (source + shift) % count) for source in range(count)]


def rms_scaled(hidden_rows, gain_row):
    values = hidden_rows.astype(jnp.float32)
    scale = lax.rsqrt(jnp.mean(values * values, axis=-1, keepdims=True) + epsilon)
    return (values * scale * gain_row).astype(jnp.bfloat16)


def gate_weights(normed, router_weight, route_rows):
    logits = jnp.dot(normed, router_weight, preferred_element_type=jnp.float32)
    scores = jax.nn.sigmoid(logits)
    expert_ids = jnp.arange(router_weight.shape[1], dtype=jnp.int32)
    chosen_mask = (route_rows[:, :, None] == expert_ids[None, None, :]).astype(jnp.float32)
    chosen = jnp.sum(scores[:, None, :] * chosen_mask, axis=2)
    return chosen / jnp.sum(chosen, axis=1, keepdims=True)


def slot_positions(route_rows, experts_count, capacity):
    flat_routes = route_rows.reshape(-1)
    onehot = (flat_routes[:, None] == jnp.arange(experts_count, dtype=jnp.int32)[None, :]).astype(
        jnp.int32
    )
    before = jnp.cumsum(onehot, axis=0) - onehot
    slot_index = jnp.sum(before * onehot, axis=1)
    return (flat_routes * capacity + slot_index).reshape(route_rows.shape)


def other_half(value):
    return lax.ppermute(value, "zhalf", [(0, 1), (1, 0)])


def half_buffer(positions, normed, slot_ids, fsdp_count, chunk):
    placing = jnp.any(positions[:, :, None] == slot_ids[None, None, :], axis=1).astype(jnp.bfloat16)
    return jnp.einsum(
        "rs,rfd->fsd",
        placing,
        normed.reshape(normed.shape[0], fsdp_count, chunk),
        preferred_element_type=jnp.float32,
    ).astype(jnp.bfloat16)


def expert_layer(entering, route_rows, gain_row, router_weight, weights, capacity):
    gate_w, up_w, down_w = weights
    rows, width = entering.shape
    experts_count = router_weight.shape[1]
    local_experts, chunk, hidden_units = gate_w.shape
    fsdp_count = lax.axis_size("fsdp")
    halves = lax.axis_size("zhalf")
    inner_devices = lax.axis_size("inner")
    half_index = lax.axis_index("zhalf")
    fsdp_index = lax.axis_index("fsdp")
    partner_entering = other_half(entering)
    partner_routes = other_half(route_rows)
    normed = rms_scaled(entering, gain_row)
    partner_normed = rms_scaled(partner_entering, gain_row)
    mix_weights = gate_weights(normed, router_weight, route_rows)
    positions = slot_positions(route_rows, experts_count, capacity)
    partner_positions = slot_positions(partner_routes, experts_count, capacity)
    half_slots = experts_count // halves * capacity
    local_ids = half_index * half_slots + jnp.arange(half_slots, dtype=jnp.int32)
    first_half = half_index == 0
    lower_normed = jnp.where(first_half, normed, partner_normed)
    upper_normed = jnp.where(first_half, partner_normed, normed)
    lower_positions = jnp.where(first_half, positions, partner_positions)
    upper_positions = jnp.where(first_half, partner_positions, positions)
    lower_buffer = half_buffer(lower_positions, lower_normed, local_ids, fsdp_count, chunk)
    upper_buffer = half_buffer(upper_positions, upper_normed, local_ids, fsdp_count, chunk)
    group_slots = local_experts * capacity
    outgoing = jnp.stack(
        [
            lower_buffer.reshape(fsdp_count, inner_devices, group_slots, chunk),
            upper_buffer.reshape(fsdp_count, inner_devices, group_slots, chunk),
        ],
        axis=2,
    ).reshape(fsdp_count * inner_devices, halves * group_slots, chunk)
    arrived = lax.all_to_all(outgoing, ("fsdp", "inner"), 0, 0, tiled=True)
    sources = fsdp_count * inner_devices * halves
    arrived = arrived.reshape(sources, local_experts, capacity, chunk)
    gate_part = jnp.einsum("sjcd,jdh->sjch", arrived, gate_w, preferred_element_type=jnp.float32)
    up_part = jnp.einsum("sjcd,jdh->sjch", arrived, up_w, preferred_element_type=jnp.float32)
    block_shape = (fsdp_count, sources // fsdp_count, local_experts, capacity, hidden_units)
    gate_blocks = gate_part.reshape(block_shape)
    up_blocks = up_part.reshape(block_shape)
    gate_sum = lax.dynamic_index_in_dim(gate_blocks, fsdp_index, 0, keepdims=False)
    up_sum = lax.dynamic_index_in_dim(up_blocks, fsdp_index, 0, keepdims=False)
    for shift in range(1, fsdp_count):
        target = (fsdp_index + shift) % fsdp_count
        outgoing_pair = jnp.stack(
            [
                lax.dynamic_index_in_dim(gate_blocks, target, 0, keepdims=False),
                lax.dynamic_index_in_dim(up_blocks, target, 0, keepdims=False),
            ]
        ).astype(jnp.bfloat16)
        got = lax.ppermute(outgoing_pair, "fsdp", ring_pairs(fsdp_count, shift))
        gate_sum = gate_sum + got[0].astype(jnp.float32)
        up_sum = up_sum + got[1].astype(jnp.float32)
    inner_act = (jax.nn.silu(gate_sum) * up_sum).astype(jnp.bfloat16)
    inner_pieces = [inner_act]
    for shift in range(1, fsdp_count):
        inner_pieces.append(lax.ppermute(inner_act, "fsdp", ring_pairs(fsdp_count, shift)))
    order = (fsdp_index - jnp.arange(fsdp_count, dtype=jnp.int32)) % fsdp_count
    inner_all = jnp.take(jnp.stack(inner_pieces), order, axis=0).reshape(
        sources, local_experts, capacity, hidden_units
    )
    inner_all = inner_all.reshape(
        fsdp_count, inner_devices, halves, local_experts, capacity, hidden_units
    )
    sending = jnp.einsum(
        "fipjch,jhd->fpijcd", inner_all, down_w, preferred_element_type=jnp.float32
    ).astype(jnp.bfloat16)
    returned = lax.all_to_all(
        sending.reshape(sources, group_slots, chunk),
        ("fsdp", "zhalf", "inner"),
        0,
        0,
        tiled=True,
    )
    slot_ids = jnp.arange(experts_count * capacity, dtype=jnp.int32)
    hits = positions[:, :, None] == slot_ids[None, None, :]
    combining = jnp.sum(jnp.where(hits, mix_weights[:, :, None], 0.0), axis=1)
    branch_sum = jnp.einsum(
        "rs,fsd->rfd",
        combining,
        returned.reshape(fsdp_count, experts_count * capacity, chunk).astype(jnp.float32),
        precision=lax.Precision.HIGHEST,
        preferred_element_type=jnp.float32,
    ).reshape(rows, width)
    return (entering.astype(jnp.float32) + branch_sum).astype(jnp.bfloat16)


def body(tokens, norm_gain, router, w_gate, w_up, w_down, routes):
    section_index = lax.axis_index("section")
    sections = lax.axis_size("section")
    token_rows, width = tokens.shape
    piece = token_rows // sections
    experts_count = router.shape[2]
    block_capacity = (7 * BLOCK * TOP + 6 * experts_count - 1) // (6 * experts_count)
    capacity = block_capacity * (piece // BLOCK)
    own_weights = (w_gate[0], w_up[0], w_down[0])
    other_weights = tuple(other_section(w) for w in own_weights)
    own_small = (norm_gain[0], router[0], routes[0])
    other_small = tuple(other_section(v) for v in own_small)
    hidden = lax.dynamic_slice_in_dim(tokens, section_index * piece, piece, 0)
    squares = []
    for layer in range(sections):
        mine = section_index == layer
        gain_row, router_weight, route_all = [
            jnp.where(mine, a, b) for a, b in zip(own_small, other_small)
        ]
        weights = tuple(jnp.where(mine, a, b) for a, b in zip(own_weights, other_weights))
        route_rows = lax.dynamic_slice_in_dim(route_all, section_index * piece, piece, 0)
        hidden = expert_layer(hidden, route_rows, gain_row, router_weight, weights, capacity)
        values = hidden.astype(jnp.float32)
        squares.append(jnp.sum(values * values))
    everyone = ("section", "fsdp", "zhalf", "inner")
    expert_devices = lax.axis_size("zhalf") * lax.axis_size("inner")
    device_count = sections * lax.axis_size("fsdp") * expert_devices
    square_rows = jnp.broadcast_to(jnp.stack(squares)[None, :], (device_count, sections))
    totals = jnp.sum(lax.all_to_all(square_rows, everyone, 0, 0, tiled=True), axis=0)
    token_total = token_rows * lax.axis_size("fsdp") * expert_devices
    stats = jnp.sqrt(totals / (token_total * width))
    layer_stats = lax.dynamic_slice_in_dim(stats, section_index, 1, 0)
    half_width = width // 2
    keep = lax.dynamic_slice_in_dim(hidden, section_index * half_width, half_width, 1)
    send = lax.dynamic_slice_in_dim(hidden, (1 - section_index) * half_width, half_width, 1)
    arrived = other_section(send)
    final_out = jnp.where(
        section_index == 0,
        jnp.concatenate([keep, arrived], axis=0),
        jnp.concatenate([arrived, keep], axis=0),
    )
    return (final_out, layer_stats)


def solution(mesh):
    sizes = dict(zip(mesh.axis_names, mesh.devices.shape))
    devices = mesh.devices.reshape(
        sizes["section"], sizes["fsdp"], 2, sizes["expert"] // 2
    )
    split_mesh = jax.sharding.Mesh(devices, ("section", "fsdp", "zhalf", "inner"))
    tokens_axes = ("fsdp", "zhalf", "inner")
    experts_axes = ("zhalf", "inner")
    in_specs = (
        P(tokens_axes, None),
        P("section", None),
        P("section", None, None),
        P("section", experts_axes, "fsdp", None),
        P("section", experts_axes, "fsdp", None),
        P("section", experts_axes, None, "fsdp"),
        P("section", tokens_axes, None),
    )
    out_specs = (P(tokens_axes, "section"), P("section"))
    return jax.shard_map(
        body, mesh=split_mesh, in_specs=in_specs, out_specs=out_specs, check_vma=False
    )
```

profile of v0, /device:TPU:0, one launch (start us, length us, event | category | flops | bytes accessed | tf_op | source)
XLA Modules:
  0.0 354.4 jit_solution(4420653212089347265)
XLA Ops:
  3.7 3.7 %collective-permute-start.5 = (bf16[64,2048]{1,0:T(8,128)(2,1)S(1)}, bf16[64,2048]{1,0:T(8,128)(2,1)S(1)}, u32[]{:S(2)}, u32[]{:S(2)}) collective-permute-start(bf16[64,2048]{1,0:T(8,128)(2,1)S(1)} %get-tuple-element.18), channel_id=1, source_target_pairs={{0,4},{4,0},{1,5},{5,1},{2,6},{6,2},{3,7},{7,3},{8,12},{12,8},{9,1... | collective-permute-start | bytes 786440 | tf_op jit(solution)/shard_map/ppermute | solution.py:47
  11.3 10.0 %collective-permute-done.6 = s32[64,6]{1,0:T(8,128)S(1)} collective-permute-done((s32[64,6]{1,0:T(8,128)S(1)}, s32[64,6]{1,0:T(8,128)S(1)}, u32[]{:S(2)}, u32[]{:S(2)}) %collective-permute-start.6) | collective-permute-done | bytes 1568 | tf_op jit(solution)/shard_map/ppermute | solution.py:47
  22.6 4.2 %collective-permute-done.11 = s32[64,6]{1,0:T(8,128)S(1)} collective-permute-done((s32[64,6]{1,0:T(8,128)S(1)}, s32[64,6]{1,0:T(8,128)S(1)}, u32[]{:S(2)}, u32[]{:S(2)}) %collective-permute-start.11) | collective-permute-done | bytes 1568 | tf_op jit(solution)/shard_map/ppermute | solution.py:47
  32.3 3.8 %all-to-all-start = ((bf16[8,112,1024]{2,1,0:T(8,128)(2,1)}), bf16[8,112,1024]{2,1,0:T(8,128)(2,1)S(1)}, u32[]{:S(2)}, u32[]{:S(2)}) async-start(bf16[8,112,1024]{2,1,0:T(8,128)(2,1)} %bitcast.19), calls=%async_computation | async-start | bytes 3670016 | tf_op jit(solution)/shard_map/all_to_all | solution.py:94
  36.2 25.4 %all-to-all-done = bf16[8,112,1024]{2,1,0:T(8,128)(2,1)S(1)} async-done(((bf16[8,112,1024]{2,1,0:T(8,128)(2,1)}), bf16[8,112,1024]{2,1,0:T(8,128)(2,1)S(1)}, u32[]{:S(2)}, u32[]{:S(2)}) %all-to-all-start) | async-done | bytes 1835040 | tf_op jit(solution)/shard_map/all_to_all | solution.py:94
  63.2 6.0 %fusion.33 = f32[2,8,4,14,768]{4,1,0,3,2:T(8,128)S(1)} fusion(bf16[4,1024,768]{2,1,0:T(8,128)(2,1)} %collective-permute-done.7, pred[]{:T(512)S(6)} %eq.215, bf16[16,4,14,1024]{3,2,1,0:T(8,128)(2,1)} %reshape.254, bf16[1,4,1024,768]{3,2,1,0:T(8,128)(2,1)} %param.13), kind=kOutput, calls=%fused_computation.35 | convolution fusion | flops 1412431872 | bytes 17170432 | tf_op jit(solution)/shard_map/sjcd,jdh->sjch/dot_general | solution.py:98
  69.4 6.3 %fusion.30 = f32[2,8,4,14,768]{4,1,0,3,2:T(8,128)S(1)} fusion(bf16[4,1024,768]{2,1,0:T(8,128)(2,1)} %collective-permute-done.4, pred[]{:T(512)S(6)} %eq.215, bf16[16,4,14,1024]{3,2,1,0:T(8,128)(2,1)S(1)} %copy-done.3, bf16[1,4,1024,768]{3,2,1,0:T(8,128)(2,1)} %param.12), kind=kOutput, calls=%fused_computation.34 | convolution fusion | flops 1412431872 | bytes 17170432 | tf_op jit(solution)/shard_map/sjcd,jdh->sjch/dot_general | solution.py:97
  77.8 31.4 %collective-permute-done.8 = bf16[2,8,4,14,768]{4,1,0,3,2:T(8,128)(2,1)S(1)} collective-permute-done((bf16[2,8,4,14,768]{4,1,0,3,2:T(8,128)(2,1)S(1)}, bf16[2,8,4,14,768]{4,1,0,3,2:T(8,128)(2,1)S(1)}, u32[]{:S(2)}, u32[]{:S(2)}) %collective-permute-start.8) | collective-permute-done | bytes 1376288 | tf_op jit(solution)/shard_map/ppermute | solution.py:112
  109.2 2.2 fusion.50
  114.6 13.3 %collective-permute-done.9 = bf16[8,4,14,768]{3,0,2,1:T(8,128)(2,1)S(1)} collective-permute-done((bf16[8,4,14,768]{3,0,2,1:T(8,128)(2,1)S(1)}, bf16[8,4,14,768]{3,0,2,1:T(8,128)(2,1)S(1)}, u32[]{:S(2)}, u32[]{:S(2)}) %collective-permute-start.9) | collective-permute-done | bytes 688160 | tf_op jit(solution)/shard_map/ppermute | solution.py:118
  129.2 4.7 %convert_bitcast_fusion.1 = bf16[2,2,4,4,14,1024]{5,4,1,2,0,3:T(8,128)(2,1)S(1)} fusion(bf16[2,4,2,4,14,768]{5,4,2,1,0,3:T(8,128)(2,1)S(1)} %bitcast.327, bf16[4,768,1024]{2,1,0:T(8,128)(2,1)} %collective-permute-done.3, pred[]{:T(512)S(6)} %eq.215, bf16[1,4,768,1024]{3,2,1,0:T(8,128)(2,1)} %param.14), kind=kOutput, calls=%fused_computation.31 | convolution fusion | flops 1413349376 | bytes 15794177 | tf_op jit(solution)/shard_map/fipjch,jhd->fpijcd/dot_general | solution.py:126
  135.7 7.2 %all-to-all-start.1 = ((bf16[16,56,1024]{2,1,0:T(8,128)(2,1)}), bf16[16,56,1024]{2,1,0:T(8,128)(2,1)S(1)}, u32[]{:S(2)}, u32[]{:S(2)}) async-start(bf16[16,56,1024]{2,1,0:T(8,128)(2,1)} %reshape.301), calls=%async_computation.1 | async-start | bytes 3670016 | tf_op jit(solution)/shard_map/all_to_all | solution.py:129
  146.0 39.2 %all-to-all-done.1 = bf16[16,56,1024]{2,1,0:T(8,128)(2,1)S(1)} async-done(((bf16[16,56,1024]{2,1,0:T(8,128)(2,1)}), bf16[16,56,1024]{2,1,0:T(8,128)(2,1)S(1)}, u32[]{:S(2)}, u32[]{:S(2)}) %all-to-all-start.1) | async-done | bytes 1835040 | tf_op jit(solution)/shard_map/all_to_all | solution.py:129
  188.8 13.9 %collective-permute-done.10 = bf16[64,2048]{1,0:T(8,128)(2,1)S(1)} collective-permute-done((bf16[64,2048]{1,0:T(8,128)(2,1)S(1)}, bf16[64,2048]{1,0:T(8,128)(2,1)S(1)}, u32[]{:S(2)}, u32[]{:S(2)}) %collective-permute-start.10) | collective-permute-done | bytes 262176 | tf_op jit(solution)/shard_map/ppermute | solution.py:47
  204.2 27.2 %all_to_all.26 = bf16[8,112,1024]{2,1,0:T(8,128)(2,1)S(1)} all-to-all(bf16[8,112,1024]{2,1,0:T(8,128)(2,1)S(1)} %bitcast.320), channel_id=1, replica_groups=mesh['section'=2,'fsdp'=2,'zhalf'=2,'inner'=4] {'fsdp','inner'}, dimensions={0} | all-to-all | bytes 3670016 | tf_op jit(solution)/shard_map/all_to_all | solution.py:94
  233.0 7.8 %fusion.36 = f32[2,8,4,14,768]{4,1,0,3,2:T(8,128)S(1)} fusion(bf16[4,1024,768]{2,1,0:T(8,128)(2,1)} %collective-permute-done.4, pred[]{:T(512)S(6)} %eq.244, bf16[16,4,14,1024]{3,2,1,0:T(8,128)(2,1)} %reshape.264, bf16[1,4,1024,768]{3,2,1,0:T(8,128)(2,1)} %param.12), kind=kOutput, calls=%fused_computation.36 | convolution fusion | flops 1412431872 | bytes 17170432 | tf_op jit(solution)/shard_map/sjcd,jdh->sjch/dot_general | solution.py:97
  240.8 7.2 %fusion.39 = f32[2,8,4,14,768]{4,1,0,3,2:T(8,128)S(1)} fusion(bf16[4,1024,768]{2,1,0:T(8,128)(2,1)} %collective-permute-done.7, pred[]{:T(512)S(6)} %eq.244, bf16[16,4,14,1024]{3,2,1,0:T(8,128)(2,1)S(1)} %copy-done.4, bf16[1,4,1024,768]{3,2,1,0:T(8,128)(2,1)} %param.13), kind=kOutput, calls=%fused_computation.37 | convolution fusion | flops 1412431872 | bytes 17170432 | tf_op jit(solution)/shard_map/sjcd,jdh->sjch/dot_general | solution.py:98
  249.0 29.2 %collective-permute-done.12 = bf16[2,8,4,14,768]{4,1,3,2,0:T(8,128)(2,1)S(1)} collective-permute-done((bf16[2,8,4,14,768]{4,1,3,2,0:T(8,128)(2,1)S(1)}, bf16[2,8,4,14,768]{4,1,3,2,0:T(8,128)(2,1)S(1)}, u32[]{:S(2)}, u32[]{:S(2)}) %collective-permute-start.12) | collective-permute-done | bytes 1376288 | tf_op jit(solution)/shard_map/ppermute | solution.py:112
  279.9 10.4 %collective-permute-done.13 = bf16[8,4,14,768]{3,0,2,1:T(8,128)(2,1)S(1)} collective-permute-done((bf16[8,4,14,768]{3,0,2,1:T(8,128)(2,1)S(1)}, bf16[8,4,14,768]{3,0,2,1:T(8,128)(2,1)S(1)}, u32[]{:S(2)}, u32[]{:S(2)}) %collective-permute-start.13) | collective-permute-done | bytes 688160 | tf_op jit(solution)/shard_map/ppermute | solution.py:118
  291.6 6.6 %convert_bitcast_fusion = bf16[2,2,4,4,14,1024]{5,4,1,2,0,3:T(8,128)(2,1)S(1)} fusion(bf16[2,4,2,4,14,768]{5,4,2,1,0,3:T(8,128)(2,1)S(1)} %bitcast.328, bf16[4,768,1024]{2,1,0:T(8,128)(2,1)} %collective-permute-done.3, pred[]{:T(512)S(6)} %eq.244, bf16[1,4,768,1024]{3,2,1,0:T(8,128)(2,1)} %param.14), kind=kOutput, calls=%fused_computation.30 | convolution fusion | flops 1413349376 | bytes 15794177 | tf_op jit(solution)/shard_map/fipjch,jhd->fpijcd/dot_general | solution.py:126
  299.9 3.8 %all-to-all-start.3 = ((bf16[16,56,1024]{2,1,0:T(8,128)(2,1)}), bf16[16,56,1024]{2,1,0:T(8,128)(2,1)S(1)}, u32[]{:S(2)}, u32[]{:S(2)}) async-start(bf16[16,56,1024]{2,1,0:T(8,128)(2,1)} %reshape.302), calls=%async_computation.3 | async-start | bytes 3670016 | tf_op jit(solution)/shard_map/all_to_all | solution.py:129
  304.5 34.5 %all-to-all-done.3 = bf16[16,56,1024]{2,1,0:T(8,128)(2,1)S(1)} async-done(((bf16[16,56,1024]{2,1,0:T(8,128)(2,1)}), bf16[16,56,1024]{2,1,0:T(8,128)(2,1)S(1)}, u32[]{:S(2)}, u32[]{:S(2)}) %all-to-all-start.3) | async-done | bytes 1835040 | tf_op jit(solution)/shard_map/all_to_all | solution.py:129
  342.8 3.1 all-to-all-start.4
  346.2 6.7 %all-to-all-done.4 = f32[32,1,2]{2,1,0:T(1,128)S(1)} async-done(((f32[32,1,2]{2,1,0:T(1,128)}), f32[32,1,2]{2,1,0:T(1,128)S(1)}, u32[]{:S(2)}, u32[]{:S(2)}) %all-to-all-start.4) | async-done | bytes 288 | tf_op jit(solution)/shard_map/all_to_all | solution.py:177
  (148 shorter events, 45.2 us)
Async XLA Ops:
  0.6 28.9 %copy-start.5 = (f32[1,2048]{1,0:T(1,128)S(1)}, f32[1,2048]{1,0:T(1,128)}, u32[]{:S(2)}) copy-start(f32[1,2048]{1,0:T(1,128)} %param.10) | copy-start | bytes 24580
  0.6 28.9 %collective-permute-start.1 = (f32[2048]{0:T(1024)}, f32[2048]{0:T(1024)S(1)}, u32[]{:S(2)}, u32[]{:S(2)}) collective-permute-start(f32[2048]{0:T(1024)} %bitcast.341), channel_id=1, source_target_pairs={{0,16},{16,0},{1,17},{17,1},{2,18},{18,2},{3,19},{19,3},{4,20},{20... | collective-permute-start | bytes 24584 | tf_op jit(solution)/shard_map/ppermute | solution.py:14
  2.0 5.6 %collective-permute-start = (s32[128,6]{1,0:T(8,128)S(1)}, s32[128,6]{1,0:T(8,128)S(1)}, u32[]{:S(2)}, u32[]{:S(2)}) collective-permute-start(s32[128,6]{1,0:T(8,128)S(1)} %bitcast.335), channel_id=1, source_target_pairs={{0,16},{16,0},{1,17},{17,1},{2,18},{18,2},{3,19},{19,3},{4,20},{20... | collective-permute-start | bytes 9224 | tf_op jit(solution)/shard_map/ppermute | solution.py:14
  2.1 61.2 %collective-permute-start.7 = (bf16[4,1024,768]{2,1,0:T(8,128)(2,1)}, bf16[4,1024,768]{2,1,0:T(8,128)(2,1)}, u32[]{:S(2)}, u32[]{:S(2)}) collective-permute-start(bf16[4,1024,768]{2,1,0:T(8,128)(2,1)} %bitcast.344), channel_id=1, source_target_pairs={{0,16},{16,0},{1,17},{17,1},{2,18},{18,2},{3,19},{19,3},{4,20},{20... | collective-permute-start | bytes 18874376 | tf_op jit(solution)/shard_map/ppermute | solution.py:14
  3.7 25.9 %collective-permute-start.5 = (bf16[64,2048]{1,0:T(8,128)(2,1)S(1)}, bf16[64,2048]{1,0:T(8,128)(2,1)S(1)}, u32[]{:S(2)}, u32[]{:S(2)}) collective-permute-start(bf16[64,2048]{1,0:T(8,128)(2,1)S(1)} %get-tuple-element.18), channel_id=1, source_target_pairs={{0,4},{4,0},{1,5},{5,1},{2,6},{6,2},{3,7},{7,3},{8,12},{12,8},{9,1... | collective-permute-start | bytes 786440 | tf_op jit(solution)/shard_map/ppermute | solution.py:47
  7.4 62.0 %collective-permute-start.4 = (bf16[4,1024,768]{2,1,0:T(8,128)(2,1)}, bf16[4,1024,768]{2,1,0:T(8,128)(2,1)}, u32[]{:S(2)}, u32[]{:S(2)}) collective-permute-start(bf16[4,1024,768]{2,1,0:T(8,128)(2,1)} %bitcast.343), channel_id=1, source_target_pairs={{0,16},{16,0},{1,17},{17,1},{2,18},{18,2},{3,19},{19,3},{4,20},{20... | collective-permute-start | bytes 18874376 | tf_op jit(solution)/shard_map/ppermute | solution.py:14
  7.6 13.7 %collective-permute-start.6 = (s32[64,6]{1,0:T(8,128)S(1)}, s32[64,6]{1,0:T(8,128)S(1)}, u32[]{:S(2)}, u32[]{:S(2)}) collective-permute-start(s32[64,6]{1,0:T(8,128)S(1)} %get-tuple-element.26), channel_id=1, source_target_pairs={{0,4},{4,0},{1,5},{5,1},{2,6},{6,2},{3,7},{7,3},{8,12},{12,8},{9,1... | collective-permute-start | bytes 4616 | tf_op jit(solution)/shard_map/ppermute | solution.py:47
  21.3 5.5 %collective-permute-start.11 = (s32[64,6]{1,0:T(8,128)S(1)}, s32[64,6]{1,0:T(8,128)S(1)}, u32[]{:S(2)}, u32[]{:S(2)}) collective-permute-start(s32[64,6]{1,0:T(8,128)S(1)} %get-tuple-element.25), channel_id=1, source_target_pairs={{0,4},{4,0},{1,5},{5,1},{2,6},{6,2},{3,7},{7,3},{8,12},{12,8},{9,1... | collective-permute-start | bytes 4616 | tf_op jit(solution)/shard_map/ppermute | solution.py:47
  32.3 29.3 %all-to-all-start = ((bf16[8,112,1024]{2,1,0:T(8,128)(2,1)}), bf16[8,112,1024]{2,1,0:T(8,128)(2,1)S(1)}, u32[]{:S(2)}, u32[]{:S(2)}) async-start(bf16[8,112,1024]{2,1,0:T(8,128)(2,1)} %bitcast.19), calls=%async_computation | async-start | bytes 3670016 | tf_op jit(solution)/shard_map/all_to_all | solution.py:94
  36.1 93.1 %collective-permute-start.3 = (bf16[4,768,1024]{2,1,0:T(8,128)(2,1)}, bf16[4,768,1024]{2,1,0:T(8,128)(2,1)}, u32[]{:S(2)}, u32[]{:S(2)}) collective-permute-start(bf16[4,768,1024]{2,1,0:T(8,128)(2,1)} %bitcast.345), channel_id=1, source_target_pairs={{0,16},{16,0},{1,17},{17,1},{2,18},{18,2},{3,19},{19,3},{4,20},{20... | collective-permute-start | bytes 18874376 | tf_op jit(solution)/shard_map/ppermute | solution.py:14
  77.3 32.0 %collective-permute-start.8 = (bf16[2,8,4,14,768]{4,1,0,3,2:T(8,128)(2,1)S(1)}, bf16[2,8,4,14,768]{4,1,0,3,2:T(8,128)(2,1)S(1)}, u32[]{:S(2)}, u32[]{:S(2)}) collective-permute-start(bf16[2,8,4,14,768]{4,1,0,3,2:T(8,128)(2,1)S(1)} %pad_maximum_fusion.2), channel_id=1, source_target_pairs={{0,8},{8,0},{1,9},{9,1},{2,10},{10,2},{3,11},{11,3},{4,12},{12,4},... | collective-permute-start | bytes 4128776 | tf_op jit(solution)/shard_map/ppermute | solution.py:112
  77.8 34.9 %copy-start.1 = (f32[2,8,4,14,768]{4,1,0,3,2:T(8,128)S(1)}, f32[2,8,4,14,768]{4,1,0,3,2:T(8,128)}, u32[]{:S(2)}) copy-start(f32[2,8,4,14,768]{4,1,0,3,2:T(8,128)} %copy-done) | copy-start | bytes 8257540
  111.5 16.5 %collective-permute-start.9 = (bf16[8,4,14,768]{3,0,2,1:T(8,128)(2,1)S(1)}, bf16[8,4,14,768]{3,0,2,1:T(8,128)(2,1)S(1)}, u32[]{:S(2)}, u32[]{:S(2)}) collective-permute-start(bf16[8,4,14,768]{3,0,2,1:T(8,128)(2,1)S(1)} %fusion.50), channel_id=1, source_target_pairs={{0,8},{8,0},{1,9},{9,1},{2,10},{10,2},{3,11},{11,3},{4,12},{12,4},... | collective-permute-start | bytes 2064392 | tf_op jit(solution)/shard_map/ppermute | solution.py:118
  135.7 7.2 %copy-start.6 = (bf16[1,2048,32]{1,2,0:T(8,128)(2,1)S(1)}, bf16[1,2048,32]{1,2,0:T(8,128)(2,1)}, u32[]{:S(2)}) copy-start(bf16[1,2048,32]{1,2,0:T(8,128)(2,1)} %param.11) | copy-start | bytes 393220
  135.7 49.6 %all-to-all-start.1 = ((bf16[16,56,1024]{2,1,0:T(8,128)(2,1)}), bf16[16,56,1024]{2,1,0:T(8,128)(2,1)S(1)}, u32[]{:S(2)}, u32[]{:S(2)}) async-start(bf16[16,56,1024]{2,1,0:T(8,128)(2,1)} %reshape.301), calls=%async_computation.1 | async-start | bytes 3670016 | tf_op jit(solution)/shard_map/all_to_all | solution.py:129
  142.9 2.6 collective-permute-start.2
  145.5 39.9 %copy-start.7 = (bf16[2048,32]{0,1:T(8,128)(2,1)}, bf16[2048,32]{0,1:T(8,128)(2,1)S(1)}, u32[]{:S(2)}) copy-start(bf16[2048,32]{0,1:T(8,128)(2,1)S(1)} %collective-permute-done.2) | copy-start | bytes 393220
  187.1 15.6 %collective-permute-start.10 = (bf16[64,2048]{1,0:T(8,128)(2,1)S(1)}, bf16[64,2048]{1,0:T(8,128)(2,1)S(1)}, u32[]{:S(2)}, u32[]{:S(2)}) collective-permute-start(bf16[64,2048]{1,0:T(8,128)(2,1)S(1)} %get-tuple-element.29), channel_id=1, source_target_pairs={{0,4},{4,0},{1,5},{5,1},{2,6},{6,2},{3,7},{7,3},{8,12},{12,8},{9,1... | collective-permute-start | bytes 786440 | tf_op jit(solution)/shard_map/ppermute | solution.py:47
  233.0 7.8 %copy-start.4 = (bf16[16,4,14,1024]{3,2,1,0:T(8,128)(2,1)S(1)}, bf16[16,4,14,1024]{3,2,1,0:T(8,128)(2,1)}, u32[]{:S(2)}) copy-start(bf16[16,4,14,1024]{3,2,1,0:T(8,128)(2,1)} %reshape.264) | copy-start | bytes 5505028
  248.4 29.8 %collective-permute-start.12 = (bf16[2,8,4,14,768]{4,1,3,2,0:T(8,128)(2,1)S(1)}, bf16[2,8,4,14,768]{4,1,3,2,0:T(8,128)(2,1)S(1)}, u32[]{:S(2)}, u32[]{:S(2)}) collective-permute-start(bf16[2,8,4,14,768]{4,1,3,2,0:T(8,128)(2,1)S(1)} %pad_maximum_fusion.4), channel_id=1, source_target_pairs={{0,8},{8,0},{1,9},{9,1},{2,10},{10,2},{3,11},{11,3},{4,12},{12,4},... | collective-permute-start | bytes 4128776 | tf_op jit(solution)/shard_map/ppermute | solution.py:112
  278.7 11.6 %collective-permute-start.13 = (bf16[8,4,14,768]{3,0,2,1:T(8,128)(2,1)S(1)}, bf16[8,4,14,768]{3,0,2,1:T(8,128)(2,1)S(1)}, u32[]{:S(2)}, u32[]{:S(2)}) collective-permute-start(bf16[8,4,14,768]{3,0,2,1:T(8,128)(2,1)S(1)} %fusion.46), channel_id=1, source_target_pairs={{0,8},{8,0},{1,9},{9,1},{2,10},{10,2},{3,11},{11,3},{4,12},{12,4},... | collective-permute-start | bytes 2064392 | tf_op jit(solution)/shard_map/ppermute | solution.py:118
  299.9 39.0 %all-to-all-start.3 = ((bf16[16,56,1024]{2,1,0:T(8,128)(2,1)}), bf16[16,56,1024]{2,1,0:T(8,128)(2,1)S(1)}, u32[]{:S(2)}, u32[]{:S(2)}) async-start(bf16[16,56,1024]{2,1,0:T(8,128)(2,1)} %reshape.302), calls=%async_computation.3 | async-start | bytes 3670016 | tf_op jit(solution)/shard_map/all_to_all | solution.py:129
  342.8 10.2 %all-to-all-start.4 = ((f32[32,1,2]{2,1,0:T(1,128)}), f32[32,1,2]{2,1,0:T(1,128)S(1)}, u32[]{:S(2)}, u32[]{:S(2)}) async-start(f32[32,1,2]{2,1,0:T(1,128)} %broadcast_in_dim.32), calls=%async_computation.4 | async-start | bytes 32768 | tf_op jit(solution)/shard_map/all_to_all | solution.py:177
  345.9 7.7 %collective-permute-start.14 = (bf16[64,1024]{1,0:T(8,128)(2,1)S(1)}, bf16[64,1024]{1,0:T(8,128)(2,1)S(1)}, u32[]{:S(2)}, u32[]{:S(2)}) collective-permute-start(bf16[64,1024]{1,0:T(8,128)(2,1)S(1)} %get-tuple-element.24), channel_id=1, source_target_pairs={{0,16},{16,0},{1,17},{17,1},{2,18},{18,2},{3,19},{19,3},{4,20},{20... | collective-permute-start | bytes 393224 | tf_op jit(solution)/shard_map/ppermute | solution.py:14
  (4 other events, 18.1 us)
where the time goes:
time: 355 us; the launch traced here: 354 us
  waiting for transfers between devices  219 us (62%)
  matrix products  44.4 us (13%)
  starting transfers between devices  30 us (8%)
  blocking collectives  27.2 us (8%)
  other arithmetic  16.8 us (5%)
  local copies, waits for them, and re-layouts  15.6 us (4%)
    all_to_all x2, waiting for transfers between devices, expert_layer(): lax.all_to_all(sending.reshape(sources, group_slots, chunk), ('fsdp', 'zh...  73.7 us
    ppermute x2, waiting for transfers between devices, expert_layer(): got = lax.ppermute(outgoing_pair, 'fsdp', ring_pairs(fsdp_count, shift))  60.6 us
    ppermute x4, waiting for transfers between devices, other_half(): return lax.ppermute(value, 'zhalf', [(0, 1), (1, 0)])  28.1 us
    all_to_all x1, blocking collectives, expert_layer(): arrived = lax.all_to_all(outgoing, ('fsdp', 'inner'), 0, 0, tiled=True)  27.2 us
    all_to_all x1, waiting for transfers between devices, expert_layer(): arrived = lax.all_to_all(outgoing, ('fsdp', 'inner'), 0, 0, tiled=True)  25.4 us
    ppermute x2, waiting for transfers between devices, expert_layer(): lax.ppermute(inner_act, 'fsdp', ring_pairs(fsdp_count, shift))  23.8 us
    dot_general x2, matrix products, expert_layer(): jnp.einsum('sjcd,jdh->sjch', arrived, gate_w, preferred_element_type=jnp....  14.1 us
    dot_general x2, matrix products, expert_layer(): jnp.einsum('sjcd,jdh->sjch', arrived, up_w, preferred_element_type=jnp.fl...  13.3 us
  transfers between devices with their start and end apart: 19, of which 12 were waited for; matrix products, arithmetic and copies ran while one was open for 10% of the time, Pallas kernels for 0%

commit v1 on v0

--- a/solution.py
+++ b/solution.py
@@ -57,7 +57,7 @@
     ).astype(jnp.bfloat16)
 
 
-def expert_layer(entering, route_rows, gain_row, router_weight, weights, capacity):
+def expert_layer(entering, route_rows, partner_routes, gain_row, router_weight, weights, capacity):
     gate_w, up_w, down_w = weights
     rows, width = entering.shape
     experts_count = router_weight.shape[1]
@@ -68,7 +68,6 @@
     half_index = lax.axis_index("zhalf")
     fsdp_index = lax.axis_index("fsdp")
     partner_entering = other_half(entering)
-    partner_routes = other_half(route_rows)
     normed = rms_scaled(entering, gain_row)
     partner_normed = rms_scaled(partner_entering, gain_row)
     mix_weights = gate_weights(normed, router_weight, route_rows)
@@ -156,18 +155,27 @@
     capacity = block_capacity * (piece // BLOCK)
     own_weights = (w_gate[0], w_up[0], w_down[0])
     other_weights = tuple(other_section(w) for w in own_weights)
-    own_small = (norm_gain[0], router[0], routes[0])
+    own_small = (norm_gain[0], router[0])
     other_small = tuple(other_section(v) for v in own_small)
+    own_routes = routes[0]
+    section_routes = other_section(own_routes)
+    half_routes = other_half(own_routes)
+    diagonal_routes = lax.ppermute(
+        own_routes, ("section", "zhalf"), [(0, 3), (3, 0), (1, 2), (2, 1)]
+    )
     hidden = lax.dynamic_slice_in_dim(tokens, section_index * piece, piece, 0)
     squares = []
     for layer in range(sections):
         mine = section_index == layer
-        gain_row, router_weight, route_all = [
-            jnp.where(mine, a, b) for a, b in zip(own_small, other_small)
-        ]
+        gain_row, router_weight = [jnp.where(mine, a, b) for a, b in zip(own_small, other_small)]
         weights = tuple(jnp.where(mine, a, b) for a, b in zip(own_weights, other_weights))
+        route_all = jnp.where(mine, own_routes, section_routes)
+        partner_all = jnp.where(mine, half_routes, diagonal_routes)
         route_rows = lax.dynamic_slice_in_dim(route_all, section_index * piece, piece, 0)
-        hidden = expert_layer(hidden, route_rows, gain_row, router_weight, weights, capacity)
+        partner_rows = lax.dynamic_slice_in_dim(partner_all, section_index * piece, piece, 0)
+        hidden = expert_layer(
+            hidden, route_rows, partner_rows, gain_row, router_weight, weights, capacity
+        )
         values = hidden.astype(jnp.float32)
         squares.append(jnp.sum(values * values))
     everyone = ("section", "fsdp", "zhalf", "inner")

time: 355 us -> 356 us (level)
    ppermute x4 -> x3, waiting for transfers between devices: 28.1 us -> 19.5 us  [other_half(): return lax.ppermute(value, 'zhalf', [(0, 1), (1, 0)])]
    all_to_all x1, waiting for transfers between devices: 25.4 us -> 29.7 us  [expert_layer(): arrived = lax.all_to_all(outgoing, ('fsdp', 'inner'), 0, 0, tiled=True)]
    ppermute x0 -> x1, starting transfers between devices: none -> 3.69 us  [body(): lax.ppermute(own_routes, ('section', 'zhalf'), [(0, 3), (3, 0), (1, 2), (...]
  transfers between devices with their start and end apart: 19 -> 19, of which waited for: 12 -> 13; matrix products, arithmetic and copies ran while one was open for 10% -> 9% of each run, Pallas kernels for 0% -> 0%
where the time goes in v1:
time: 356 us; the launch traced here: 355 us
  waiting for transfers between devices  218 us (61%)
  matrix products  44.4 us (12%)
  starting transfers between devices  31.1 us (9%)
  blocking collectives  27.7 us (8%)
  other arithmetic  16.8 us (5%)
  local copies, waits for them, and re-layouts  15.6 us (4%)
    all_to_all x2, waiting for transfers between devices, expert_layer(): lax.all_to_all(sending.reshape(sources, group_slots, chunk), ('fsdp', 'zh...  73.1 us
    ppermute x2, waiting for transfers between devices, expert_layer(): got = lax.ppermute(outgoing_pair, 'fsdp', ring_pairs(fsdp_count, shift))  59.9 us
    all_to_all x1, waiting for transfers between devices, expert_layer(): arrived = lax.all_to_all(outgoing, ('fsdp', 'inner'), 0, 0, tiled=True)  29.7 us
    all_to_all x1, blocking collectives, expert_layer(): arrived = lax.all_to_all(outgoing, ('fsdp', 'inner'), 0, 0, tiled=True)  27.7 us
    ppermute x2, waiting for transfers between devices, expert_layer(): lax.ppermute(inner_act, 'fsdp', ring_pairs(fsdp_count, shift))  26 us
    ppermute x3, waiting for transfers between devices, other_half(): return lax.ppermute(value, 'zhalf', [(0, 1), (1, 0)])  19.5 us
    dot_general x2, matrix products, expert_layer(): jnp.einsum('sjcd,jdh->sjch', arrived, up_w, preferred_element_type=jnp.fl...  13.9 us
    dot_general x2, matrix products, expert_layer(): jnp.einsum('sjcd,jdh->sjch', arrived, gate_w, preferred_element_type=jnp....  13.5 us
  transfers between devices with their start and end apart: 19, of which 13 were waited for; matrix products, arithmetic and copies ran while one was open for 9% of the time, Pallas kernels for 0%

profile of v1, /device:TPU:0, one launch (start us, length us, event | category | flops | bytes accessed | tf_op | source)
XLA Modules:
  0.0 355.0 jit_solution(4544960229909372104)
XLA Ops:
  2.0 3.7 %collective-permute-start.7 = (s32[128,6]{1,0:T(8,128)S(1)}, s32[128,6]{1,0:T(8,128)S(1)}, u32[]{:S(2)}, u32[]{:S(2)}) collective-permute-start(s32[128,6]{1,0:T(8,128)S(1)} %bitcast.336), channel_id=1, source_target_pairs={{0,20},{20,0},{4,16},{16,4},{1,21},{21,1},{5,17},{17,5},{2,22},{22... | collective-permute-start | bytes 9224 | tf_op jit(solution)/shard_map/ppermute | solution.py:163
  20.0 4.5 %collective-permute-done.5 = bf16[64,2048]{1,0:T(8,128)(2,1)S(1)} collective-permute-done((bf16[64,2048]{1,0:T(8,128)(2,1)S(1)}, bf16[64,2048]{1,0:T(8,128)(2,1)S(1)}, u32[]{:S(2)}, u32[]{:S(2)}) %collective-permute-start.5) | collective-permute-done | bytes 262176 | tf_op jit(solution)/shard_map/ppermute | solution.py:47
  27.2 5.0 %all-to-all-start = ((bf16[8,112,1024]{2,1,0:T(8,128)(2,1)}), bf16[8,112,1024]{2,1,0:T(8,128)(2,1)S(1)}, u32[]{:S(2)}, u32[]{:S(2)}) async-start(bf16[8,112,1024]{2,1,0:T(8,128)(2,1)} %bitcast.19), calls=%async_computation | async-start | bytes 3670016 | tf_op jit(solution)/shard_map/all_to_all | solution.py:93
  32.5 29.7 %all-to-all-done = bf16[8,112,1024]{2,1,0:T(8,128)(2,1)S(1)} async-done(((bf16[8,112,1024]{2,1,0:T(8,128)(2,1)}), bf16[8,112,1024]{2,1,0:T(8,128)(2,1)S(1)}, u32[]{:S(2)}, u32[]{:S(2)}) %all-to-all-start) | async-done | bytes 1835040 | tf_op jit(solution)/shard_map/all_to_all | solution.py:93
  63.8 6.0 %fusion.33 = f32[2,8,4,14,768]{4,1,0,3,2:T(8,128)S(1)} fusion(bf16[4,1024,768]{2,1,0:T(8,128)(2,1)} %collective-permute-done.8, pred[]{:T(512)S(6)} %eq.215, bf16[16,4,14,1024]{3,2,1,0:T(8,128)(2,1)} %reshape.254, bf16[1,4,1024,768]{3,2,1,0:T(8,128)(2,1)} %param.13), kind=kOutput, calls=%fused_computation.35 | convolution fusion | flops 1412431872 | bytes 17170432 | tf_op jit(solution)/shard_map/sjcd,jdh->sjch/dot_general | solution.py:97
  70.0 6.3 %fusion.30 = f32[2,8,4,14,768]{4,1,0,3,2:T(8,128)S(1)} fusion(bf16[4,1024,768]{2,1,0:T(8,128)(2,1)} %collective-permute-done.4, pred[]{:T(512)S(6)} %eq.215, bf16[16,4,14,1024]{3,2,1,0:T(8,128)(2,1)S(1)} %copy-done.3, bf16[1,4,1024,768]{3,2,1,0:T(8,128)(2,1)} %param.12), kind=kOutput, calls=%fused_computation.34 | convolution fusion | flops 1412431872 | bytes 17170432 | tf_op jit(solution)/shard_map/sjcd,jdh->sjch/dot_general | solution.py:96
  78.5 30.8 %collective-permute-done.9 = bf16[2,8,4,14,768]{4,1,0,3,2:T(8,128)(2,1)S(1)} collective-permute-done((bf16[2,8,4,14,768]{4,1,0,3,2:T(8,128)(2,1)S(1)}, bf16[2,8,4,14,768]{4,1,0,3,2:T(8,128)(2,1)S(1)}, u32[]{:S(2)}, u32[]{:S(2)}) %collective-permute-start.9) | collective-permute-done | bytes 1376288 | tf_op jit(solution)/shard_map/ppermute | solution.py:111
  109.2 2.2 fusion.50
  114.0 15.2 %collective-permute-done.10 = bf16[8,4,14,768]{3,0,2,1:T(8,128)(2,1)S(1)} collective-permute-done((bf16[8,4,14,768]{3,0,2,1:T(8,128)(2,1)S(1)}, bf16[8,4,14,768]{3,0,2,1:T(8,128)(2,1)S(1)}, u32[]{:S(2)}, u32[]{:S(2)}) %collective-permute-start.10) | collective-permute-done | bytes 688160 | tf_op jit(solution)/shard_map/ppermute | solution.py:117
  130.6 4.7 %convert_bitcast_fusion.1 = bf16[2,2,4,4,14,1024]{5,4,1,2,0,3:T(8,128)(2,1)S(1)} fusion(bf16[2,4,2,4,14,768]{5,4,2,1,0,3:T(8,128)(2,1)S(1)} %bitcast.327, bf16[4,768,1024]{2,1,0:T(8,128)(2,1)} %collective-permute-done.3, pred[]{:T(512)S(6)} %eq.215, bf16[1,4,768,1024]{3,2,1,0:T(8,128)(2,1)} %param.14), kind=kOutput, calls=%fused_computation.31 | convolution fusion | flops 1413349376 | bytes 15794177 | tf_op jit(solution)/shard_map/fipjch,jhd->fpijcd/dot_general | solution.py:125
  137.0 5.4 %all-to-all-start.1 = ((bf16[16,56,1024]{2,1,0:T(8,128)(2,1)}), bf16[16,56,1024]{2,1,0:T(8,128)(2,1)S(1)}, u32[]{:S(2)}, u32[]{:S(2)}) async-start(bf16[16,56,1024]{2,1,0:T(8,128)(2,1)} %reshape.301), calls=%async_computation.1 | async-start | bytes 3670016 | tf_op jit(solution)/shard_map/all_to_all | solution.py:128
  142.5 2.2 collective-permute-start.2
  146.2 38.1 %all-to-all-done.1 = bf16[16,56,1024]{2,1,0:T(8,128)(2,1)S(1)} async-done(((bf16[16,56,1024]{2,1,0:T(8,128)(2,1)}), bf16[16,56,1024]{2,1,0:T(8,128)(2,1)S(1)}, u32[]{:S(2)}, u32[]{:S(2)}) %all-to-all-start.1) | async-done | bytes 1835040 | tf_op jit(solution)/shard_map/all_to_all | solution.py:128
  188.1 12.9 %collective-permute-done.11 = bf16[64,2048]{1,0:T(8,128)(2,1)S(1)} collective-permute-done((bf16[64,2048]{1,0:T(8,128)(2,1)S(1)}, bf16[64,2048]{1,0:T(8,128)(2,1)S(1)}, u32[]{:S(2)}, u32[]{:S(2)}) %collective-permute-start.11) | collective-permute-done | bytes 262176 | tf_op jit(solution)/shard_map/ppermute | solution.py:47
  202.5 27.7 %all_to_all.26 = bf16[8,112,1024]{2,1,0:T(8,128)(2,1)S(1)} all-to-all(bf16[8,112,1024]{2,1,0:T(8,128)(2,1)S(1)} %bitcast.320), channel_id=1, replica_groups=mesh['section'=2,'fsdp'=2,'zhalf'=2,'inner'=4] {'fsdp','inner'}, dimensions={0} | all-to-all | bytes 3670016 | tf_op jit(solution)/shard_map/all_to_all | solution.py:93
  231.8 7.8 %fusion.39 = f32[2,8,4,14,768]{4,1,0,3,2:T(8,128)S(1)} fusion(bf16[4,1024,768]{2,1,0:T(8,128)(2,1)} %collective-permute-done.8, pred[]{:T(512)S(6)} %eq.244, bf16[16,4,14,1024]{3,2,1,0:T(8,128)(2,1)} %reshape.264, bf16[1,4,1024,768]{3,2,1,0:T(8,128)(2,1)} %param.13), kind=kOutput, calls=%fused_computation.37 | convolution fusion | flops 1412431872 | bytes 17170432 | tf_op jit(solution)/shard_map/sjcd,jdh->sjch/dot_general | solution.py:97
  239.7 7.2 %fusion.36 = f32[2,8,4,14,768]{4,1,0,3,2:T(8,128)S(1)} fusion(bf16[4,1024,768]{2,1,0:T(8,128)(2,1)} %collective-permute-done.4, pred[]{:T(512)S(6)} %eq.244, bf16[16,4,14,1024]{3,2,1,0:T(8,128)(2,1)S(1)} %copy-done.4, bf16[1,4,1024,768]{3,2,1,0:T(8,128)(2,1)} %param.12), kind=kOutput, calls=%fused_computation.36 | convolution fusion | flops 1412431872 | bytes 17170432 | tf_op jit(solution)/shard_map/sjcd,jdh->sjch/dot_general | solution.py:96
  247.8 29.2 %collective-permute-done.12 = bf16[2,8,4,14,768]{4,1,3,2,0:T(8,128)(2,1)S(1)} collective-permute-done((bf16[2,8,4,14,768]{4,1,3,2,0:T(8,128)(2,1)S(1)}, bf16[2,8,4,14,768]{4,1,3,2,0:T(8,128)(2,1)S(1)}, u32[]{:S(2)}, u32[]{:S(2)}) %collective-permute-start.12) | collective-permute-done | bytes 1376288 | tf_op jit(solution)/shard_map/ppermute | solution.py:111
  278.7 10.7 %collective-permute-done.13 = bf16[8,4,14,768]{3,0,2,1:T(8,128)(2,1)S(1)} collective-permute-done((bf16[8,4,14,768]{3,0,2,1:T(8,128)(2,1)S(1)}, bf16[8,4,14,768]{3,0,2,1:T(8,128)(2,1)S(1)}, u32[]{:S(2)}, u32[]{:S(2)}) %collective-permute-start.13) | collective-permute-done | bytes 688160 | tf_op jit(solution)/shard_map/ppermute | solution.py:117
  290.8 6.6 %convert_bitcast_fusion = bf16[2,2,4,4,14,1024]{5,4,1,2,0,3:T(8,128)(2,1)S(1)} fusion(bf16[2,4,2,4,14,768]{5,4,2,1,0,3:T(8,128)(2,1)S(1)} %bitcast.328, bf16[4,768,1024]{2,1,0:T(8,128)(2,1)} %collective-permute-done.3, pred[]{:T(512)S(6)} %eq.244, bf16[1,4,768,1024]{3,2,1,0:T(8,128)(2,1)} %param.14), kind=kOutput, calls=%fused_computation.30 | convolution fusion | flops 1413349376 | bytes 15794177 | tf_op jit(solution)/shard_map/fipjch,jhd->fpijcd/dot_general | solution.py:125
  299.0 4.8 %all-to-all-start.3 = ((bf16[16,56,1024]{2,1,0:T(8,128)(2,1)}), bf16[16,56,1024]{2,1,0:T(8,128)(2,1)S(1)}, u32[]{:S(2)}, u32[]{:S(2)}) async-start(bf16[16,56,1024]{2,1,0:T(8,128)(2,1)} %reshape.302), calls=%async_computation.3 | async-start | bytes 3670016 | tf_op jit(solution)/shard_map/all_to_all | solution.py:128
  304.5 35.0 %all-to-all-done.3 = bf16[16,56,1024]{2,1,0:T(8,128)(2,1)S(1)} async-done(((bf16[16,56,1024]{2,1,0:T(8,128)(2,1)}), bf16[16,56,1024]{2,1,0:T(8,128)(2,1)S(1)}, u32[]{:S(2)}, u32[]{:S(2)}) %all-to-all-start.3) | async-done | bytes 1835040 | tf_op jit(solution)/shard_map/all_to_all | solution.py:128
  343.4 3.1 all-to-all-start.4
  346.8 6.7 %all-to-all-done.4 = f32[32,1,2]{2,1,0:T(1,128)S(1)} async-done(((f32[32,1,2]{2,1,0:T(1,128)}), f32[32,1,2]{2,1,0:T(1,128)S(1)}, u32[]{:S(2)}, u32[]{:S(2)}) %all-to-all-start.4) | async-done | bytes 288 | tf_op jit(solution)/shard_map/all_to_all | solution.py:185
  (149 shorter events, 48.1 us)
Async XLA Ops:
  0.6 19.4 %copy-start.5 = (f32[1,2048]{1,0:T(1,128)S(1)}, f32[1,2048]{1,0:T(1,128)}, u32[]{:S(2)}) copy-start(f32[1,2048]{1,0:T(1,128)} %param.10) | copy-start | bytes 24580
  1.4 11.4 %collective-permute-start = (s32[128,6]{1,0:T(8,128)S(1)}, s32[128,6]{1,0:T(8,128)S(1)}, u32[]{:S(2)}, u32[]{:S(2)}) collective-permute-start(s32[128,6]{1,0:T(8,128)S(1)} %bitcast.335), channel_id=1, source_target_pairs={{0,16},{16,0},{1,17},{17,1},{2,18},{18,2},{3,19},{19,3},{4,20},{20... | collective-permute-start | bytes 9224 | tf_op jit(solution)/shard_map/ppermute | solution.py:14
  2.0 7.5 %collective-permute-start.7 = (s32[128,6]{1,0:T(8,128)S(1)}, s32[128,6]{1,0:T(8,128)S(1)}, u32[]{:S(2)}, u32[]{:S(2)}) collective-permute-start(s32[128,6]{1,0:T(8,128)S(1)} %bitcast.336), channel_id=1, source_target_pairs={{0,20},{20,0},{4,16},{16,4},{1,21},{21,1},{5,17},{17,5},{2,22},{22... | collective-permute-start | bytes 9224 | tf_op jit(solution)/shard_map/ppermute | solution.py:163
  5.7 6.9 %collective-permute-start.6 = (s32[128,6]{1,0:T(8,128)S(1)}, s32[128,6]{1,0:T(8,128)S(1)}, u32[]{:S(2)}, u32[]{:S(2)}) collective-permute-start(s32[128,6]{1,0:T(8,128)S(1)} %bitcast.337), channel_id=1, source_target_pairs={{0,4},{4,0},{1,5},{5,1},{2,6},{6,2},{3,7},{7,3},{8,12},{12,8},{9,1... | collective-permute-start | bytes 9224 | tf_op jit(solution)/shard_map/ppermute | solution.py:47
  5.7 14.3 %collective-permute-start.1 = (f32[2048]{0:T(1024)}, f32[2048]{0:T(1024)S(1)}, u32[]{:S(2)}, u32[]{:S(2)}) collective-permute-start(f32[2048]{0:T(1024)} %bitcast.343), channel_id=1, source_target_pairs={{0,16},{16,0},{1,17},{17,1},{2,18},{18,2},{3,19},{19,3},{4,20},{20... | collective-permute-start | bytes 24584 | tf_op jit(solution)/shard_map/ppermute | solution.py:14
  5.8 58.0 %collective-permute-start.8 = (bf16[4,1024,768]{2,1,0:T(8,128)(2,1)}, bf16[4,1024,768]{2,1,0:T(8,128)(2,1)}, u32[]{:S(2)}, u32[]{:S(2)}) collective-permute-start(bf16[4,1024,768]{2,1,0:T(8,128)(2,1)} %bitcast.345), channel_id=1, source_target_pairs={{0,16},{16,0},{1,17},{17,1},{2,18},{18,2},{3,19},{19,3},{4,20},{20... | collective-permute-start | bytes 18874376 | tf_op jit(solution)/shard_map/ppermute | solution.py:14
  9.5 15.1 %collective-permute-start.5 = (bf16[64,2048]{1,0:T(8,128)(2,1)S(1)}, bf16[64,2048]{1,0:T(8,128)(2,1)S(1)}, u32[]{:S(2)}, u32[]{:S(2)}) collective-permute-start(bf16[64,2048]{1,0:T(8,128)(2,1)S(1)} %get-tuple-element.18), channel_id=1, source_target_pairs={{0,4},{4,0},{1,5},{5,1},{2,6},{6,2},{3,7},{7,3},{8,12},{12,8},{9,1... | collective-permute-start | bytes 786440 | tf_op jit(solution)/shard_map/ppermute | solution.py:47
  12.5 57.5 %collective-permute-start.4 = (bf16[4,1024,768]{2,1,0:T(8,128)(2,1)}, bf16[4,1024,768]{2,1,0:T(8,128)(2,1)}, u32[]{:S(2)}, u32[]{:S(2)}) collective-permute-start(bf16[4,1024,768]{2,1,0:T(8,128)(2,1)} %bitcast.346), channel_id=1, source_target_pairs={{0,16},{16,0},{1,17},{17,1},{2,18},{18,2},{3,19},{19,3},{4,20},{20... | collective-permute-start | bytes 18874376 | tf_op jit(solution)/shard_map/ppermute | solution.py:14
  27.2 34.9 %all-to-all-start = ((bf16[8,112,1024]{2,1,0:T(8,128)(2,1)}), bf16[8,112,1024]{2,1,0:T(8,128)(2,1)S(1)}, u32[]{:S(2)}, u32[]{:S(2)}) async-start(bf16[8,112,1024]{2,1,0:T(8,128)(2,1)} %bitcast.19), calls=%async_computation | async-start | bytes 3670016 | tf_op jit(solution)/shard_map/all_to_all | solution.py:93
  32.2 98.3 %collective-permute-start.3 = (bf16[4,768,1024]{2,1,0:T(8,128)(2,1)}, bf16[4,768,1024]{2,1,0:T(8,128)(2,1)}, u32[]{:S(2)}, u32[]{:S(2)}) collective-permute-start(bf16[4,768,1024]{2,1,0:T(8,128)(2,1)} %bitcast.347), channel_id=1, source_target_pairs={{0,16},{16,0},{1,17},{17,1},{2,18},{18,2},{3,19},{19,3},{4,20},{20... | collective-permute-start | bytes 18874376 | tf_op jit(solution)/shard_map/ppermute | solution.py:14
  69.9 6.4 %copy-start = (f32[2,8,4,14,768]{4,1,0,3,2:T(8,128)}, f32[2,8,4,14,768]{4,1,0,3,2:T(8,128)S(1)}, u32[]{:S(2)}) copy-start(f32[2,8,4,14,768]{4,1,0,3,2:T(8,128)S(1)} %fusion.33) | copy-start | bytes 8257540
  77.9 31.4 %collective-permute-start.9 = (bf16[2,8,4,14,768]{4,1,0,3,2:T(8,128)(2,1)S(1)}, bf16[2,8,4,14,768]{4,1,0,3,2:T(8,128)(2,1)S(1)}, u32[]{:S(2)}, u32[]{:S(2)}) collective-permute-start(bf16[2,8,4,14,768]{4,1,0,3,2:T(8,128)(2,1)S(1)} %pad_maximum_fusion.2), channel_id=1, source_target_pairs={{0,8},{8,0},{1,9},{9,1},{2,10},{10,2},{3,11},{11,3},{4,12},{12,4},... | collective-permute-start | bytes 4128776 | tf_op jit(solution)/shard_map/ppermute | solution.py:111
  78.5 33.7 %copy-start.1 = (f32[2,8,4,14,768]{4,1,0,3,2:T(8,128)S(1)}, f32[2,8,4,14,768]{4,1,0,3,2:T(8,128)}, u32[]{:S(2)}) copy-start(f32[2,8,4,14,768]{4,1,0,3,2:T(8,128)} %copy-done) | copy-start | bytes 8257540
  111.5 17.8 %collective-permute-start.10 = (bf16[8,4,14,768]{3,0,2,1:T(8,128)(2,1)S(1)}, bf16[8,4,14,768]{3,0,2,1:T(8,128)(2,1)S(1)}, u32[]{:S(2)}, u32[]{:S(2)}) collective-permute-start(bf16[8,4,14,768]{3,0,2,1:T(8,128)(2,1)S(1)} %fusion.50), channel_id=1, source_target_pairs={{0,8},{8,0},{1,9},{9,1},{2,10},{10,2},{3,11},{11,3},{4,12},{12,4},... | collective-permute-start | bytes 2064392 | tf_op jit(solution)/shard_map/ppermute | solution.py:117
  137.0 47.3 %all-to-all-start.1 = ((bf16[16,56,1024]{2,1,0:T(8,128)(2,1)}), bf16[16,56,1024]{2,1,0:T(8,128)(2,1)S(1)}, u32[]{:S(2)}, u32[]{:S(2)}) async-start(bf16[16,56,1024]{2,1,0:T(8,128)(2,1)} %reshape.301), calls=%async_computation.1 | async-start | bytes 3670016 | tf_op jit(solution)/shard_map/all_to_all | solution.py:128
  142.5 3.2 collective-permute-start.2
  145.7 38.8 %copy-start.7 = (bf16[2048,32]{0,1:T(8,128)(2,1)}, bf16[2048,32]{0,1:T(8,128)(2,1)S(1)}, u32[]{:S(2)}) copy-start(bf16[2048,32]{0,1:T(8,128)(2,1)S(1)} %collective-permute-done.2) | copy-start | bytes 393220
  186.2 14.8 %collective-permute-start.11 = (bf16[64,2048]{1,0:T(8,128)(2,1)S(1)}, bf16[64,2048]{1,0:T(8,128)(2,1)S(1)}, u32[]{:S(2)}, u32[]{:S(2)}) collective-permute-start(bf16[64,2048]{1,0:T(8,128)(2,1)S(1)} %get-tuple-element.31), channel_id=1, source_target_pairs={{0,4},{4,0},{1,5},{5,1},{2,6},{6,2},{3,7},{7,3},{8,12},{12,8},{9,1... | collective-permute-start | bytes 786440 | tf_op jit(solution)/shard_map/ppermute | solution.py:47
  231.8 7.9 %copy-start.4 = (bf16[16,4,14,1024]{3,2,1,0:T(8,128)(2,1)S(1)}, bf16[16,4,14,1024]{3,2,1,0:T(8,128)(2,1)}, u32[]{:S(2)}) copy-start(bf16[16,4,14,1024]{3,2,1,0:T(8,128)(2,1)} %reshape.264) | copy-start | bytes 5505028
  247.2 29.8 %collective-permute-start.12 = (bf16[2,8,4,14,768]{4,1,3,2,0:T(8,128)(2,1)S(1)}, bf16[2,8,4,14,768]{4,1,3,2,0:T(8,128)(2,1)S(1)}, u32[]{:S(2)}, u32[]{:S(2)}) collective-permute-start(bf16[2,8,4,14,768]{4,1,3,2,0:T(8,128)(2,1)S(1)} %pad_maximum_fusion.4), channel_id=1, source_target_pairs={{0,8},{8,0},{1,9},{9,1},{2,10},{10,2},{3,11},{11,3},{4,12},{12,4},... | collective-permute-start | bytes 4128776 | tf_op jit(solution)/shard_map/ppermute | solution.py:111
  277.6 11.9 %collective-permute-start.13 = (bf16[8,4,14,768]{3,0,2,1:T(8,128)(2,1)S(1)}, bf16[8,4,14,768]{3,0,2,1:T(8,128)(2,1)S(1)}, u32[]{:S(2)}, u32[]{:S(2)}) collective-permute-start(bf16[8,4,14,768]{3,0,2,1:T(8,128)(2,1)S(1)} %fusion.46), channel_id=1, source_target_pairs={{0,8},{8,0},{1,9},{9,1},{2,10},{10,2},{3,11},{11,3},{4,12},{12,4},... | collective-permute-start | bytes 2064392 | tf_op jit(solution)/shard_map/ppermute | solution.py:117
  299.0 40.5 %all-to-all-start.3 = ((bf16[16,56,1024]{2,1,0:T(8,128)(2,1)}), bf16[16,56,1024]{2,1,0:T(8,128)(2,1)S(1)}, u32[]{:S(2)}, u32[]{:S(2)}) async-start(bf16[16,56,1024]{2,1,0:T(8,128)(2,1)} %reshape.302), calls=%async_computation.3 | async-start | bytes 3670016 | tf_op jit(solution)/shard_map/all_to_all | solution.py:128
  343.4 10.2 %all-to-all-start.4 = ((f32[32,1,2]{2,1,0:T(1,128)}), f32[32,1,2]{2,1,0:T(1,128)S(1)}, u32[]{:S(2)}, u32[]{:S(2)}) async-start(f32[32,1,2]{2,1,0:T(1,128)} %broadcast_in_dim.32), calls=%async_computation.4 | async-start | bytes 32768 | tf_op jit(solution)/shard_map/all_to_all | solution.py:185
  346.5 7.7 %collective-permute-start.14 = (bf16[64,1024]{1,0:T(8,128)(2,1)S(1)}, bf16[64,1024]{1,0:T(8,128)(2,1)S(1)}, u32[]{:S(2)}, u32[]{:S(2)}) collective-permute-start(bf16[64,1024]{1,0:T(8,128)(2,1)S(1)} %get-tuple-element.24), channel_id=1, source_target_pairs={{0,16},{16,0},{1,17},{17,1},{2,18},{18,2},{3,19},{19,3},{4,20},{20... | collective-permute-start | bytes 393224 | tf_op jit(solution)/shard_map/ppermute | solution.py:14
  (4 other events, 18.1 us)

commit v2 on v1

--- a/solution.py
+++ b/solution.py
@@ -93,22 +93,26 @@
     arrived = lax.all_to_all(outgoing, ("fsdp", "inner"), 0, 0, tiled=True)
     sources = fsdp_count * inner_devices * halves
     arrived = arrived.reshape(sources, local_experts, capacity, chunk)
-    gate_part = jnp.einsum("sjcd,jdh->sjch", arrived, gate_w, preferred_element_type=jnp.float32)
-    up_part = jnp.einsum("sjcd,jdh->sjch", arrived, up_w, preferred_element_type=jnp.float32)
-    block_shape = (fsdp_count, sources // fsdp_count, local_experts, capacity, hidden_units)
-    gate_blocks = gate_part.reshape(block_shape)
-    up_blocks = up_part.reshape(block_shape)
-    gate_sum = lax.dynamic_index_in_dim(gate_blocks, fsdp_index, 0, keepdims=False)
-    up_sum = lax.dynamic_index_in_dim(up_blocks, fsdp_index, 0, keepdims=False)
+    arrived_blocks = arrived.reshape(fsdp_count, sources // fsdp_count, local_experts, capacity, chunk)
+
+    def gate_and_up(rows_in):
+        gate_part = jnp.einsum(
+            "sjcd,jdh->sjch", rows_in, gate_w, preferred_element_type=jnp.float32
+        )
+        up_part = jnp.einsum("sjcd,jdh->sjch", rows_in, up_w, preferred_element_type=jnp.float32)
+        return gate_part, up_part
+
+    received = []
     for shift in range(1, fsdp_count):
         target = (fsdp_index + shift) % fsdp_count
         outgoing_pair = jnp.stack(
-            [
-                lax.dynamic_index_in_dim(gate_blocks, target, 0, keepdims=False),
-                lax.dynamic_index_in_dim(up_blocks, target, 0, keepdims=False),
-            ]
+            gate_and_up(lax.dynamic_index_in_dim(arrived_blocks, target, 0, keepdims=False))
         ).astype(jnp.bfloat16)
-        got = lax.ppermute(outgoing_pair, "fsdp", ring_pairs(fsdp_count, shift))
+        received.append(lax.ppermute(outgoing_pair, "fsdp", ring_pairs(fsdp_count, shift)))
+    gate_sum, up_sum = gate_and_up(
+        lax.dynamic_index_in_dim(arrived_blocks, fsdp_index, 0, keepdims=False)
+    )
+    for got in received:
         gate_sum = gate_sum + got[0].astype(jnp.float32)
         up_sum = up_sum + got[1].astype(jnp.float32)
     inner_act = (jax.nn.silu(gate_sum) * up_sum).astype(jnp.bfloat16)

time: 356 us -> 354 us (level)
  waiting for transfers between devices: 218 us -> 198 us
  matrix products: 44.4 us -> 62.2 us
  other arithmetic: 16.8 us -> 11.9 us
    dot_general x4 -> x8, matrix products: 27.4 us -> 45.2 us  [the longest x4 23 us: gate_and_up(): jnp.einsum('sjcd,jdh->sjch', rows_in, up_w, preferred_element_type=jnp.fl...]
    ppermute x2, waiting for transfers between devices: 59.9 us -> 46.2 us  [expert_layer(): lax.ppermute(outgoing_pair, 'fsdp', ring_pairs(fsdp_count, shift))]
    ppermute x3, waiting for transfers between devices: 19.5 us -> 12.4 us  [other_half(): return lax.ppermute(value, 'zhalf', [(0, 1), (1, 0)])]
    ppermute x3, starting transfers between devices: 2.92 us -> 8.76 us  [other_half(): return lax.ppermute(value, 'zhalf', [(0, 1), (1, 0)])]
    another operation x7, local copies, waits for them, and re-layouts: 1.02 us -> 6.65 us  [the longest x2 5.09 us: expert_layer(): arrived.reshape(fsdp_count, sources // fsdp_count, local_experts, capacit...]
    ppermute x1, waiting for transfers between devices: 2.09 us -> 7.51 us  [body(): lax.ppermute(own_routes, ('section', 'zhalf'), [(0, 3), (3, 0), (1, 2), (...]
    convert_element_type x4 -> x0, other arithmetic: 5.23 us -> none  [expert_layer(): inner_act = (jax.nn.silu(gate_sum) * up_sum).astype(jnp.bfloat16)]
    ppermute x1, starting transfers between devices: 3.69 us -> 0.01 us  [body(): lax.ppermute(own_routes, ('section', 'zhalf'), [(0, 3), (3, 0), (1, 2), (...]
  transfers between devices with their start and end apart: 19 -> 19, of which waited for: 13 -> 11; matrix products, arithmetic and copies ran while one was open for 9% -> 12% of each run, Pallas kernels for 0% -> 0%
where the time goes in v2:
time: 354 us; the launch traced here: 353 us
  waiting for transfers between devices  198 us (56%)
  matrix products  62.2 us (18%)
  starting transfers between devices  33.1 us (9%)
  blocking collectives  28.8 us (8%)
  local copies, waits for them, and re-layouts  17.7 us (5%)
  other arithmetic  11.9 us (3%)
    all_to_all x2, waiting for transfers between devices, expert_layer(): lax.all_to_all(sending.reshape(sources, group_slots, chunk), ('fsdp', 'zh...  69.5 us
    ppermute x2, waiting for transfers between devices, expert_layer(): lax.ppermute(outgoing_pair, 'fsdp', ring_pairs(fsdp_count, shift))  46.2 us
    all_to_all x1, waiting for transfers between devices, expert_layer(): arrived = lax.all_to_all(outgoing, ('fsdp', 'inner'), 0, 0, tiled=True)  29.9 us
    all_to_all x1, blocking collectives, expert_layer(): arrived = lax.all_to_all(outgoing, ('fsdp', 'inner'), 0, 0, tiled=True)  28.8 us
    ppermute x2, waiting for transfers between devices, expert_layer(): lax.ppermute(inner_act, 'fsdp', ring_pairs(fsdp_count, shift))  25.2 us
    dot_general x4, matrix products, gate_and_up(): jnp.einsum('sjcd,jdh->sjch', rows_in, up_w, preferred_element_type=jnp.fl...  23 us
    dot_general x4, matrix products, gate_and_up(): jnp.einsum('sjcd,jdh->sjch', rows_in, gate_w, preferred_element_type=jnp....  22.1 us
    ppermute x3, waiting for transfers between devices, other_half(): return lax.ppermute(value, 'zhalf', [(0, 1), (1, 0)])  12.4 us
  transfers between devices with their start and end apart: 19, of which 11 were waited for; matrix products, arithmetic and copies ran while one was open for 12% of the time, Pallas kernels for 0%

profile of v2, /device:TPU:0, one launch (start us, length us, event | category | flops | bytes accessed | tf_op | source)
XLA Modules:
  0.0 353.4 jit_solution(5316175169366647797)
XLA Ops:
  10.4 7.5 %collective-permute-done.7 = s32[128,6]{1,0:T(8,128)S(1)} collective-permute-done((s32[128,6]{1,0:T(8,128)S(1)}, s32[128,6]{1,0:T(8,128)S(1)}, u32[]{:S(2)}, u32[]{:S(2)}) %collective-permute-start.7) | collective-permute-done | bytes 3104 | tf_op jit(solution)/shard_map/ppermute | solution.py:167
  28.1 4.5 %all-to-all-start = ((bf16[8,112,1024]{2,1,0:T(8,128)(2,1)}), bf16[8,112,1024]{2,1,0:T(8,128)(2,1)}, u32[]{:S(2)}, u32[]{:S(2)}) async-start(bf16[8,112,1024]{2,1,0:T(8,128)(2,1)} %bitcast.19), calls=%async_computation | async-start | bytes 3670016 | tf_op jit(solution)/shard_map/all_to_all | solution.py:93
  33.2 29.9 %all-to-all-done = bf16[8,112,1024]{2,1,0:T(8,128)(2,1)} async-done(((bf16[8,112,1024]{2,1,0:T(8,128)(2,1)}), bf16[8,112,1024]{2,1,0:T(8,128)(2,1)}, u32[]{:S(2)}, u32[]{:S(2)}) %all-to-all-start) | async-done | bytes 1835040 | tf_op jit(solution)/shard_map/all_to_all | solution.py:93
  66.0 4.6 %fusion.54 = bf16[1,8,4,14,768]{4,3,1,2,0:T(8,128)(2,1)S(1)} fusion(bf16[4,1024,768]{2,1,0:T(8,128)(2,1)} %collective-permute-done.8, pred[]{:T(512)S(6)} %eq.215, bf16[1,8,4,14,1024]{4,3,2,1,0:T(8,128)(2,1)S(1)} %get-tuple-element.21, bf16[1,4,1024,768]{3,2,1,0:T(8,128)(2,1)} %param.13), kind=kOutput, calls=%fused_computation.64 | convolution fusion | flops 708132864 | bytes 14188545 | tf_op jit(solution)/shard_map/sjcd,jdh->sjch/dot_general | solution.py:102
  70.6 4.6 %fusion.57 = bf16[1,8,4,14,768]{4,3,1,2,0:T(8,128)(2,1)S(1)} fusion(bf16[4,1024,768]{2,1,0:T(8,128)(2,1)} %collective-permute-done.4, pred[]{:T(512)S(6)} %eq.215, bf16[1,8,4,14,1024]{4,3,2,1,0:T(8,128)(2,1)S(1)} %get-tuple-element.21, bf16[1,4,1024,768]{3,2,1,0:T(8,128)(2,1)} %param.12), kind=kOutput, calls=%fused_computation.65 | convolution fusion | flops 708132864 | bytes 14188545 | tf_op jit(solution)/shard_map/sjcd,jdh->sjch/dot_general | solution.py:99
  76.5 4.6 %fusion.18 = f32[4,768,8,14]{1,3,2,0:T(8,128)S(1)} fusion(bf16[4,1024,768]{2,1,0:T(8,128)(2,1)} %collective-permute-done.4, pred[]{:T(512)S(6)} %eq.215, bf16[1,8,4,14,1024]{4,3,2,1,0:T(8,128)(2,1)S(1)} %get-tuple-element.22, bf16[1,4,1024,768]{3,2,1,0:T(8,128)(2,1)} %param.12), kind=kOutput, calls=%fused_computation.20 | convolution fusion | flops 707788800 | bytes 14876673 | tf_op jit(solution)/shard_map/sjcd,jdh->sjch/dot_general | solution.py:99
  81.1 25.7 %collective-permute-done.9 = bf16[2,8,4,14,768]{4,1,3,2,0:T(8,128)(2,1)S(1)} collective-permute-done((bf16[2,8,4,14,768]{4,1,3,2,0:T(8,128)(2,1)S(1)}, bf16[2,8,4,14,768]{4,1,3,2,0:T(8,128)(2,1)S(1)}, u32[]{:S(2)}, u32[]{:S(2)}) %collective-permute-start.9) | collective-permute-done | bytes 1376288 | tf_op jit(solution)/shard_map/ppermute | solution.py:111
  106.9 5.1 %fusion.33 = bf16[8,4,14,768]{3,2,0,1:T(8,128)(2,1)S(1)} fusion(f32[4,768,8,14]{1,3,2,0:T(8,128)S(1)} %fusion.18, bf16[1,8,4,14,768]{4,1,3,2,0:T(8,128)(2,1)S(1)} %get-tuple-element.26, bf16[1,8,4,14,768]{4,1,3,2,0:T(8,128)(2,1)S(1)} %get-tuple-element.25, bf16[1,8,4,14,1024]{4,3,2,1,0:T(8,128)(2,1)S(1)} %get-tuple-element.22, ...), kind=kOutput, calls=%fused_computation.48 | convolution fusion | flops 711229440 | bytes 16941056 | tf_op jit(solution)/shard_map/sjcd,jdh->sjch/dot_general | solution.py:102
  112.9 14.9 %collective-permute-done.10 = bf16[8,4,14,768]{3,0,2,1:T(8,128)(2,1)S(1)} collective-permute-done((bf16[8,4,14,768]{3,0,2,1:T(8,128)(2,1)S(1)}, bf16[8,4,14,768]{3,0,2,1:T(8,128)(2,1)S(1)}, u32[]{:S(2)}, u32[]{:S(2)}) %collective-permute-start.10) | collective-permute-done | bytes 688160 | tf_op jit(solution)/shard_map/ppermute | solution.py:121
  129.0 4.7 %convert_bitcast_fusion.1 = bf16[2,2,4,4,14,1024]{5,4,1,2,0,3:T(8,128)(2,1)S(1)} fusion(bf16[4,768,1024]{2,1,0:T(8,128)(2,1)} %collective-permute-done.3, pred[]{:T(512)S(6)} %eq.215, bf16[2,4,2,4,14,768]{5,4,2,1,3,0:T(8,128)(2,1)S(1)} %bitcast.365, bf16[1,4,768,1024]{3,2,1,0:T(8,128)(2,1)} %param.14), kind=kOutput, calls=%fused_computation.35 | convolution fusion | flops 1413349376 | bytes 15794177 | tf_op jit(solution)/shard_map/fipjch,jhd->fpijcd/dot_general | solution.py:129
  135.6 4.6 %all-to-all-start.1 = ((bf16[16,56,1024]{2,1,0:T(8,128)(2,1)}), bf16[16,56,1024]{2,1,0:T(8,128)(2,1)S(1)}, u32[]{:S(2)}, u32[]{:S(2)}) async-start(bf16[16,56,1024]{2,1,0:T(8,128)(2,1)} %reshape.281), calls=%async_computation.1 | async-start | bytes 3670016 | tf_op jit(solution)/shard_map/all_to_all | solution.py:132
  145.6 36.3 %all-to-all-done.1 = bf16[16,56,1024]{2,1,0:T(8,128)(2,1)S(1)} async-done(((bf16[16,56,1024]{2,1,0:T(8,128)(2,1)}), bf16[16,56,1024]{2,1,0:T(8,128)(2,1)S(1)}, u32[]{:S(2)}, u32[]{:S(2)}) %all-to-all-start.1) | async-done | bytes 1835040 | tf_op jit(solution)/shard_map/all_to_all | solution.py:132
  185.5 12.4 %collective-permute-done.11 = bf16[64,2048]{1,0:T(8,128)(2,1)S(1)} collective-permute-done((bf16[64,2048]{1,0:T(8,128)(2,1)S(1)}, bf16[64,2048]{1,0:T(8,128)(2,1)S(1)}, u32[]{:S(2)}, u32[]{:S(2)}) %collective-permute-start.11) | collective-permute-done | bytes 262176 | tf_op jit(solution)/shard_map/ppermute | solution.py:47
  199.5 28.8 %all_to_all.26 = bf16[8,112,1024]{2,1,0:T(8,128)(2,1)} all-to-all(bf16[8,112,1024]{2,1,0:T(8,128)(2,1)S(1)} %bitcast.354), channel_id=1, replica_groups=mesh['section'=2,'fsdp'=2,'zhalf'=2,'inner'=4] {'fsdp','inner'}, dimensions={0} | all-to-all | bytes 3670016 | tf_op jit(solution)/shard_map/all_to_all | solution.py:93
  231.0 6.5 %fusion.51 = bf16[1,8,4,14,768]{4,3,1,2,0:T(8,128)(2,1)S(1)} fusion(bf16[4,1024,768]{2,1,0:T(8,128)(2,1)} %collective-permute-done.4, pred[]{:T(512)S(6)} %eq.244, bf16[1,8,4,14,1024]{4,3,2,1,0:T(8,128)(2,1)S(1)} %get-tuple-element.19, bf16[1,4,1024,768]{3,2,1,0:T(8,128)(2,1)} %param.12), kind=kOutput, calls=%fused_computation.63 | convolution fusion | flops 708132864 | bytes 14188545 | tf_op jit(solution)/shard_map/sjcd,jdh->sjch/dot_general | solution.py:99
  237.5 6.5 %fusion.48 = bf16[1,8,4,14,768]{4,3,1,2,0:T(8,128)(2,1)S(1)} fusion(bf16[4,1024,768]{2,1,0:T(8,128)(2,1)} %collective-permute-done.8, pred[]{:T(512)S(6)} %eq.244, bf16[1,8,4,14,1024]{4,3,2,1,0:T(8,128)(2,1)S(1)} %get-tuple-element.19, bf16[1,4,1024,768]{3,2,1,0:T(8,128)(2,1)} %param.13), kind=kOutput, calls=%fused_computation.62 | convolution fusion | flops 708132864 | bytes 14188545 | tf_op jit(solution)/shard_map/sjcd,jdh->sjch/dot_general | solution.py:102
  245.2 6.4 %fusion.10 = f32[4,768,8,14]{1,3,2,0:T(8,128)S(1)} fusion(bf16[4,1024,768]{2,1,0:T(8,128)(2,1)} %collective-permute-done.4, pred[]{:T(512)S(6)} %eq.244, bf16[1,8,4,14,1024]{4,3,2,1,0:T(8,128)(2,1)S(1)} %get-tuple-element.20, bf16[1,4,1024,768]{3,2,1,0:T(8,128)(2,1)} %param.12), kind=kOutput, calls=%fused_computation.12 | convolution fusion | flops 707788800 | bytes 14876673 | tf_op jit(solution)/shard_map/sjcd,jdh->sjch/dot_general | solution.py:99
  251.6 20.5 %collective-permute-done.12 = bf16[2,8,4,14,768]{4,1,3,2,0:T(8,128)(2,1)S(1)} collective-permute-done((bf16[2,8,4,14,768]{4,1,3,2,0:T(8,128)(2,1)S(1)}, bf16[2,8,4,14,768]{4,1,3,2,0:T(8,128)(2,1)S(1)}, u32[]{:S(2)}, u32[]{:S(2)}) %collective-permute-start.12) | collective-permute-done | bytes 1376288 | tf_op jit(solution)/shard_map/ppermute | solution.py:111
  272.2 6.9 %fusion.31 = bf16[8,4,14,768]{3,2,0,1:T(8,128)(2,1)S(1)} fusion(f32[4,768,8,14]{1,3,2,0:T(8,128)S(1)} %fusion.10, bf16[1,8,4,14,768]{4,1,3,2,0:T(8,128)(2,1)S(1)} %get-tuple-element.24, bf16[1,8,4,14,768]{4,1,3,2,0:T(8,128)(2,1)S(1)} %get-tuple-element.23, bf16[1,8,4,14,1024]{4,3,2,1,0:T(8,128)(2,1)S(1)} %get-tuple-element.20, ...), kind=kOutput, calls=%fused_computation.44 | convolution fusion | flops 711229440 | bytes 16941056 | tf_op jit(solution)/shard_map/sjcd,jdh->sjch/dot_general | solution.py:102
  280.0 10.4 %collective-permute-done.13 = bf16[8,4,14,768]{3,0,2,1:T(8,128)(2,1)S(1)} collective-permute-done((bf16[8,4,14,768]{3,0,2,1:T(8,128)(2,1)S(1)}, bf16[8,4,14,768]{3,0,2,1:T(8,128)(2,1)S(1)}, u32[]{:S(2)}, u32[]{:S(2)}) %collective-permute-start.13) | collective-permute-done | bytes 688160 | tf_op jit(solution)/shard_map/ppermute | solution.py:121
  291.6 6.5 %convert_bitcast_fusion = bf16[2,2,4,4,14,1024]{5,4,1,2,0,3:T(8,128)(2,1)S(1)} fusion(bf16[4,768,1024]{2,1,0:T(8,128)(2,1)} %collective-permute-done.3, pred[]{:T(512)S(6)} %eq.244, bf16[2,4,2,4,14,768]{5,4,2,1,3,0:T(8,128)(2,1)S(1)} %bitcast.366, bf16[1,4,768,1024]{3,2,1,0:T(8,128)(2,1)} %param.14), kind=kOutput, calls=%fused_computation.34 | convolution fusion | flops 1413349376 | bytes 15794177 | tf_op jit(solution)/shard_map/fipjch,jhd->fpijcd/dot_general | solution.py:129
  299.8 4.3 %all-to-all-start.3 = ((bf16[16,56,1024]{2,1,0:T(8,128)(2,1)}), bf16[16,56,1024]{2,1,0:T(8,128)(2,1)S(1)}, u32[]{:S(2)}, u32[]{:S(2)}) async-start(bf16[16,56,1024]{2,1,0:T(8,128)(2,1)} %reshape.282), calls=%async_computation.3 | async-start | bytes 3670016 | tf_op jit(solution)/shard_map/all_to_all | solution.py:132
  304.8 33.2 %all-to-all-done.3 = bf16[16,56,1024]{2,1,0:T(8,128)(2,1)S(1)} async-done(((bf16[16,56,1024]{2,1,0:T(8,128)(2,1)}), bf16[16,56,1024]{2,1,0:T(8,128)(2,1)S(1)}, u32[]{:S(2)}, u32[]{:S(2)}) %all-to-all-start.3) | async-done | bytes 1835040 | tf_op jit(solution)/shard_map/all_to_all | solution.py:132
  345.3 6.7 %all-to-all-done.4 = f32[32,1,2]{2,1,0:T(1,128)S(1)} async-done(((f32[32,1,2]{2,1,0:T(1,128)}), f32[32,1,2]{2,1,0:T(1,128)S(1)}, u32[]{:S(2)}, u32[]{:S(2)}) %all-to-all-start.4) | async-done | bytes 288 | tf_op jit(solution)/shard_map/all_to_all | solution.py:189
  (157 shorter events, 56.0 us)
Async XLA Ops:
  0.6 24.7 %copy-start.6 = (f32[1,2048]{1,0:T(1,128)S(1)}, f32[1,2048]{1,0:T(1,128)}, u32[]{:S(2)}) copy-start(f32[1,2048]{1,0:T(1,128)} %param.10) | copy-start | bytes 24580
  1.4 8.4 %collective-permute-start.6 = (s32[128,6]{1,0:T(8,128)S(1)}, s32[128,6]{1,0:T(8,128)S(1)}, u32[]{:S(2)}, u32[]{:S(2)}) collective-permute-start(s32[128,6]{1,0:T(8,128)S(1)} %bitcast.371), channel_id=1, source_target_pairs={{0,4},{4,0},{1,5},{5,1},{2,6},{6,2},{3,7},{7,3},{8,12},{12,8},{9,1... | collective-permute-start | bytes 9224 | tf_op jit(solution)/shard_map/ppermute | solution.py:47
  5.6 12.3 %collective-permute-start.7 = (s32[128,6]{1,0:T(8,128)S(1)}, s32[128,6]{1,0:T(8,128)S(1)}, u32[]{:S(2)}, u32[]{:S(2)}) collective-permute-start(s32[128,6]{1,0:T(8,128)S(1)} %bitcast.372), channel_id=1, source_target_pairs={{0,20},{20,0},{4,16},{16,4},{1,21},{21,1},{5,17},{17,5},{2,22},{22... | collective-permute-start | bytes 9224 | tf_op jit(solution)/shard_map/ppermute | solution.py:167
  5.6 12.9 %collective-permute-start = (s32[128,6]{1,0:T(8,128)S(1)}, s32[128,6]{1,0:T(8,128)S(1)}, u32[]{:S(2)}, u32[]{:S(2)}) collective-permute-start(s32[128,6]{1,0:T(8,128)S(1)} %bitcast.373), channel_id=1, source_target_pairs={{0,16},{16,0},{1,17},{17,1},{2,18},{18,2},{3,19},{19,3},{4,20},{20... | collective-permute-start | bytes 9224 | tf_op jit(solution)/shard_map/ppermute | solution.py:14
  6.9 18.5 %collective-permute-start.5 = (bf16[64,2048]{1,0:T(8,128)(2,1)S(1)}, bf16[64,2048]{1,0:T(8,128)(2,1)S(1)}, u32[]{:S(2)}, u32[]{:S(2)}) collective-permute-start(bf16[64,2048]{1,0:T(8,128)(2,1)S(1)} %get-tuple-element.18), channel_id=1, source_target_pairs={{0,4},{4,0},{1,5},{5,1},{2,6},{6,2},{3,7},{7,3},{8,12},{12,8},{9,1... | collective-permute-start | bytes 786440 | tf_op jit(solution)/shard_map/ppermute | solution.py:47
  9.8 15.6 %collective-permute-start.1 = (f32[2048]{0:T(1024)}, f32[2048]{0:T(1024)S(1)}, u32[]{:S(2)}, u32[]{:S(2)}) collective-permute-start(f32[2048]{0:T(1024)} %bitcast.379), channel_id=1, source_target_pairs={{0,16},{16,0},{1,17},{17,1},{2,18},{18,2},{3,19},{19,3},{4,20},{20... | collective-permute-start | bytes 24584 | tf_op jit(solution)/shard_map/ppermute | solution.py:14
  9.8 56.1 %collective-permute-start.8 = (bf16[4,1024,768]{2,1,0:T(8,128)(2,1)}, bf16[4,1024,768]{2,1,0:T(8,128)(2,1)}, u32[]{:S(2)}, u32[]{:S(2)}) collective-permute-start(bf16[4,1024,768]{2,1,0:T(8,128)(2,1)} %bitcast.382), channel_id=1, source_target_pairs={{0,16},{16,0},{1,17},{17,1},{2,18},{18,2},{3,19},{19,3},{4,20},{20... | collective-permute-start | bytes 18874376 | tf_op jit(solution)/shard_map/ppermute | solution.py:14
  17.9 52.7 %collective-permute-start.4 = (bf16[4,1024,768]{2,1,0:T(8,128)(2,1)}, bf16[4,1024,768]{2,1,0:T(8,128)(2,1)}, u32[]{:S(2)}, u32[]{:S(2)}) collective-permute-start(bf16[4,1024,768]{2,1,0:T(8,128)(2,1)} %bitcast.381), channel_id=1, source_target_pairs={{0,16},{16,0},{1,17},{17,1},{2,18},{18,2},{3,19},{19,3},{4,20},{20... | collective-permute-start | bytes 18874376 | tf_op jit(solution)/shard_map/ppermute | solution.py:14
  18.5 7.1 %copy-start.2 = (s32[64,6]{1,0:T(8,128)}, s32[64,6]{1,0:T(8,128)S(1)}, u32[]{:S(2)}) copy-start(s32[64,6]{1,0:T(8,128)S(1)} %get-tuple-element.33) | copy-start | bytes 4612
  28.1 35.0 %all-to-all-start = ((bf16[8,112,1024]{2,1,0:T(8,128)(2,1)}), bf16[8,112,1024]{2,1,0:T(8,128)(2,1)}, u32[]{:S(2)}, u32[]{:S(2)}) async-start(bf16[8,112,1024]{2,1,0:T(8,128)(2,1)} %bitcast.19), calls=%async_computation | async-start | bytes 3670016 | tf_op jit(solution)/shard_map/all_to_all | solution.py:93
  32.6 96.3 %collective-permute-start.3 = (bf16[4,768,1024]{2,1,0:T(8,128)(2,1)}, bf16[4,768,1024]{2,1,0:T(8,128)(2,1)}, u32[]{:S(2)}, u32[]{:S(2)}) collective-permute-start(bf16[4,768,1024]{2,1,0:T(8,128)(2,1)} %bitcast.383), channel_id=1, source_target_pairs={{0,16},{16,0},{1,17},{17,1},{2,18},{18,2},{3,19},{19,3},{4,20},{20... | collective-permute-start | bytes 18874376 | tf_op jit(solution)/shard_map/ppermute | solution.py:14
  75.9 30.9 %collective-permute-start.9 = (bf16[2,8,4,14,768]{4,1,3,2,0:T(8,128)(2,1)S(1)}, bf16[2,8,4,14,768]{4,1,3,2,0:T(8,128)(2,1)S(1)}, u32[]{:S(2)}, u32[]{:S(2)}) collective-permute-start(bf16[2,8,4,14,768]{4,1,3,2,0:T(8,128)(2,1)S(1)} %copy.168), channel_id=1, source_target_pairs={{0,8},{8,0},{1,9},{9,1},{2,10},{10,2},{3,11},{11,3},{4,12},{12,4},... | collective-permute-start | bytes 4128776 | tf_op jit(solution)/shard_map/ppermute | solution.py:111
  112.2 15.5 %collective-permute-start.10 = (bf16[8,4,14,768]{3,0,2,1:T(8,128)(2,1)S(1)}, bf16[8,4,14,768]{3,0,2,1:T(8,128)(2,1)S(1)}, u32[]{:S(2)}, u32[]{:S(2)}) collective-permute-start(bf16[8,4,14,768]{3,0,2,1:T(8,128)(2,1)S(1)} %copy.171), channel_id=1, source_target_pairs={{0,8},{8,0},{1,9},{9,1},{2,10},{10,2},{3,11},{11,3},{4,12},{12,4},... | collective-permute-start | bytes 2064392 | tf_op jit(solution)/shard_map/ppermute | solution.py:121
  135.6 4.6 %copy-start.7 = (bf16[1,2048,32]{1,2,0:T(8,128)(2,1)S(1)}, bf16[1,2048,32]{1,2,0:T(8,128)(2,1)}, u32[]{:S(2)}) copy-start(bf16[1,2048,32]{1,2,0:T(8,128)(2,1)} %param.11) | copy-start | bytes 393220
  135.6 46.3 %all-to-all-start.1 = ((bf16[16,56,1024]{2,1,0:T(8,128)(2,1)}), bf16[16,56,1024]{2,1,0:T(8,128)(2,1)S(1)}, u32[]{:S(2)}, u32[]{:S(2)}) async-start(bf16[16,56,1024]{2,1,0:T(8,128)(2,1)} %reshape.281), calls=%async_computation.1 | async-start | bytes 3670016 | tf_op jit(solution)/shard_map/all_to_all | solution.py:132
  140.2 4.9 %collective-permute-start.2 = (bf16[2048,32]{0,1:T(8,128)(2,1)S(1)}, bf16[2048,32]{0,1:T(8,128)(2,1)S(1)}, u32[]{:S(2)}, u32[]{:S(2)}) collective-permute-start(bf16[2048,32]{0,1:T(8,128)(2,1)S(1)} %bitcast.384), channel_id=1, source_target_pairs={{0,16},{16,0},{1,17},{17,1},{2,18},{18,2},{3,19},{19,3},{4,20},{20... | collective-permute-start | bytes 393224 | tf_op jit(solution)/shard_map/ppermute | solution.py:14
  145.1 37.0 %copy-start.9 = (bf16[2048,32]{0,1:T(8,128)(2,1)}, bf16[2048,32]{0,1:T(8,128)(2,1)S(1)}, u32[]{:S(2)}) copy-start(bf16[2048,32]{0,1:T(8,128)(2,1)S(1)} %collective-permute-done.2) | copy-start | bytes 393220
  183.8 15.5 %copy-start = (bf16[64,2048]{1,0:T(8,128)(2,1)}, bf16[64,2048]{1,0:T(8,128)(2,1)S(1)}, u32[]{:S(2)}) copy-start(bf16[64,2048]{1,0:T(8,128)(2,1)S(1)} %get-tuple-element.39) | copy-start | bytes 786436
  183.8 14.2 %collective-permute-start.11 = (bf16[64,2048]{1,0:T(8,128)(2,1)S(1)}, bf16[64,2048]{1,0:T(8,128)(2,1)S(1)}, u32[]{:S(2)}, u32[]{:S(2)}) collective-permute-start(bf16[64,2048]{1,0:T(8,128)(2,1)S(1)} %get-tuple-element.39), channel_id=1, source_target_pairs={{0,4},{4,0},{1,5},{5,1},{2,6},{6,2},{3,7},{7,3},{8,12},{12,8},{9,1... | collective-permute-start | bytes 786440 | tf_op jit(solution)/shard_map/ppermute | solution.py:47
  244.6 27.6 %collective-permute-start.12 = (bf16[2,8,4,14,768]{4,1,3,2,0:T(8,128)(2,1)S(1)}, bf16[2,8,4,14,768]{4,1,3,2,0:T(8,128)(2,1)S(1)}, u32[]{:S(2)}, u32[]{:S(2)}) collective-permute-start(bf16[2,8,4,14,768]{4,1,3,2,0:T(8,128)(2,1)S(1)} %copy.189), channel_id=1, source_target_pairs={{0,8},{8,0},{1,9},{9,1},{2,10},{10,2},{3,11},{11,3},{4,12},{12,4},... | collective-permute-start | bytes 4128776 | tf_op jit(solution)/shard_map/ppermute | solution.py:111
  279.3 11.0 %collective-permute-start.13 = (bf16[8,4,14,768]{3,0,2,1:T(8,128)(2,1)S(1)}, bf16[8,4,14,768]{3,0,2,1:T(8,128)(2,1)S(1)}, u32[]{:S(2)}, u32[]{:S(2)}) collective-permute-start(bf16[8,4,14,768]{3,0,2,1:T(8,128)(2,1)S(1)} %copy.192), channel_id=1, source_target_pairs={{0,8},{8,0},{1,9},{9,1},{2,10},{10,2},{3,11},{11,3},{4,12},{12,4},... | collective-permute-start | bytes 2064392 | tf_op jit(solution)/shard_map/ppermute | solution.py:121
  299.8 38.2 %all-to-all-start.3 = ((bf16[16,56,1024]{2,1,0:T(8,128)(2,1)}), bf16[16,56,1024]{2,1,0:T(8,128)(2,1)S(1)}, u32[]{:S(2)}, u32[]{:S(2)}) async-start(bf16[16,56,1024]{2,1,0:T(8,128)(2,1)} %reshape.282), calls=%async_computation.3 | async-start | bytes 3670016 | tf_op jit(solution)/shard_map/all_to_all | solution.py:132
  341.9 10.2 %all-to-all-start.4 = ((f32[32,1,2]{2,1,0:T(1,128)}), f32[32,1,2]{2,1,0:T(1,128)S(1)}, u32[]{:S(2)}, u32[]{:S(2)}) async-start(f32[32,1,2]{2,1,0:T(1,128)} %broadcast_in_dim.32), calls=%async_computation.4 | async-start | bytes 32768 | tf_op jit(solution)/shard_map/all_to_all | solution.py:189
  345.0 7.7 %collective-permute-start.14 = (bf16[64,1024]{1,0:T(8,128)(2,1)S(1)}, bf16[64,1024]{1,0:T(8,128)(2,1)S(1)}, u32[]{:S(2)}, u32[]{:S(2)}) collective-permute-start(bf16[64,1024]{1,0:T(8,128)(2,1)S(1)} %get-tuple-element.32), channel_id=1, source_target_pairs={{0,16},{16,0},{1,17},{17,1},{2,18},{18,2},{3,19},{19,3},{4,20},{20... | collective-permute-start | bytes 393224 | tf_op jit(solution)/shard_map/ppermute | solution.py:14
  (6 other events, 22.9 us)

commit v3 on v2

--- a/solution.py
+++ b/solution.py
@@ -58,10 +58,10 @@
 
 
 def expert_layer(entering, route_rows, partner_routes, gain_row, router_weight, weights, capacity):
-    gate_w, up_w, down_w = weights
+    gate_up_w, down_w = weights
     rows, width = entering.shape
     experts_count = router_weight.shape[1]
-    local_experts, chunk, hidden_units = gate_w.shape
+    local_experts, hidden_units, chunk = down_w.shape
     fsdp_count = lax.axis_size("fsdp")
     halves = lax.axis_size("zhalf")
     inner_devices = lax.axis_size("inner")
@@ -96,25 +96,20 @@
     arrived_blocks = arrived.reshape(fsdp_count, sources // fsdp_count, local_experts, capacity, chunk)
 
     def gate_and_up(rows_in):
-        gate_part = jnp.einsum(
-            "sjcd,jdh->sjch", rows_in, gate_w, preferred_element_type=jnp.float32
-        )
-        up_part = jnp.einsum("sjcd,jdh->sjch", rows_in, up_w, preferred_element_type=jnp.float32)
-        return gate_part, up_part
+        return jnp.einsum("sjcd,jdh->sjch", rows_in, gate_up_w, preferred_element_type=jnp.float32)
 
     received = []
     for shift in range(1, fsdp_count):
         target = (fsdp_index + shift) % fsdp_count
-        outgoing_pair = jnp.stack(
-            gate_and_up(lax.dynamic_index_in_dim(arrived_blocks, target, 0, keepdims=False))
+        outgoing_part = gate_and_up(
+            lax.dynamic_index_in_dim(arrived_blocks, target, 0, keepdims=False)
         ).astype(jnp.bfloat16)
-        received.append(lax.ppermute(outgoing_pair, "fsdp", ring_pairs(fsdp_count, shift)))
-    gate_sum, up_sum = gate_and_up(
-        lax.dynamic_index_in_dim(arrived_blocks, fsdp_index, 0, keepdims=False)
-    )
+        received.append(lax.ppermute(outgoing_part, "fsdp", ring_pairs(fsdp_count, shift)))
+    both_sum = gate_and_up(lax.dynamic_index_in_dim(arrived_blocks, fsdp_index, 0, keepdims=False))
     for got in received:
-        gate_sum = gate_sum + got[0].astype(jnp.float32)
-        up_sum = up_sum + got[1].astype(jnp.float32)
+        both_sum = both_sum + got.astype(jnp.float32)
+    gate_sum = both_sum[..., :hidden_units]
+    up_sum = both_sum[..., hidden_units:]
     inner_act = (jax.nn.silu(gate_sum) * up_sum).astype(jnp.bfloat16)
     inner_pieces = [inner_act]
     for shift in range(1, fsdp_count):
@@ -172,7 +167,8 @@
     for layer in range(sections):
         mine = section_index == layer
         gain_row, router_weight = [jnp.where(mine, a, b) for a, b in zip(own_small, other_small)]
-        weights = tuple(jnp.where(mine, a, b) for a, b in zip(own_weights, other_weights))
+        gate_sel, up_sel, down_sel = [jnp.where(mine, a, b) for a, b in zip(own_weights, other_weights)]
+        weights = lax.optimization_barrier((jnp.concatenate([gate_sel, up_sel], axis=-1), down_sel))
         route_all = jnp.where(mine, own_routes, section_routes)
         partner_all = jnp.where(mine, half_routes, diagonal_routes)
         route_rows = lax.dynamic_slice_in_dim(route_all, section_index * piece, piece, 0)

time: 354 us -> 390 us (1.10)
  waiting for transfers between devices: 198 us -> 233 us
  other arithmetic: 11.9 us -> 41.5 us
  blocking collectives: 28.8 us -> 0 us
  matrix products: 62.2 us -> 42.4 us
  starting transfers between devices: 33.1 us -> 49.1 us
  local copies, waits for them, and re-layouts: 17.7 us -> 22.5 us
    all_to_all x1 -> x0, blocking collectives: 28.8 us -> none  [expert_layer(): arrived = lax.all_to_all(outgoing, ('fsdp', 'inner'), 0, 0, tiled=True)]
    all_to_all x1 -> x2, waiting for transfers between devices: 29.9 us -> 48.8 us  [expert_layer(): arrived = lax.all_to_all(outgoing, ('fsdp', 'inner'), 0, 0, tiled=True)]
    select_n x1 -> x4, other arithmetic: 0.01 us -> 18.2 us  [body(): jnp.where(mine, a, b)]
    all_to_all x2, starting transfers between devices: 8.82 us -> 26.6 us  [expert_layer(): lax.all_to_all(sending.reshape(sources, group_slots, chunk), ('fsdp', 'zh...]
    dot_general x8 -> x4, matrix products: 45.2 us -> 27.5 us  [gate_and_up(): jnp.einsum('sjcd,jdh->sjch', rows_in, gate_up_w, preferred_element_type=j...]
    concatenate x0 -> x1, other arithmetic: none -> 8.72 us  [body(): jnp.concatenate([gate_sel, up_sel], axis=-1)]
    ppermute x3, waiting for transfers between devices: 12.4 us -> 21 us  [other_half(): return lax.ppermute(value, 'zhalf', [(0, 1), (1, 0)])]
    ppermute x3, starting transfers between devices: 8.76 us -> 0.21 us  [other_half(): return lax.ppermute(value, 'zhalf', [(0, 1), (1, 0)])]
  transfers between devices with their start and end apart: 19 -> 20, of which waited for: 11 -> 14; matrix products, arithmetic and copies ran while one was open for 12% -> 10% of each run, Pallas kernels for 0% -> 0%
where the time goes in v3:
time: 390 us
  waiting for transfers between devices  233 us (60%)
  starting transfers between devices  49.1 us (13%)
  matrix products  42.4 us (11%)
  other arithmetic  41.5 us (11%)
  local copies, waits for them, and re-layouts  22.5 us (6%)
    all_to_all x2, waiting for transfers between devices, expert_layer(): lax.all_to_all(sending.reshape(sources, group_slots, chunk), ('fsdp', 'zh...  77.8 us
    ppermute x2, waiting for transfers between devices, expert_layer(): lax.ppermute(outgoing_part, 'fsdp', ring_pairs(fsdp_count, shift))  54 us
    all_to_all x2, waiting for transfers between devices, expert_layer(): arrived = lax.all_to_all(outgoing, ('fsdp', 'inner'), 0, 0, tiled=True)  48.8 us
    dot_general x4, matrix products, gate_and_up(): jnp.einsum('sjcd,jdh->sjch', rows_in, gate_up_w, preferred_element_type=j...  27.5 us
    all_to_all x2, starting transfers between devices, expert_layer(): lax.all_to_all(sending.reshape(sources, group_slots, chunk), ('fsdp', 'zh...  26.6 us
    ppermute x2, waiting for transfers between devices, expert_layer(): lax.ppermute(inner_act, 'fsdp', ring_pairs(fsdp_count, shift))  21.3 us
    ppermute x3, waiting for transfers between devices, other_half(): return lax.ppermute(value, 'zhalf', [(0, 1), (1, 0)])  21 us
    select_n x4, other arithmetic, body(): jnp.where(mine, a, b)  18.2 us
  transfers between devices with their start and end apart: 20, of which 14 were waited for; matrix products, arithmetic and copies ran while one was open for 10% of the time, Pallas kernels for 0%

profile of v3, /device:TPU:0, one launch (start us, length us, event | category | flops | bytes accessed | tf_op | source)
XLA Modules:
  0.0 389.7 jit_solution(285417184381784171)
XLA Ops:
  20.1 6.9 %collective-permute-done.6 = bf16[64,2048]{1,0:T(8,128)(2,1)S(1)} collective-permute-done((bf16[64,2048]{1,0:T(8,128)(2,1)S(1)}, bf16[64,2048]{1,0:T(8,128)(2,1)S(1)}, u32[]{:S(2)}, u32[]{:S(2)}) %collective-permute-start.6) | collective-permute-done | bytes 262176 | tf_op jit(solution)/shard_map/ppermute | solution.py:47
  34.3 25.3 %all-to-all-done = bf16[8,112,1024]{2,1,0:T(8,128)(2,1)} async-done(((bf16[8,112,1024]{2,1,0:T(8,128)(2,1)}), bf16[8,112,1024]{2,1,0:T(8,128)(2,1)}, u32[]{:S(2)}, u32[]{:S(2)}) %all-to-all-start) | async-done | bytes 1835040 | tf_op jit(solution)/shard_map/all_to_all | solution.py:93
  63.6 5.3 %broadcast_select_fusion.1 = (bf16[4,1024,768]{2,1,0:T(8,128)(2,1)S(1)}, bf16[4,1024,768]{2,1,0:T(8,128)(2,1)S(1)}) fusion(bf16[4,1024,768]{2,1,0:T(8,128)(2,1)} %collective-permute-done.4, pred[]{:T(512)S(6)} %eq.244, bf16[1,4,1024,768]{3,2,1,0:T(8,128)(2,1)} %param.13, pred[]{:T(512)S(6)} %eq.215), kind=kLoop, calls=%fused_computation.17 | loop fusion | flops 6291456 | bytes 25165826 | tf_op jit(solution)/shard_map/jit(_where)/select_n | solution.py:170
  68.9 5.4 %broadcast_select_fusion.2 = (bf16[4,1024,768]{2,1,0:T(8,128)(2,1)S(1)}, bf16[4,1024,768]{2,1,0:T(8,128)(2,1)S(1)}) fusion(bf16[4,1024,768]{2,1,0:T(8,128)(2,1)} %collective-permute-done.3, pred[]{:T(512)S(6)} %eq.244, bf16[1,4,1024,768]{3,2,1,0:T(8,128)(2,1)} %param.12, pred[]{:T(512)S(6)} %eq.215), kind=kLoop, calls=%fused_computation.18 | loop fusion | flops 6291456 | bytes 25165826 | tf_op jit(solution)/shard_map/jit(_where)/select_n | solution.py:170
  74.3 8.7 %pad_maximum_fusion = (bf16[4,1024,1536]{2,1,0:T(8,128)(2,1)}, bf16[4,1024,1536]{2,1,0:T(8,128)(2,1)}) fusion(bf16[4,1024,768]{2,1,0:T(8,128)(2,1)S(1)} %get-tuple-element.32, bf16[4,1024,768]{2,1,0:T(8,128)(2,1)S(1)} %get-tuple-element.30, bf16[4,1024,768]{2,1,0:T(8,128)(2,1)S(1)} %get-tuple-element.31, bf16[4,1024,768]{2,1,0:T(8,128)(2,1)S(1)} %get-tuple-element.29), kind=kLoop, calls=%fused_computation.2 | loop fusion | flops 50331648 | bytes 50331648 | tf_op jit(solution)/shard_map/concatenate | solution.py:171
  83.1 7.5 %broadcast_select_fusion = (bf16[4,768,1024]{2,1,0:T(8,128)(2,1)}, bf16[4,768,1024]{2,1,0:T(8,128)(2,1)}) fusion(bf16[4,768,1024]{2,1,0:T(8,128)(2,1)} %collective-permute-done.5, pred[]{:T(512)S(6)} %eq.244, bf16[1,4,768,1024]{3,2,1,0:T(8,128)(2,1)S(1)} %bitcast.258, pred[]{:T(512)S(6)} %eq.215), kind=kLoop, calls=%fused_computation.16 | loop fusion | flops 6291456 | bytes 25165826 | tf_op jit(solution)/shard_map/jit(_where)/select_n | solution.py:170
  90.6 6.6 %fusion.33 = bf16[8,4,14,1536]{3,2,0,1:T(8,128)(2,1)S(1)} fusion(bf16[4,1024,1536]{2,1,0:T(8,128)(2,1)} %get-tuple-element.8, bf16[1,8,4,14,1024]{4,3,2,1,0:T(8,128)(2,1)} %get-tuple-element.36), kind=kOutput, calls=%fused_computation.29 | convolution fusion | flops 1409974272 | bytes 14876672 | tf_op jit(solution)/shard_map/sjcd,jdh->sjch/dot_general | solution.py:99
  98.5 27.8 %collective-permute-done.9 = bf16[8,4,14,1536]{3,0,2,1:T(8,128)(2,1)S(1)} collective-permute-done((bf16[8,4,14,1536]{3,0,2,1:T(8,128)(2,1)S(1)}, bf16[8,4,14,1536]{3,0,2,1:T(8,128)(2,1)S(1)}, u32[]{:S(2)}, u32[]{:S(2)}) %collective-permute-start.9) | collective-permute-done | bytes 1376288 | tf_op jit(solution)/shard_map/ppermute | solution.py:107
  127.5 7.2 %fusion.15 = f32[8,4,14,1536]{3,2,0,1:T(8,128)S(1)} fusion(bf16[4,1024,1536]{2,1,0:T(8,128)(2,1)} %get-tuple-element.8, bf16[8,4,14,1536]{3,0,2,1:T(8,128)(2,1)} %copy-done.7, bf16[1,8,4,14,1024]{4,3,2,1,0:T(8,128)(2,1)} %get-tuple-element.35), kind=kOutput, calls=%fused_computation.23 | convolution fusion | flops 1410662400 | bytes 17629184 | tf_op jit(solution)/shard_map/sjcd,jdh->sjch/dot_general | solution.py:99
  137.0 11.2 %collective-permute-done.10 = bf16[8,4,14,768]{3,0,2,1:T(8,128)(2,1)S(1)} collective-permute-done((bf16[8,4,14,768]{3,0,2,1:T(8,128)(2,1)S(1)}, bf16[8,4,14,768]{3,0,2,1:T(8,128)(2,1)S(1)}, u32[]{:S(2)}, u32[]{:S(2)}) %collective-permute-start.10) | collective-permute-done | bytes 688160 | tf_op jit(solution)/shard_map/ppermute | solution.py:116
  149.5 4.6 %convert_bitcast_fusion.1 = bf16[2,2,4,4,14,1024]{5,4,1,2,0,3:T(8,128)(2,1)S(1)} fusion(bf16[4,768,1024]{2,1,0:T(8,128)(2,1)} %get-tuple-element.7, bf16[2,4,2,4,14,768]{5,4,2,1,3,0:T(8,128)(2,1)S(1)} %bitcast.266), kind=kOutput, calls=%fused_computation.35 | convolution fusion | flops 1410203648 | bytes 9502720 | tf_op jit(solution)/shard_map/fipjch,jhd->fpijcd/dot_general | solution.py:124
  155.8 11.6 %all-to-all-start.1 = ((bf16[16,56,1024]{2,1,0:T(8,128)(2,1)}), bf16[16,56,1024]{2,1,0:T(8,128)(2,1)S(1)}, u32[]{:S(2)}, u32[]{:S(2)}) async-start(bf16[16,56,1024]{2,1,0:T(8,128)(2,1)} %reshape.267), calls=%async_computation.1 | async-start | bytes 3670016 | tf_op jit(solution)/shard_map/all_to_all | solution.py:127
  169.4 38.2 %all-to-all-done.1 = bf16[16,56,1024]{2,1,0:T(8,128)(2,1)S(1)} async-done(((bf16[16,56,1024]{2,1,0:T(8,128)(2,1)}), bf16[16,56,1024]{2,1,0:T(8,128)(2,1)S(1)}, u32[]{:S(2)}, u32[]{:S(2)}) %all-to-all-start.1) | async-done | bytes 1835040 | tf_op jit(solution)/shard_map/all_to_all | solution.py:127
  209.6 11.4 %collective-permute-done.11 = bf16[64,2048]{1,0:T(8,128)(2,1)S(1)} collective-permute-done((bf16[64,2048]{1,0:T(8,128)(2,1)S(1)}, bf16[64,2048]{1,0:T(8,128)(2,1)S(1)}, u32[]{:S(2)}, u32[]{:S(2)}) %collective-permute-start.11) | collective-permute-done | bytes 262176 | tf_op jit(solution)/shard_map/ppermute | solution.py:47
  223.7 4.5 %all-to-all-start.2 = ((bf16[8,112,1024]{2,1,0:T(8,128)(2,1)}), bf16[8,112,1024]{2,1,0:T(8,128)(2,1)}, u32[]{:S(2)}, u32[]{:S(2)}) async-start(bf16[8,112,1024]{2,1,0:T(8,128)(2,1)} %bitcast.46), calls=%async_computation.2 | async-start | bytes 3670016 | tf_op jit(solution)/shard_map/all_to_all | solution.py:93
  228.2 23.5 %all-to-all-done.2 = bf16[8,112,1024]{2,1,0:T(8,128)(2,1)} async-done(((bf16[8,112,1024]{2,1,0:T(8,128)(2,1)}), bf16[8,112,1024]{2,1,0:T(8,128)(2,1)}, u32[]{:S(2)}, u32[]{:S(2)}) %all-to-all-start.2) | async-done | bytes 1835040 | tf_op jit(solution)/shard_map/all_to_all | solution.py:93
  255.6 6.4 %fusion.30 = bf16[8,4,14,1536]{3,2,0,1:T(8,128)(2,1)S(1)} fusion(bf16[4,1024,1536]{2,1,0:T(8,128)(2,1)} %get-tuple-element.10, bf16[1,8,4,14,1024]{4,3,2,1,0:T(8,128)(2,1)S(1)} %get-tuple-element.34), kind=kOutput, calls=%fused_computation.28 | convolution fusion | flops 1409974272 | bytes 14876672 | tf_op jit(solution)/shard_map/sjcd,jdh->sjch/dot_general | solution.py:99
  263.8 26.2 %collective-permute-done.12 = bf16[8,4,14,1536]{3,0,2,1:T(8,128)(2,1)S(1)} collective-permute-done((bf16[8,4,14,1536]{3,0,2,1:T(8,128)(2,1)S(1)}, bf16[8,4,14,1536]{3,0,2,1:T(8,128)(2,1)S(1)}, u32[]{:S(2)}, u32[]{:S(2)}) %collective-permute-start.12) | collective-permute-done | bytes 1376288 | tf_op jit(solution)/shard_map/ppermute | solution.py:107
  291.1 7.2 %fusion.21 = f32[8,4,14,1536]{3,2,0,1:T(8,128)S(1)} fusion(bf16[4,1024,1536]{2,1,0:T(8,128)(2,1)} %get-tuple-element.10, bf16[8,4,14,1536]{3,0,2,1:T(8,128)(2,1)} %copy-done.8, bf16[1,8,4,14,1024]{4,3,2,1,0:T(8,128)(2,1)} %get-tuple-element.33), kind=kOutput, calls=%fused_computation.25 | convolution fusion | flops 1410662400 | bytes 17629184 | tf_op jit(solution)/shard_map/sjcd,jdh->sjch/dot_general | solution.py:99
  301.3 10.1 %collective-permute-done.13 = bf16[8,4,14,768]{3,0,2,1:T(8,128)(2,1)S(1)} collective-permute-done((bf16[8,4,14,768]{3,0,2,1:T(8,128)(2,1)S(1)}, bf16[8,4,14,768]{3,0,2,1:T(8,128)(2,1)S(1)}, u32[]{:S(2)}, u32[]{:S(2)}) %collective-permute-start.13) | collective-permute-done | bytes 688160 | tf_op jit(solution)/shard_map/ppermute | solution.py:116
  312.6 4.6 %convert_bitcast_fusion = bf16[2,2,4,4,14,1024]{5,4,1,2,0,3:T(8,128)(2,1)S(1)} fusion(bf16[4,768,1024]{2,1,0:T(8,128)(2,1)} %get-tuple-element.9, bf16[2,4,2,4,14,768]{5,4,2,1,3,0:T(8,128)(2,1)S(1)} %bitcast.265), kind=kOutput, calls=%fused_computation.34 | convolution fusion | flops 1410203648 | bytes 9502720 | tf_op jit(solution)/shard_map/fipjch,jhd->fpijcd/dot_general | solution.py:124
  318.9 15.0 %all-to-all-start.3 = ((bf16[16,56,1024]{2,1,0:T(8,128)(2,1)}), bf16[16,56,1024]{2,1,0:T(8,128)(2,1)S(1)}, u32[]{:S(2)}, u32[]{:S(2)}) async-start(bf16[16,56,1024]{2,1,0:T(8,128)(2,1)} %reshape.268), calls=%async_computation.3 | async-start | bytes 3670016 | tf_op jit(solution)/shard_map/all_to_all | solution.py:127
  334.7 39.6 %all-to-all-done.3 = bf16[16,56,1024]{2,1,0:T(8,128)(2,1)S(1)} async-done(((bf16[16,56,1024]{2,1,0:T(8,128)(2,1)}), bf16[16,56,1024]{2,1,0:T(8,128)(2,1)S(1)}, u32[]{:S(2)}, u32[]{:S(2)}) %all-to-all-start.3) | async-done | bytes 1835040 | tf_op jit(solution)/shard_map/all_to_all | solution.py:127
  381.6 6.7 %all-to-all-done.4 = f32[32,1,2]{2,1,0:T(1,128)S(1)} async-done(((f32[32,1,2]{2,1,0:T(1,128)}), f32[32,1,2]{2,1,0:T(1,128)S(1)}, u32[]{:S(2)}, u32[]{:S(2)}) %all-to-all-start.4) | async-done | bytes 288 | tf_op jit(solution)/shard_map/all_to_all | solution.py:185
  (167 shorter events, 66.7 us)
Async XLA Ops:
  0.6 19.4 %copy-start.6 = (f32[1,2048]{1,0:T(1,128)S(1)}, f32[1,2048]{1,0:T(1,128)}, u32[]{:S(2)}) copy-start(f32[1,2048]{1,0:T(1,128)} %param.10) | copy-start | bytes 24580
  1.4 11.4 %collective-permute-start = (s32[128,6]{1,0:T(8,128)S(1)}, s32[128,6]{1,0:T(8,128)S(1)}, u32[]{:S(2)}, u32[]{:S(2)}) collective-permute-start(s32[128,6]{1,0:T(8,128)S(1)} %bitcast.271), channel_id=1, source_target_pairs={{0,16},{16,0},{1,17},{17,1},{2,18},{18,2},{3,19},{19,3},{4,20},{20... | collective-permute-start | bytes 9224 | tf_op jit(solution)/shard_map/ppermute | solution.py:14
  2.0 7.5 %collective-permute-start.8 = (s32[128,6]{1,0:T(8,128)S(1)}, s32[128,6]{1,0:T(8,128)S(1)}, u32[]{:S(2)}, u32[]{:S(2)}) collective-permute-start(s32[128,6]{1,0:T(8,128)S(1)} %bitcast.272), channel_id=1, source_target_pairs={{0,20},{20,0},{4,16},{16,4},{1,21},{21,1},{5,17},{17,5},{2,22},{22... | collective-permute-start | bytes 9224 | tf_op jit(solution)/shard_map/ppermute | solution.py:162
  5.7 6.9 %collective-permute-start.7 = (s32[128,6]{1,0:T(8,128)S(1)}, s32[128,6]{1,0:T(8,128)S(1)}, u32[]{:S(2)}, u32[]{:S(2)}) collective-permute-start(s32[128,6]{1,0:T(8,128)S(1)} %bitcast.273), channel_id=1, source_target_pairs={{0,4},{4,0},{1,5},{5,1},{2,6},{6,2},{3,7},{7,3},{8,12},{12,8},{9,1... | collective-permute-start | bytes 9224 | tf_op jit(solution)/shard_map/ppermute | solution.py:47
  5.7 14.3 %collective-permute-start.1 = (f32[2048]{0:T(1024)}, f32[2048]{0:T(1024)S(1)}, u32[]{:S(2)}, u32[]{:S(2)}) collective-permute-start(f32[2048]{0:T(1024)} %bitcast.279), channel_id=1, source_target_pairs={{0,16},{16,0},{1,17},{17,1},{2,18},{18,2},{3,19},{19,3},{4,20},{20... | collective-permute-start | bytes 24584 | tf_op jit(solution)/shard_map/ppermute | solution.py:14
  5.8 57.8 %collective-permute-start.4 = (bf16[4,1024,768]{2,1,0:T(8,128)(2,1)}, bf16[4,1024,768]{2,1,0:T(8,128)(2,1)}, u32[]{:S(2)}, u32[]{:S(2)}) collective-permute-start(bf16[4,1024,768]{2,1,0:T(8,128)(2,1)} %bitcast.254), channel_id=1, source_target_pairs={{0,16},{16,0},{1,17},{17,1},{2,18},{18,2},{3,19},{19,3},{4,20},{20... | collective-permute-start | bytes 18874376 | tf_op jit(solution)/shard_map/ppermute | solution.py:14
  9.5 59.4 %collective-permute-start.3 = (bf16[4,1024,768]{2,1,0:T(8,128)(2,1)}, bf16[4,1024,768]{2,1,0:T(8,128)(2,1)}, u32[]{:S(2)}, u32[]{:S(2)}) collective-permute-start(bf16[4,1024,768]{2,1,0:T(8,128)(2,1)} %bitcast.255), channel_id=1, source_target_pairs={{0,16},{16,0},{1,17},{17,1},{2,18},{18,2},{3,19},{19,3},{4,20},{20... | collective-permute-start | bytes 18874376 | tf_op jit(solution)/shard_map/ppermute | solution.py:14
  12.5 14.4 %collective-permute-start.6 = (bf16[64,2048]{1,0:T(8,128)(2,1)S(1)}, bf16[64,2048]{1,0:T(8,128)(2,1)S(1)}, u32[]{:S(2)}, u32[]{:S(2)}) collective-permute-start(bf16[64,2048]{1,0:T(8,128)(2,1)S(1)} %get-tuple-element.26), channel_id=1, source_target_pairs={{0,4},{4,0},{1,5},{5,1},{2,6},{6,2},{3,7},{7,3},{8,12},{12,8},{9,1... | collective-permute-start | bytes 786440 | tf_op jit(solution)/shard_map/ppermute | solution.py:47
  29.7 29.9 %all-to-all-start = ((bf16[8,112,1024]{2,1,0:T(8,128)(2,1)}), bf16[8,112,1024]{2,1,0:T(8,128)(2,1)}, u32[]{:S(2)}, u32[]{:S(2)}) async-start(bf16[8,112,1024]{2,1,0:T(8,128)(2,1)} %bitcast.20), calls=%async_computation | async-start | bytes 3670016 | tf_op jit(solution)/shard_map/all_to_all | solution.py:93
  34.2 48.9 %collective-permute-start.5 = (bf16[4,768,1024]{2,1,0:T(8,128)(2,1)}, bf16[4,768,1024]{2,1,0:T(8,128)(2,1)}, u32[]{:S(2)}, u32[]{:S(2)}) collective-permute-start(bf16[4,768,1024]{2,1,0:T(8,128)(2,1)} %bitcast.256), channel_id=1, source_target_pairs={{0,16},{16,0},{1,17},{17,1},{2,18},{18,2},{3,19},{19,3},{4,20},{20... | collective-permute-start | bytes 18874376 | tf_op jit(solution)/shard_map/ppermute | solution.py:14
  97.9 28.4 %collective-permute-start.9 = (bf16[8,4,14,1536]{3,0,2,1:T(8,128)(2,1)S(1)}, bf16[8,4,14,1536]{3,0,2,1:T(8,128)(2,1)S(1)}, u32[]{:S(2)}, u32[]{:S(2)}) collective-permute-start(bf16[8,4,14,1536]{3,0,2,1:T(8,128)(2,1)S(1)} %copy.164), channel_id=1, source_target_pairs={{0,8},{8,0},{1,9},{9,1},{2,10},{10,2},{3,11},{11,3},{4,12},{12,4},... | collective-permute-start | bytes 4128776 | tf_op jit(solution)/shard_map/ppermute | solution.py:107
  135.4 12.8 %collective-permute-start.10 = (bf16[8,4,14,768]{3,0,2,1:T(8,128)(2,1)S(1)}, bf16[8,4,14,768]{3,0,2,1:T(8,128)(2,1)S(1)}, u32[]{:S(2)}, u32[]{:S(2)}) collective-permute-start(bf16[8,4,14,768]{3,0,2,1:T(8,128)(2,1)S(1)} %copy.166), channel_id=1, source_target_pairs={{0,8},{8,0},{1,9},{9,1},{2,10},{10,2},{3,11},{11,3},{4,12},{12,4},... | collective-permute-start | bytes 2064392 | tf_op jit(solution)/shard_map/ppermute | solution.py:116
  155.8 51.8 %all-to-all-start.1 = ((bf16[16,56,1024]{2,1,0:T(8,128)(2,1)}), bf16[16,56,1024]{2,1,0:T(8,128)(2,1)S(1)}, u32[]{:S(2)}, u32[]{:S(2)}) async-start(bf16[16,56,1024]{2,1,0:T(8,128)(2,1)} %reshape.267), calls=%async_computation.1 | async-start | bytes 3670016 | tf_op jit(solution)/shard_map/all_to_all | solution.py:127
  167.4 1.4 collective-permute-start.2
  168.8 38.9 %copy-start.11 = (bf16[2048,32]{0,1:T(8,128)(2,1)}, bf16[2048,32]{0,1:T(8,128)(2,1)S(1)}, u32[]{:S(2)}) copy-start(bf16[2048,32]{0,1:T(8,128)(2,1)S(1)} %collective-permute-done.2) | copy-start | bytes 393220
  209.4 11.6 %collective-permute-start.11 = (bf16[64,2048]{1,0:T(8,128)(2,1)S(1)}, bf16[64,2048]{1,0:T(8,128)(2,1)S(1)}, u32[]{:S(2)}, u32[]{:S(2)}) collective-permute-start(bf16[64,2048]{1,0:T(8,128)(2,1)S(1)} %get-tuple-element.49), channel_id=1, source_target_pairs={{0,4},{4,0},{1,5},{5,1},{2,6},{6,2},{3,7},{7,3},{8,12},{12,8},{9,1... | collective-permute-start | bytes 786440 | tf_op jit(solution)/shard_map/ppermute | solution.py:47
  223.7 28.1 %all-to-all-start.2 = ((bf16[8,112,1024]{2,1,0:T(8,128)(2,1)}), bf16[8,112,1024]{2,1,0:T(8,128)(2,1)}, u32[]{:S(2)}, u32[]{:S(2)}) async-start(bf16[8,112,1024]{2,1,0:T(8,128)(2,1)} %bitcast.46), calls=%async_computation.2 | async-start | bytes 3670016 | tf_op jit(solution)/shard_map/all_to_all | solution.py:93
  262.7 27.2 %collective-permute-start.12 = (bf16[8,4,14,1536]{3,0,2,1:T(8,128)(2,1)S(1)}, bf16[8,4,14,1536]{3,0,2,1:T(8,128)(2,1)S(1)}, u32[]{:S(2)}, u32[]{:S(2)}) collective-permute-start(bf16[8,4,14,1536]{3,0,2,1:T(8,128)(2,1)S(1)} %copy.184), channel_id=1, source_target_pairs={{0,8},{8,0},{1,9},{9,1},{2,10},{10,2},{3,11},{11,3},{4,12},{12,4},... | collective-permute-start | bytes 4128776 | tf_op jit(solution)/shard_map/ppermute | solution.py:107
  299.0 12.4 %collective-permute-start.13 = (bf16[8,4,14,768]{3,0,2,1:T(8,128)(2,1)S(1)}, bf16[8,4,14,768]{3,0,2,1:T(8,128)(2,1)S(1)}, u32[]{:S(2)}, u32[]{:S(2)}) collective-permute-start(bf16[8,4,14,768]{3,0,2,1:T(8,128)(2,1)S(1)} %copy.186), channel_id=1, source_target_pairs={{0,8},{8,0},{1,9},{9,1},{2,10},{10,2},{3,11},{11,3},{4,12},{12,4},... | collective-permute-start | bytes 2064392 | tf_op jit(solution)/shard_map/ppermute | solution.py:116
  318.9 15.2 %copy-start.10 = (bf16[1,2048,32]{1,2,0:T(8,128)(2,1)S(1)}, bf16[1,2048,32]{1,2,0:T(8,128)(2,1)}, u32[]{:S(2)}) copy-start(bf16[1,2048,32]{1,2,0:T(8,128)(2,1)} %param.11) | copy-start | bytes 393220
  318.9 15.2 %copy-start.12 = (bf16[2048,32]{0,1:T(8,128)(2,1)S(1)}, bf16[2048,32]{0,1:T(8,128)(2,1)}, u32[]{:S(2)}) copy-start(bf16[2048,32]{0,1:T(8,128)(2,1)} %copy-done.11) | copy-start | bytes 393220
  318.9 55.4 %all-to-all-start.3 = ((bf16[16,56,1024]{2,1,0:T(8,128)(2,1)}), bf16[16,56,1024]{2,1,0:T(8,128)(2,1)S(1)}, u32[]{:S(2)}, u32[]{:S(2)}) async-start(bf16[16,56,1024]{2,1,0:T(8,128)(2,1)} %reshape.268), calls=%async_computation.3 | async-start | bytes 3670016 | tf_op jit(solution)/shard_map/all_to_all | solution.py:127
  378.1 10.2 %all-to-all-start.4 = ((f32[32,1,2]{2,1,0:T(1,128)}), f32[32,1,2]{2,1,0:T(1,128)S(1)}, u32[]{:S(2)}, u32[]{:S(2)}) async-start(f32[32,1,2]{2,1,0:T(1,128)} %broadcast_in_dim.32), calls=%async_computation.4 | async-start | bytes 32768 | tf_op jit(solution)/shard_map/all_to_all | solution.py:185
  381.2 7.7 %collective-permute-start.14 = (bf16[64,1024]{1,0:T(8,128)(2,1)S(1)}, bf16[64,1024]{1,0:T(8,128)(2,1)S(1)}, u32[]{:S(2)}, u32[]{:S(2)}) collective-permute-start(bf16[64,1024]{1,0:T(8,128)(2,1)S(1)} %get-tuple-element.42), channel_id=1, source_target_pairs={{0,16},{16,0},{1,17},{17,1},{2,18},{18,2},{3,19},{19,3},{4,20},{20... | collective-permute-start | bytes 393224 | tf_op jit(solution)/shard_map/ppermute | solution.py:14
  (11 other events, 117.0 us)

commit v4 on v2

--- a/solution.py
+++ b/solution.py
@@ -76,21 +76,24 @@
     half_slots = experts_count // halves * capacity
     local_ids = half_index * half_slots + jnp.arange(half_slots, dtype=jnp.int32)
     first_half = half_index == 0
-    lower_normed = jnp.where(first_half, normed, partner_normed)
-    upper_normed = jnp.where(first_half, partner_normed, normed)
-    lower_positions = jnp.where(first_half, positions, partner_positions)
-    upper_positions = jnp.where(first_half, partner_positions, positions)
-    lower_buffer = half_buffer(lower_positions, lower_normed, local_ids, fsdp_count, chunk)
-    upper_buffer = half_buffer(upper_positions, upper_normed, local_ids, fsdp_count, chunk)
     group_slots = local_experts * capacity
-    outgoing = jnp.stack(
-        [
-            lower_buffer.reshape(fsdp_count, inner_devices, group_slots, chunk),
-            upper_buffer.reshape(fsdp_count, inner_devices, group_slots, chunk),
-        ],
-        axis=2,
-    ).reshape(fsdp_count * inner_devices, halves * group_slots, chunk)
-    arrived = lax.all_to_all(outgoing, ("fsdp", "inner"), 0, 0, tiled=True)
+    own_buffer = half_buffer(positions, normed, local_ids, fsdp_count, chunk)
+    own_arrived = lax.all_to_all(
+        own_buffer.reshape(fsdp_count * inner_devices, group_slots, chunk), ("fsdp", "inner"), 0, 0, tiled=True
+    )
+    partner_buffer = half_buffer(partner_positions, partner_normed, local_ids, fsdp_count, chunk)
+    partner_arrived = lax.all_to_all(
+        partner_buffer.reshape(fsdp_count * inner_devices, group_slots, chunk),
+        ("fsdp", "inner"),
+        0,
+        0,
+        tiled=True,
+    )
+    arrived = jnp.where(
+        first_half,
+        jnp.stack([own_arrived, partner_arrived], axis=1),
+        jnp.stack([partner_arrived, own_arrived], axis=1),
+    )
     sources = fsdp_count * inner_devices * halves
     arrived = arrived.reshape(sources, local_experts, capacity, chunk)
     arrived_blocks = arrived.reshape(fsdp_count, sources // fsdp_count, local_experts, capacity, chunk)

time: 354 us -> 374 us (1.056)
  blocking collectives: 28.8 us -> 16.1 us
  matrix products: 62.2 us -> 73.9 us
  waiting for transfers between devices: 198 us -> 209 us
  local copies, waits for them, and re-layouts: 17.7 us -> 23.8 us
  starting transfers between devices: 33.1 us -> 38.8 us
    dot_general x2, matrix products: 11.3 us -> 24.4 us  [expert_layer(): jnp.einsum('fipjch,jhd->fpijcd', inner_all, down_w, preferred_element_typ...]
    all_to_all x1, blocking collectives: 28.8 us -> 16.1 us  [expert_layer(): lax.all_to_all(partner_buffer.reshape(fsdp_count * inner_devices, group_s...]
    all_to_all x1 -> x3, waiting for transfers between devices: 29.9 us -> 42.6 us  [the longest x2 28.9 us: expert_layer(): lax.all_to_all(own_buffer.reshape(fsdp_count * inner_devices, group_slots...]
    ppermute x1, waiting for transfers between devices: 7.51 us -> 0.01 us  [body(): lax.ppermute(own_routes, ('section', 'zhalf'), [(0, 3), (3, 0), (1, 2), (...]
    select_n x4, local copies, waits for them, and re-layouts: 0.28 us -> 7.32 us  [expert_layer(): jnp.where(first_half, jnp.stack([own_arrived, partner_arrived], axis=1),...]
    all_to_all x1 -> x3, starting transfers between devices: 4.51 us -> 11.2 us  [the longest x2 7.26 us: expert_layer(): lax.all_to_all(own_buffer.reshape(fsdp_count * inner_devices, group_slots...]
    dot_general x4, matrix products: 22.1 us -> 16.7 us  [gate_and_up(): jnp.einsum('sjcd,jdh->sjch', rows_in, gate_w, preferred_element_type=jnp....]
    another operation x5 -> x3, local copies, waits for them, and re-layouts: 5.75 us -> 0.66 us  [the longest x2 5.09 us: expert_layer(): arrived.reshape(fsdp_count, sources // fsdp_count, local_experts, capacit...]
  transfers between devices with their start and end apart: 19 -> 21, of which waited for: 11 -> 13; matrix products, arithmetic and copies ran while one was open for 12% -> 12% of each run, Pallas kernels for 0% -> 0%
where the time goes in v4:
time: 374 us
  waiting for transfers between devices  209 us (56%)
  matrix products  73.9 us (20%)
  starting transfers between devices  38.8 us (10%)
  local copies, waits for them, and re-layouts  23.8 us (6%)
  blocking collectives  16.1 us (4%)
  other arithmetic  11.5 us (3%)
    all_to_all x2, waiting for transfers between devices, expert_layer(): lax.all_to_all(sending.reshape(sources, group_slots, chunk), ('fsdp', 'zh...  68.3 us
    ppermute x2, waiting for transfers between devices, expert_layer(): lax.ppermute(outgoing_pair, 'fsdp', ring_pairs(fsdp_count, shift))  47.4 us
    all_to_all x2, waiting for transfers between devices, expert_layer(): lax.all_to_all(own_buffer.reshape(fsdp_count * inner_devices, group_slots...  28.9 us
    ppermute x2, waiting for transfers between devices, expert_layer(): lax.ppermute(inner_act, 'fsdp', ring_pairs(fsdp_count, shift))  26.6 us
    dot_general x2, matrix products, expert_layer(): jnp.einsum('fipjch,jhd->fpijcd', inner_all, down_w, preferred_element_typ...  24.4 us
    dot_general x4, matrix products, gate_and_up(): jnp.einsum('sjcd,jdh->sjch', rows_in, up_w, preferred_element_type=jnp.fl...  24.3 us
    dot_general x4, matrix products, gate_and_up(): jnp.einsum('sjcd,jdh->sjch', rows_in, gate_w, preferred_element_type=jnp....  16.7 us
    all_to_all x1, blocking collectives, expert_layer(): lax.all_to_all(partner_buffer.reshape(fsdp_count * inner_devices, group_s...  16.1 us
  transfers between devices with their start and end apart: 21, of which 13 were waited for; matrix products, arithmetic and copies ran while one was open for 12% of the time, Pallas kernels for 0%

profile of v4, /device:TPU:0, one launch (start us, length us, event | category | flops | bytes accessed | tf_op | source)
XLA Modules:
  0.0 374.2 jit_solution(13550461304890472666)
XLA Ops:
  1.3 4.1 %collective-permute-start.6 = (s32[128,6]{0,1:T(8,128)S(1)}, s32[128,6]{0,1:T(8,128)S(1)}, u32[]{:S(2)}, u32[]{:S(2)}) collective-permute-start(s32[128,6]{0,1:T(8,128)S(1)} %bitcast.383), channel_id=1, source_target_pairs={{0,4},{4,0},{1,5},{5,1},{2,6},{6,2},{3,7},{7,3},{8,12},{12,8},{9,1... | collective-permute-start | bytes 9224 | tf_op jit(solution)/shard_map/ppermute | solution.py:47
  24.0 3.9 %all-to-all-start.1 = ((bf16[8,56,1024]{2,1,0:T(8,128)(2,1)}), bf16[8,56,1024]{2,1,0:T(8,128)(2,1)S(1)}, u32[]{:S(2)}, u32[]{:S(2)}) async-start(bf16[8,56,1024]{2,1,0:T(8,128)(2,1)} %bitcast.16), calls=%async_computation.1 | async-start | bytes 1835008 | tf_op jit(solution)/shard_map/all_to_all | solution.py:85
  29.3 13.7 %all-to-all-done.1 = bf16[8,56,1024]{2,1,0:T(8,128)(2,1)S(1)} async-done(((bf16[8,56,1024]{2,1,0:T(8,128)(2,1)}), bf16[8,56,1024]{2,1,0:T(8,128)(2,1)S(1)}, u32[]{:S(2)}, u32[]{:S(2)}) %all-to-all-start.1) | async-done | bytes 917536 | tf_op jit(solution)/shard_map/all_to_all | solution.py:85
  46.7 12.9 %all-to-all-done = bf16[8,56,1024]{2,1,0:T(8,128)(2,1)S(1)} async-done(((bf16[8,56,1024]{2,1,0:T(8,128)(2,1)}), bf16[8,56,1024]{2,1,0:T(8,128)(2,1)S(1)}, u32[]{:S(2)}, u32[]{:S(2)}) %all-to-all-start) | async-done | bytes 917536 | tf_op jit(solution)/shard_map/all_to_all | solution.py:81
  65.5 5.0 %fusion.54 = bf16[1,8,4,14,768]{4,3,1,2,0:T(8,128)(2,1)S(1)} fusion(bf16[4,1024,768]{2,1,0:T(8,128)(2,1)} %collective-permute-done.8, pred[]{:T(512)S(6)} %eq.215, bf16[1,8,4,14,1024]{4,1,0,3,2:T(8,128)(2,1)S(1)} %get-tuple-element.17, bf16[1,4,1024,768]{3,2,1,0:T(8,128)(2,1)} %param.13), kind=kOutput, calls=%fused_computation.64 | convolution fusion | flops 708132864 | bytes 14188545 | tf_op jit(solution)/shard_map/sjcd,jdh->sjch/dot_general | solution.py:105
  77.4 28.3 %collective-permute-done.9 = bf16[2,8,4,14,768]{4,1,3,2,0:T(8,128)(2,1)S(1)} collective-permute-done((bf16[2,8,4,14,768]{4,1,3,2,0:T(8,128)(2,1)S(1)}, bf16[2,8,4,14,768]{4,1,3,2,0:T(8,128)(2,1)S(1)}, u32[]{:S(2)}, u32[]{:S(2)}) %collective-permute-start.9) | collective-permute-done | bytes 1376288 | tf_op jit(solution)/shard_map/ppermute | solution.py:114
  105.8 5.3 %fusion.33 = bf16[8,4,14,768]{3,2,0,1:T(8,128)(2,1)S(1)} fusion(f32[4,768,8,14]{1,3,2,0:T(8,128)S(1)} %copy-done.14, bf16[1,8,4,14,768]{4,1,3,2,0:T(8,128)(2,1)S(1)} %get-tuple-element.22, bf16[1,8,4,14,768]{4,1,3,2,0:T(8,128)(2,1)S(1)} %get-tuple-element.21, bf16[1,8,4,14,1024]{4,1,0,3,2:T(8,128)(2,1)S(1)} %get-tuple-element.18, ...), kind=kOutput, calls=%fused_computation.48 | convolution fusion | flops 711229440 | bytes 16941056 | tf_op jit(solution)/shard_map/sjcd,jdh->sjch/dot_general | solution.py:105
  112.0 16.2 %collective-permute-done.10 = bf16[8,4,14,768]{3,0,2,1:T(8,128)(2,1)S(1)} collective-permute-done((bf16[8,4,14,768]{3,0,2,1:T(8,128)(2,1)S(1)}, bf16[8,4,14,768]{3,0,2,1:T(8,128)(2,1)S(1)}, u32[]{:S(2)}, u32[]{:S(2)}) %collective-permute-start.10) | collective-permute-done | bytes 688160 | tf_op jit(solution)/shard_map/ppermute | solution.py:124
  129.4 17.6 %convert_bitcast_fusion.1 = bf16[2,2,4,4,14,1024]{5,4,1,2,0,3:T(8,128)(2,1)S(1)} fusion(bf16[4,768,1024]{2,1,0:T(8,128)(2,1)} %collective-permute-done.3, pred[]{:T(512)S(6)} %eq.215, bf16[2,4,2,4,14,768]{5,4,2,1,3,0:T(8,128)(2,1)S(1)} %bitcast.371, bf16[1,4,768,1024]{3,2,1,0:T(8,128)(2,1)} %param.14), kind=kOutput, calls=%fused_computation.35 | convolution fusion | flops 1413349376 | bytes 15794177 | tf_op jit(solution)/shard_map/fipjch,jhd->fpijcd/dot_general | solution.py:132
  148.7 4.9 %all-to-all-start.2 = ((bf16[16,56,1024]{2,1,0:T(8,128)(2,1)}), bf16[16,56,1024]{2,1,0:T(8,128)(2,1)S(1)}, u32[]{:S(2)}, u32[]{:S(2)}) async-start(bf16[16,56,1024]{2,1,0:T(8,128)(2,1)} %reshape.297), calls=%async_computation.2 | async-start | bytes 3670016 | tf_op jit(solution)/shard_map/all_to_all | solution.py:135
  158.1 37.6 %all-to-all-done.2 = bf16[16,56,1024]{2,1,0:T(8,128)(2,1)S(1)} async-done(((bf16[16,56,1024]{2,1,0:T(8,128)(2,1)}), bf16[16,56,1024]{2,1,0:T(8,128)(2,1)S(1)}, u32[]{:S(2)}, u32[]{:S(2)}) %all-to-all-start.2) | async-done | bytes 1835040 | tf_op jit(solution)/shard_map/all_to_all | solution.py:135
  199.8 12.6 %collective-permute-done.11 = bf16[64,2048]{1,0:T(8,128)(2,1)S(1)} collective-permute-done((bf16[64,2048]{1,0:T(8,128)(2,1)S(1)}, bf16[64,2048]{1,0:T(8,128)(2,1)S(1)}, u32[]{:S(2)}, u32[]{:S(2)}) %collective-permute-start.11) | collective-permute-done | bytes 262176 | tf_op jit(solution)/shard_map/ppermute | solution.py:47
  218.3 16.0 %all-to-all-done.3 = bf16[8,56,1024]{2,1,0:T(8,128)(2,1)S(1)} async-done(((bf16[8,56,1024]{2,1,0:T(8,128)(2,1)}), bf16[8,56,1024]{2,1,0:T(8,128)(2,1)S(1)}, u32[]{:S(2)}, u32[]{:S(2)}) %all-to-all-start.3) | async-done | bytes 917536 | tf_op jit(solution)/shard_map/all_to_all | solution.py:81
  234.3 16.1 %all_to_all.36 = bf16[8,56,1024]{2,1,0:T(8,128)(2,1)S(1)} all-to-all(bf16[8,56,1024]{2,1,0:T(8,128)(2,1)S(1)} %bitcast.362), channel_id=1, replica_groups=mesh['section'=2,'fsdp'=2,'zhalf'=2,'inner'=4] {'fsdp','inner'}, dimensions={0} | all-to-all | bytes 1835008 | tf_op jit(solution)/shard_map/all_to_all | solution.py:85
  256.1 6.8 %fusion.48 = bf16[1,8,4,14,768]{4,3,1,2,0:T(8,128)(2,1)S(1)} fusion(bf16[4,1024,768]{2,1,0:T(8,128)(2,1)} %collective-permute-done.8, pred[]{:T(512)S(6)} %eq.244, bf16[1,8,4,14,1024]{4,1,0,3,2:T(8,128)(2,1)S(1)} %get-tuple-element.15, bf16[1,4,1024,768]{3,2,1,0:T(8,128)(2,1)} %param.13), kind=kOutput, calls=%fused_computation.62 | convolution fusion | flops 708132864 | bytes 14188545 | tf_op jit(solution)/shard_map/sjcd,jdh->sjch/dot_general | solution.py:105
  263.0 5.0 %fusion.51 = bf16[1,8,4,14,768]{4,3,1,2,0:T(8,128)(2,1)S(1)} fusion(bf16[4,1024,768]{2,1,0:T(8,128)(2,1)} %collective-permute-done.4, pred[]{:T(512)S(6)} %eq.244, bf16[1,8,4,14,1024]{4,1,0,3,2:T(8,128)(2,1)S(1)} %get-tuple-element.15, bf16[1,4,1024,768]{3,2,1,0:T(8,128)(2,1)S(1)} %bitcast.390), kind=kOutput, calls=%fused_computation.63 | convolution fusion | flops 708132864 | bytes 14188545 | tf_op jit(solution)/shard_map/sjcd,jdh->sjch/dot_general | solution.py:102
  269.3 6.1 %fusion.10 = f32[4,768,8,14]{1,3,2,0:T(8,128)} fusion(bf16[4,1024,768]{2,1,0:T(8,128)(2,1)} %collective-permute-done.4, pred[]{:T(512)S(6)} %eq.244, bf16[1,8,4,14,1024]{4,1,0,3,2:T(8,128)(2,1)S(1)} %get-tuple-element.16, bf16[1,4,1024,768]{3,2,1,0:T(8,128)(2,1)S(1)} %bitcast.390), kind=kOutput, calls=%fused_computation.12 | convolution fusion | flops 707788800 | bytes 14876673 | tf_op jit(solution)/shard_map/sjcd,jdh->sjch/dot_general | solution.py:102
  275.4 19.1 %collective-permute-done.12 = bf16[2,8,4,14,768]{4,1,3,2,0:T(8,128)(2,1)S(1)} collective-permute-done((bf16[2,8,4,14,768]{4,1,3,2,0:T(8,128)(2,1)S(1)}, bf16[2,8,4,14,768]{4,1,3,2,0:T(8,128)(2,1)S(1)}, u32[]{:S(2)}, u32[]{:S(2)}) %collective-permute-start.12) | collective-permute-done | bytes 1376288 | tf_op jit(solution)/shard_map/ppermute | solution.py:114
  294.6 7.2 %fusion.31 = bf16[8,4,14,768]{3,2,0,1:T(8,128)(2,1)S(1)} fusion(f32[4,768,8,14]{1,3,2,0:T(8,128)S(1)} %copy-done.13, bf16[1,8,4,14,768]{4,1,3,2,0:T(8,128)(2,1)S(1)} %get-tuple-element.20, bf16[1,8,4,14,768]{4,1,3,2,0:T(8,128)(2,1)S(1)} %get-tuple-element.19, bf16[1,8,4,14,1024]{4,1,0,3,2:T(8,128)(2,1)S(1)} %get-tuple-element.16, ...), kind=kOutput, calls=%fused_computation.44 | convolution fusion | flops 711229440 | bytes 16941056 | tf_op jit(solution)/shard_map/sjcd,jdh->sjch/dot_general | solution.py:105
  302.6 10.4 %collective-permute-done.13 = bf16[8,4,14,768]{3,0,2,1:T(8,128)(2,1)S(1)} collective-permute-done((bf16[8,4,14,768]{3,0,2,1:T(8,128)(2,1)S(1)}, bf16[8,4,14,768]{3,0,2,1:T(8,128)(2,1)S(1)}, u32[]{:S(2)}, u32[]{:S(2)}) %collective-permute-start.13) | collective-permute-done | bytes 688160 | tf_op jit(solution)/shard_map/ppermute | solution.py:124
  314.2 6.8 %convert_bitcast_fusion = bf16[2,2,4,4,14,1024]{5,4,1,2,0,3:T(8,128)(2,1)S(1)} fusion(bf16[4,768,1024]{2,1,0:T(8,128)(2,1)} %collective-permute-done.3, pred[]{:T(512)S(6)} %eq.244, bf16[2,4,2,4,14,768]{5,4,2,1,3,0:T(8,128)(2,1)S(1)} %bitcast.372, bf16[1,4,768,1024]{3,2,1,0:T(8,128)(2,1)} %param.14), kind=kOutput, calls=%fused_computation.34 | convolution fusion | flops 1413349376 | bytes 15794177 | tf_op jit(solution)/shard_map/fipjch,jhd->fpijcd/dot_general | solution.py:132
  322.7 3.9 %all-to-all-start.5 = ((bf16[16,56,1024]{2,1,0:T(8,128)(2,1)}), bf16[16,56,1024]{2,1,0:T(8,128)(2,1)S(1)}, u32[]{:S(2)}, u32[]{:S(2)}) async-start(bf16[16,56,1024]{2,1,0:T(8,128)(2,1)} %reshape.298), calls=%async_computation.5 | async-start | bytes 3670016 | tf_op jit(solution)/shard_map/all_to_all | solution.py:135
  327.1 30.7 %all-to-all-done.5 = bf16[16,56,1024]{2,1,0:T(8,128)(2,1)S(1)} async-done(((bf16[16,56,1024]{2,1,0:T(8,128)(2,1)}), bf16[16,56,1024]{2,1,0:T(8,128)(2,1)S(1)}, u32[]{:S(2)}, u32[]{:S(2)}) %all-to-all-start.5) | async-done | bytes 1835040 | tf_op jit(solution)/shard_map/all_to_all | solution.py:135
  365.9 6.7 %all-to-all-done.6 = f32[32,1,2]{2,1,0:T(1,128)S(1)} async-done(((f32[32,1,2]{2,1,0:T(1,128)}), f32[32,1,2]{2,1,0:T(1,128)S(1)}, u32[]{:S(2)}, u32[]{:S(2)}) %all-to-all-start.6) | async-done | bytes 288 | tf_op jit(solution)/shard_map/all_to_all | solution.py:192
  (184 shorter events, 75.7 us)
Async XLA Ops:
  1.3 9.3 %collective-permute-start.6 = (s32[128,6]{0,1:T(8,128)S(1)}, s32[128,6]{0,1:T(8,128)S(1)}, u32[]{:S(2)}, u32[]{:S(2)}) collective-permute-start(s32[128,6]{0,1:T(8,128)S(1)} %bitcast.383), channel_id=1, source_target_pairs={{0,4},{4,0},{1,5},{5,1},{2,6},{6,2},{3,7},{7,3},{8,12},{12,8},{9,1... | collective-permute-start | bytes 9224 | tf_op jit(solution)/shard_map/ppermute | solution.py:47
  5.4 5.5 %collective-permute-start.7 = (s32[128,6]{0,1:T(8,128)S(1)}, s32[128,6]{0,1:T(8,128)S(1)}, u32[]{:S(2)}, u32[]{:S(2)}) collective-permute-start(s32[128,6]{0,1:T(8,128)S(1)} %bitcast.384), channel_id=1, source_target_pairs={{0,20},{20,0},{4,16},{16,4},{1,21},{21,1},{5,17},{17,5},{2,22},{22... | collective-permute-start | bytes 9224 | tf_op jit(solution)/shard_map/ppermute | solution.py:170
  5.4 4.2 %collective-permute-start = (s32[128,6]{0,1:T(8,128)S(1)}, s32[128,6]{0,1:T(8,128)S(1)}, u32[]{:S(2)}, u32[]{:S(2)}) collective-permute-start(s32[128,6]{0,1:T(8,128)S(1)} %bitcast.385), channel_id=1, source_target_pairs={{0,16},{16,0},{1,17},{17,1},{2,18},{18,2},{3,19},{19,3},{4,20},{20... | collective-permute-start | bytes 9224 | tf_op jit(solution)/shard_map/ppermute | solution.py:14
  5.5 13.3 %collective-permute-start.1 = (f32[2048]{0:T(1024)}, f32[2048]{0:T(1024)S(1)}, u32[]{:S(2)}, u32[]{:S(2)}) collective-permute-start(f32[2048]{0:T(1024)} %bitcast.381), channel_id=1, source_target_pairs={{0,16},{16,0},{1,17},{17,1},{2,18},{18,2},{3,19},{19,3},{4,20},{20... | collective-permute-start | bytes 24584 | tf_op jit(solution)/shard_map/ppermute | solution.py:14
  7.0 15.2 %collective-permute-start.5 = (bf16[64,2048]{1,0:T(8,128)(2,1)S(1)}, bf16[64,2048]{1,0:T(8,128)(2,1)S(1)}, u32[]{:S(2)}, u32[]{:S(2)}) collective-permute-start(bf16[64,2048]{1,0:T(8,128)(2,1)S(1)} %get-tuple-element.14), channel_id=1, source_target_pairs={{0,4},{4,0},{1,5},{5,1},{2,6},{6,2},{3,7},{7,3},{8,12},{12,8},{9,1... | collective-permute-start | bytes 786440 | tf_op jit(solution)/shard_map/ppermute | solution.py:47
  9.6 55.8 %collective-permute-start.8 = (bf16[4,1024,768]{2,1,0:T(8,128)(2,1)}, bf16[4,1024,768]{2,1,0:T(8,128)(2,1)}, u32[]{:S(2)}, u32[]{:S(2)}) collective-permute-start(bf16[4,1024,768]{2,1,0:T(8,128)(2,1)} %bitcast.391), channel_id=1, source_target_pairs={{0,16},{16,0},{1,17},{17,1},{2,18},{18,2},{3,19},{19,3},{4,20},{20... | collective-permute-start | bytes 18874376 | tf_op jit(solution)/shard_map/ppermute | solution.py:14
  10.6 59.9 %collective-permute-start.4 = (bf16[4,1024,768]{2,1,0:T(8,128)(2,1)}, bf16[4,1024,768]{2,1,0:T(8,128)(2,1)}, u32[]{:S(2)}, u32[]{:S(2)}) collective-permute-start(bf16[4,1024,768]{2,1,0:T(8,128)(2,1)} %bitcast.386), channel_id=1, source_target_pairs={{0,16},{16,0},{1,17},{17,1},{2,18},{18,2},{3,19},{19,3},{4,20},{20... | collective-permute-start | bytes 18874376 | tf_op jit(solution)/shard_map/ppermute | solution.py:14
  24.0 19.0 %all-to-all-start.1 = ((bf16[8,56,1024]{2,1,0:T(8,128)(2,1)}), bf16[8,56,1024]{2,1,0:T(8,128)(2,1)S(1)}, u32[]{:S(2)}, u32[]{:S(2)}) async-start(bf16[8,56,1024]{2,1,0:T(8,128)(2,1)} %bitcast.16), calls=%async_computation.1 | async-start | bytes 1835008 | tf_op jit(solution)/shard_map/all_to_all | solution.py:85
  43.0 16.5 %all-to-all-start = ((bf16[8,56,1024]{2,1,0:T(8,128)(2,1)}), bf16[8,56,1024]{2,1,0:T(8,128)(2,1)S(1)}, u32[]{:S(2)}, u32[]{:S(2)}) async-start(bf16[8,56,1024]{2,1,0:T(8,128)(2,1)} %bitcast.11), calls=%async_computation | async-start | bytes 1835008 | tf_op jit(solution)/shard_map/all_to_all | solution.py:81
  46.6 82.9 %collective-permute-start.3 = (bf16[4,768,1024]{2,1,0:T(8,128)(2,1)}, bf16[4,768,1024]{2,1,0:T(8,128)(2,1)}, u32[]{:S(2)}, u32[]{:S(2)}) collective-permute-start(bf16[4,768,1024]{2,1,0:T(8,128)(2,1)} %bitcast.392), channel_id=1, source_target_pairs={{0,16},{16,0},{1,17},{17,1},{2,18},{18,2},{3,19},{19,3},{4,20},{20... | collective-permute-start | bytes 18874376 | tf_op jit(solution)/shard_map/ppermute | solution.py:14
  73.4 32.3 %collective-permute-start.9 = (bf16[2,8,4,14,768]{4,1,3,2,0:T(8,128)(2,1)S(1)}, bf16[2,8,4,14,768]{4,1,3,2,0:T(8,128)(2,1)S(1)}, u32[]{:S(2)}, u32[]{:S(2)}) collective-permute-start(bf16[2,8,4,14,768]{4,1,3,2,0:T(8,128)(2,1)S(1)} %copy.204), channel_id=1, source_target_pairs={{0,8},{8,0},{1,9},{9,1},{2,10},{10,2},{3,11},{11,3},{4,12},{12,4},... | collective-permute-start | bytes 4128776 | tf_op jit(solution)/shard_map/ppermute | solution.py:114
  77.4 28.4 %copy-start.14 = (f32[4,768,8,14]{1,3,2,0:T(8,128)S(1)}, f32[4,768,8,14]{1,3,2,0:T(8,128)}, u32[]{:S(2)}) copy-start(f32[4,768,8,14]{1,3,2,0:T(8,128)} %fusion.18) | copy-start | bytes 4128772
  111.3 16.9 %collective-permute-start.10 = (bf16[8,4,14,768]{3,0,2,1:T(8,128)(2,1)S(1)}, bf16[8,4,14,768]{3,0,2,1:T(8,128)(2,1)S(1)}, u32[]{:S(2)}, u32[]{:S(2)}) collective-permute-start(bf16[8,4,14,768]{3,0,2,1:T(8,128)(2,1)S(1)} %copy.207), channel_id=1, source_target_pairs={{0,8},{8,0},{1,9},{9,1},{2,10},{10,2},{3,11},{11,3},{4,12},{12,4},... | collective-permute-start | bytes 2064392 | tf_op jit(solution)/shard_map/ppermute | solution.py:124
  148.7 46.9 %all-to-all-start.2 = ((bf16[16,56,1024]{2,1,0:T(8,128)(2,1)}), bf16[16,56,1024]{2,1,0:T(8,128)(2,1)S(1)}, u32[]{:S(2)}, u32[]{:S(2)}) async-start(bf16[16,56,1024]{2,1,0:T(8,128)(2,1)} %reshape.297), calls=%async_computation.2 | async-start | bytes 3670016 | tf_op jit(solution)/shard_map/all_to_all | solution.py:135
  153.7 4.0 %collective-permute-start.2 = (bf16[2048,32]{0,1:T(8,128)(2,1)S(1)}, bf16[2048,32]{0,1:T(8,128)(2,1)S(1)}, u32[]{:S(2)}, u32[]{:S(2)}) collective-permute-start(bf16[2048,32]{0,1:T(8,128)(2,1)S(1)} %bitcast.393), channel_id=1, source_target_pairs={{0,16},{16,0},{1,17},{17,1},{2,18},{18,2},{3,19},{19,3},{4,20},{20... | collective-permute-start | bytes 393224 | tf_op jit(solution)/shard_map/ppermute | solution.py:14
  157.6 38.2 %copy-start.11 = (bf16[2048,32]{0,1:T(8,128)(2,1)}, bf16[2048,32]{0,1:T(8,128)(2,1)S(1)}, u32[]{:S(2)}) copy-start(bf16[2048,32]{0,1:T(8,128)(2,1)S(1)} %collective-permute-done.2) | copy-start | bytes 393220
  197.5 14.8 %collective-permute-start.11 = (bf16[64,2048]{1,0:T(8,128)(2,1)S(1)}, bf16[64,2048]{1,0:T(8,128)(2,1)S(1)}, u32[]{:S(2)}, u32[]{:S(2)}) collective-permute-start(bf16[64,2048]{1,0:T(8,128)(2,1)S(1)} %get-tuple-element.35), channel_id=1, source_target_pairs={{0,4},{4,0},{1,5},{5,1},{2,6},{6,2},{3,7},{7,3},{8,12},{12,8},{9,1... | collective-permute-start | bytes 786440 | tf_op jit(solution)/shard_map/ppermute | solution.py:47
  214.1 20.2 %all-to-all-start.3 = ((bf16[8,56,1024]{2,1,0:T(8,128)(2,1)}), bf16[8,56,1024]{2,1,0:T(8,128)(2,1)S(1)}, u32[]{:S(2)}, u32[]{:S(2)}) async-start(bf16[8,56,1024]{2,1,0:T(8,128)(2,1)} %bitcast.46), calls=%async_computation.3 | async-start | bytes 1835008 | tf_op jit(solution)/shard_map/all_to_all | solution.py:81
  268.6 25.8 %collective-permute-start.12 = (bf16[2,8,4,14,768]{4,1,3,2,0:T(8,128)(2,1)S(1)}, bf16[2,8,4,14,768]{4,1,3,2,0:T(8,128)(2,1)S(1)}, u32[]{:S(2)}, u32[]{:S(2)}) collective-permute-start(bf16[2,8,4,14,768]{4,1,3,2,0:T(8,128)(2,1)S(1)} %copy.226), channel_id=1, source_target_pairs={{0,8},{8,0},{1,9},{9,1},{2,10},{10,2},{3,11},{11,3},{4,12},{12,4},... | collective-permute-start | bytes 4128776 | tf_op jit(solution)/shard_map/ppermute | solution.py:114
  275.4 19.2 %copy-start.13 = (f32[4,768,8,14]{1,3,2,0:T(8,128)S(1)}, f32[4,768,8,14]{1,3,2,0:T(8,128)}, u32[]{:S(2)}) copy-start(f32[4,768,8,14]{1,3,2,0:T(8,128)} %fusion.10) | copy-start | bytes 4128772
  302.0 11.0 %collective-permute-start.13 = (bf16[8,4,14,768]{3,0,2,1:T(8,128)(2,1)S(1)}, bf16[8,4,14,768]{3,0,2,1:T(8,128)(2,1)S(1)}, u32[]{:S(2)}, u32[]{:S(2)}) collective-permute-start(bf16[8,4,14,768]{3,0,2,1:T(8,128)(2,1)S(1)} %copy.229), channel_id=1, source_target_pairs={{0,8},{8,0},{1,9},{9,1},{2,10},{10,2},{3,11},{11,3},{4,12},{12,4},... | collective-permute-start | bytes 2064392 | tf_op jit(solution)/shard_map/ppermute | solution.py:124
  322.7 35.0 %all-to-all-start.5 = ((bf16[16,56,1024]{2,1,0:T(8,128)(2,1)}), bf16[16,56,1024]{2,1,0:T(8,128)(2,1)S(1)}, u32[]{:S(2)}, u32[]{:S(2)}) async-start(bf16[16,56,1024]{2,1,0:T(8,128)(2,1)} %reshape.298), calls=%async_computation.5 | async-start | bytes 3670016 | tf_op jit(solution)/shard_map/all_to_all | solution.py:135
  362.4 10.2 %all-to-all-start.6 = ((f32[32,1,2]{2,1,0:T(1,128)}), f32[32,1,2]{2,1,0:T(1,128)S(1)}, u32[]{:S(2)}, u32[]{:S(2)}) async-start(f32[32,1,2]{2,1,0:T(1,128)} %broadcast_in_dim.32), calls=%async_computation.6 | async-start | bytes 32768 | tf_op jit(solution)/shard_map/all_to_all | solution.py:192
  365.5 7.7 %collective-permute-start.14 = (bf16[64,1024]{1,0:T(8,128)(2,1)S(1)}, bf16[64,1024]{1,0:T(8,128)(2,1)S(1)}, u32[]{:S(2)}, u32[]{:S(2)}) collective-permute-start(bf16[64,1024]{1,0:T(8,128)(2,1)S(1)} %get-tuple-element.24), channel_id=1, source_target_pairs={{0,16},{16,0},{1,17},{17,1},{2,18},{18,2},{3,19},{19,3},{4,20},{20... | collective-permute-start | bytes 393224 | tf_op jit(solution)/shard_map/ppermute | solution.py:14
  (16 other events, 112.6 us)

commit v5 on v3

--- a/solution.py
+++ b/solution.py
@@ -58,7 +58,7 @@
 
 
 def expert_layer(entering, route_rows, partner_routes, gain_row, router_weight, weights, capacity):
-    gate_up_w, down_w = weights
+    down_w = weights[-1]
     rows, width = entering.shape
     experts_count = router_weight.shape[1]
     local_experts, hidden_units, chunk = down_w.shape
@@ -96,7 +96,11 @@
     arrived_blocks = arrived.reshape(fsdp_count, sources // fsdp_count, local_experts, capacity, chunk)
 
     def gate_and_up(rows_in):
-        return jnp.einsum("sjcd,jdh->sjch", rows_in, gate_up_w, preferred_element_type=jnp.float32)
+        parts = [
+            jnp.einsum("sjcd,jdh->sjch", rows_in, w, preferred_element_type=jnp.float32)
+            for w in weights[:-1]
+        ]
+        return parts[0] if len(parts) == 1 else jnp.concatenate(parts, axis=-1)
 
     received = []
     for shift in range(1, fsdp_count):
@@ -167,8 +171,12 @@
     for layer in range(sections):
         mine = section_index == layer
         gain_row, router_weight = [jnp.where(mine, a, b) for a, b in zip(own_small, other_small)]
-        gate_sel, up_sel, down_sel = [jnp.where(mine, a, b) for a, b in zip(own_weights, other_weights)]
-        weights = lax.optimization_barrier((jnp.concatenate([gate_sel, up_sel], axis=-1), down_sel))
+        if layer == 0:
+            weights = tuple(jnp.where(mine, a, b) for a, b in zip(own_weights, other_weights))
+        else:
+            pairs = lax.optimization_barrier((own_weights, other_weights, hidden))[:2]
+            gate_sel, up_sel, down_sel = [jnp.where(mine, a, b) for a, b in zip(*pairs)]
+            weights = (jnp.concatenate([gate_sel, up_sel], axis=-1), down_sel)
         route_all = jnp.where(mine, own_routes, section_routes)
         partner_all = jnp.where(mine, half_routes, diagonal_routes)
         route_rows = lax.dynamic_slice_in_dim(route_all, section_index * piece, piece, 0)

time: 390 us -> 370 us (0.949)
  starting transfers between devices: 49.1 us -> 34.6 us
  other arithmetic: 41.5 us -> 27.5 us
  waiting for transfers between devices: 233 us -> 246 us
    select_n x4 -> x1, other arithmetic: 18.2 us -> 0.01 us  [body(): jnp.where(mine, a, b)]
    all_to_all x2, starting transfers between devices: 26.6 us -> 9.3 us  [expert_layer(): lax.all_to_all(sending.reshape(sources, group_slots, chunk), ('fsdp', 'zh...]
    select_n x0 -> x1, other arithmetic: none -> 10.8 us  [body(): gate_sel, up_sel, down_sel = [jnp.where(mine, a, b) for a, b in zip(*pairs)]]
    ppermute x2, waiting for transfers between devices: 21.3 us -> 31.8 us  [expert_layer(): lax.ppermute(inner_act, 'fsdp', ring_pairs(fsdp_count, shift))]
    concatenate x1, other arithmetic: 8.72 us -> 0.17 us  [gate_and_up(): return parts[0] if len(parts) == 1 else jnp.concatenate(parts, axis=-1)]
    dot_general x4 -> x6, matrix products: 27.5 us -> 24.3 us  [gate_and_up(): jnp.einsum('sjcd,jdh->sjch', rows_in, w, preferred_element_type=jnp.float32)]
  transfers between devices with their start and end apart: 20 -> 20, of which waited for: 14 -> 14; matrix products, arithmetic and copies ran while one was open for 10% -> 14% of each run, Pallas kernels for 0% -> 0%
where the time goes in v5:
time: 370 us; the launch traced here: 369 us
  waiting for transfers between devices  246 us (66%)
  matrix products  39.8 us (11%)
  starting transfers between devices  34.6 us (9%)
  other arithmetic  27.5 us (7%)
  local copies, waits for them, and re-layouts  20.3 us (5%)
    all_to_all x2, waiting for transfers between devices, expert_layer(): lax.all_to_all(sending.reshape(sources, group_slots, chunk), ('fsdp', 'zh...  78.6 us
    ppermute x2, waiting for transfers between devices, expert_layer(): lax.ppermute(outgoing_part, 'fsdp', ring_pairs(fsdp_count, shift))  56 us
    all_to_all x2, waiting for transfers between devices, expert_layer(): arrived = lax.all_to_all(outgoing, ('fsdp', 'inner'), 0, 0, tiled=True)  50.2 us
    ppermute x2, waiting for transfers between devices, expert_layer(): lax.ppermute(inner_act, 'fsdp', ring_pairs(fsdp_count, shift))  31.8 us
    dot_general x6, matrix products, gate_and_up(): jnp.einsum('sjcd,jdh->sjch', rows_in, w, preferred_element_type=jnp.float32)  24.3 us
    ppermute x3, waiting for transfers between devices, other_half(): return lax.ppermute(value, 'zhalf', [(0, 1), (1, 0)])  19.5 us
    select_n x1, other arithmetic, body(): gate_sel, up_sel, down_sel = [jnp.where(mine, a, b) for a, b in zip(*pairs)]  10.8 us
    dot_general x2, matrix products, expert_layer(): jnp.einsum('fipjch,jhd->fpijcd', inner_all, down_w, preferred_element_typ...  9.71 us
  transfers between devices with their start and end apart: 20, of which 14 were waited for; matrix products, arithmetic and copies ran while one was open for 14% of the time, Pallas kernels for 0%

profile of v5, /device:TPU:0, one launch (start us, length us, event | category | flops | bytes accessed | tf_op | source)
XLA Modules:
  0.0 369.5 jit_solution(5263240650950282077)
XLA Ops:
  2.0 3.7 collective-permute-start.7
  20.0 4.5 %collective-permute-done.5 = bf16[64,2048]{1,0:T(8,128)(2,1)S(1)} collective-permute-done((bf16[64,2048]{1,0:T(8,128)(2,1)S(1)}, bf16[64,2048]{1,0:T(8,128)(2,1)S(1)}, u32[]{:S(2)}, u32[]{:S(2)}) %collective-permute-start.5) | collective-permute-done | bytes 262176 | tf_op jit(solution)/shard_map/ppermute | solution.py:47
  27.3 5.0 %all-to-all-start = ((bf16[8,112,1024]{2,1,0:T(8,128)(2,1)}), bf16[8,112,1024]{2,1,0:T(8,128)(2,1)}, u32[]{:S(2)}, u32[]{:S(2)}) async-start(bf16[8,112,1024]{2,1,0:T(8,128)(2,1)} %bitcast.19), calls=%async_computation | async-start | bytes 3670016 | tf_op jit(solution)/shard_map/all_to_all | solution.py:93
  32.5 29.8 %all-to-all-done = bf16[8,112,1024]{2,1,0:T(8,128)(2,1)} async-done(((bf16[8,112,1024]{2,1,0:T(8,128)(2,1)}), bf16[8,112,1024]{2,1,0:T(8,128)(2,1)}, u32[]{:S(2)}, u32[]{:S(2)}) %all-to-all-start) | async-done | bytes 1835040 | tf_op jit(solution)/shard_map/all_to_all | solution.py:93
  66.3 4.8 %fusion.44 = bf16[8,4,14,768]{3,2,0,1:T(8,128)(2,1)S(1)} fusion(bf16[4,1024,768]{2,1,0:T(8,128)(2,1)} %collective-permute-done.8, pred[]{:T(512)S(6)} %eq.215, bf16[1,8,4,14,1024]{4,3,2,1,0:T(8,128)(2,1)S(1)} %get-tuple-element.33, bf16[1,4,1024,768]{3,2,1,0:T(8,128)(2,1)} %param.13), kind=kOutput, calls=%fused_computation.57 | convolution fusion | flops 708132864 | bytes 14188545 | tf_op jit(solution)/shard_map/sjcd,jdh->sjch/dot_general | solution.py:100
  71.1 4.8 %fusion.47 = bf16[8,4,14,768]{3,2,0,1:T(8,128)(2,1)S(1)} fusion(bf16[4,1024,768]{2,1,0:T(8,128)(2,1)} %collective-permute-done.4, pred[]{:T(512)S(6)} %eq.215, bf16[1,8,4,14,1024]{4,3,2,1,0:T(8,128)(2,1)S(1)} %get-tuple-element.33, bf16[1,4,1024,768]{3,2,1,0:T(8,128)(2,1)} %param.12), kind=kOutput, calls=%fused_computation.58 | convolution fusion | flops 708132864 | bytes 14188545 | tf_op jit(solution)/shard_map/sjcd,jdh->sjch/dot_general | solution.py:100
  78.5 3.2 fusion.35
  84.8 24.8 %collective-permute-done.9 = bf16[8,4,14,1536]{3,0,2,1:T(8,128)(2,1)} collective-permute-done((bf16[8,4,14,1536]{3,0,2,1:T(8,128)(2,1)}, bf16[8,4,14,1536]{3,0,2,1:T(8,128)(2,1)}, u32[]{:S(2)}, u32[]{:S(2)}) %collective-permute-start.9) | collective-permute-done | bytes 1376288 | tf_op jit(solution)/shard_map/ppermute | solution.py:111
  113.4 16.6 %collective-permute-done.10 = bf16[8,4,14,768]{3,0,2,1:T(8,128)(2,1)S(1)} collective-permute-done((bf16[8,4,14,768]{3,0,2,1:T(8,128)(2,1)S(1)}, bf16[8,4,14,768]{3,0,2,1:T(8,128)(2,1)S(1)}, u32[]{:S(2)}, u32[]{:S(2)}) %collective-permute-start.10) | collective-permute-done | bytes 688160 | tf_op jit(solution)/shard_map/ppermute | solution.py:120
  131.3 5.0 %convert_bitcast_fusion.1 = bf16[2,2,4,4,14,1024]{5,4,1,2,0,3:T(8,128)(2,1)S(1)} fusion(bf16[4,768,1024]{2,1,0:T(8,128)(2,1)} %collective-permute-done.3, pred[]{:T(512)S(6)} %eq.215, bf16[2,4,2,4,14,768]{5,4,2,1,3,0:T(8,128)(2,1)S(1)} %bitcast.302, bf16[1,4,768,1024]{3,2,1,0:T(8,128)(2,1)} %param.14), kind=kOutput, calls=%fused_computation.35 | convolution fusion | flops 1413349376 | bytes 15794177 | tf_op jit(solution)/shard_map/fipjch,jhd->fpijcd/dot_general | solution.py:128
  138.0 5.4 %all-to-all-start.1 = ((bf16[16,56,1024]{2,1,0:T(8,128)(2,1)}), bf16[16,56,1024]{2,1,0:T(8,128)(2,1)S(1)}, u32[]{:S(2)}, u32[]{:S(2)}) async-start(bf16[16,56,1024]{2,1,0:T(8,128)(2,1)} %reshape.268), calls=%async_computation.1 | async-start | bytes 3670016 | tf_op jit(solution)/shard_map/all_to_all | solution.py:131
  147.2 38.0 %all-to-all-done.1 = bf16[16,56,1024]{2,1,0:T(8,128)(2,1)S(1)} async-done(((bf16[16,56,1024]{2,1,0:T(8,128)(2,1)}), bf16[16,56,1024]{2,1,0:T(8,128)(2,1)S(1)}, u32[]{:S(2)}, u32[]{:S(2)}) %all-to-all-start.1) | async-done | bytes 1835040 | tf_op jit(solution)/shard_map/all_to_all | solution.py:131
  189.1 12.9 %collective-permute-done.11 = bf16[64,2048]{1,0:T(8,128)(2,1)S(1)} collective-permute-done((bf16[64,2048]{1,0:T(8,128)(2,1)S(1)}, bf16[64,2048]{1,0:T(8,128)(2,1)S(1)}, u32[]{:S(2)}, u32[]{:S(2)}) %collective-permute-start.11) | collective-permute-done | bytes 262176 | tf_op jit(solution)/shard_map/ppermute | solution.py:47
  204.7 4.3 %all-to-all-start.2 = ((bf16[8,112,1024]{2,1,0:T(8,128)(2,1)}), bf16[8,112,1024]{2,1,0:T(8,128)(2,1)}, u32[]{:S(2)}, u32[]{:S(2)}) async-start(bf16[8,112,1024]{2,1,0:T(8,128)(2,1)} %bitcast.51), calls=%async_computation.2 | async-start | bytes 3670016 | tf_op jit(solution)/shard_map/all_to_all | solution.py:93
  209.0 10.8 %broadcast_select_fusion = (bf16[4,1024,768]{2,1,0:T(8,128)(2,1)}, bf16[4,1024,768]{2,1,0:T(8,128)(2,1)}) fusion(bf16[4,1024,768]{2,1,0:T(8,128)(2,1)} %bitcast.285, bf16[4,1024,768]{2,1,0:T(8,128)(2,1)} %collective-permute-done.8, pred[]{:T(512)S(6)} %eq.244, bf16[4,1024,768]{2,1,0:T(8,128)(2,1)} %bitcast.289, bf16[4,1024,768]{2,1,0:T(8,128)(2,1)} %collective-permute-done.4), kind=kLoop, calls=%fused_computation.19 | loop fusion | flops 6291456 | bytes 37748736 | tf_op jit(solution)/shard_map/jit(_where)/select_n | solution.py:178
  219.7 20.4 %all-to-all-done.2 = bf16[8,112,1024]{2,1,0:T(8,128)(2,1)} async-done(((bf16[8,112,1024]{2,1,0:T(8,128)(2,1)}), bf16[8,112,1024]{2,1,0:T(8,128)(2,1)}, u32[]{:S(2)}, u32[]{:S(2)}) %all-to-all-start.2) | async-done | bytes 1835040 | tf_op jit(solution)/shard_map/all_to_all | solution.py:93
  243.0 6.1 %fusion.21 = bf16[8,4,14,1536]{3,2,0,1:T(8,128)(2,1)S(1)} fusion(bf16[4,1024,768]{2,1,0:T(8,128)(2,1)} %get-tuple-element.50, bf16[4,1024,768]{2,1,0:T(8,128)(2,1)} %get-tuple-element.51, bf16[1,8,4,14,1024]{4,3,2,1,0:T(8,128)(2,1)S(1)} %get-tuple-element.32), kind=kOutput, calls=%fused_computation.29 | convolution fusion | flops 1435140096 | bytes 14876672 | tf_op jit(solution)/shard_map/sjcd,jdh->sjch/dot_general | solution.py:100
  250.4 31.3 %collective-permute-done.12 = bf16[8,4,14,1536]{3,0,2,1:T(8,128)(2,1)S(1)} collective-permute-done((bf16[8,4,14,1536]{3,0,2,1:T(8,128)(2,1)S(1)}, bf16[8,4,14,1536]{3,0,2,1:T(8,128)(2,1)S(1)}, u32[]{:S(2)}, u32[]{:S(2)}) %collective-permute-start.12) | collective-permute-done | bytes 1376288 | tf_op jit(solution)/shard_map/ppermute | solution.py:111
  286.0 15.2 %collective-permute-done.13 = bf16[8,4,14,768]{3,0,2,1:T(8,128)(2,1)S(1)} collective-permute-done((bf16[8,4,14,768]{3,0,2,1:T(8,128)(2,1)S(1)}, bf16[8,4,14,768]{3,0,2,1:T(8,128)(2,1)S(1)}, u32[]{:S(2)}, u32[]{:S(2)}) %collective-permute-start.13) | collective-permute-done | bytes 688160 | tf_op jit(solution)/shard_map/ppermute | solution.py:120
  302.4 4.7 %convert_bitcast_fusion = bf16[2,2,4,4,14,1024]{5,4,1,2,0,3:T(8,128)(2,1)S(1)} fusion(bf16[4,768,1024]{2,1,0:T(8,128)(2,1)} %bitcast.319, bf16[4,768,1024]{2,1,0:T(8,128)(2,1)} %collective-permute-done.3, pred[]{:T(512)S(6)} %eq.244, bf16[2,4,2,4,14,768]{5,4,2,1,3,0:T(8,128)(2,1)S(1)} %bitcast.303), kind=kOutput, calls=%fused_computation.34 | convolution fusion | flops 1413349376 | bytes 15794177 | tf_op jit(solution)/shard_map/fipjch,jhd->fpijcd/dot_general | solution.py:128
  308.9 3.9 %all-to-all-start.3 = ((bf16[16,56,1024]{2,1,0:T(8,128)(2,1)}), bf16[16,56,1024]{2,1,0:T(8,128)(2,1)S(1)}, u32[]{:S(2)}, u32[]{:S(2)}) async-start(bf16[16,56,1024]{2,1,0:T(8,128)(2,1)} %reshape.269), calls=%async_computation.3 | async-start | bytes 3670016 | tf_op jit(solution)/shard_map/all_to_all | solution.py:131
  313.5 40.6 %all-to-all-done.3 = bf16[16,56,1024]{2,1,0:T(8,128)(2,1)S(1)} async-done(((bf16[16,56,1024]{2,1,0:T(8,128)(2,1)}), bf16[16,56,1024]{2,1,0:T(8,128)(2,1)S(1)}, u32[]{:S(2)}, u32[]{:S(2)}) %all-to-all-start.3) | async-done | bytes 1835040 | tf_op jit(solution)/shard_map/all_to_all | solution.py:131
  357.9 3.1 all-to-all-start.4
  361.3 6.7 %all-to-all-done.4 = f32[32,1,2]{2,1,0:T(1,128)S(1)} async-done(((f32[32,1,2]{2,1,0:T(1,128)}), f32[32,1,2]{2,1,0:T(1,128)S(1)}, u32[]{:S(2)}, u32[]{:S(2)}) %all-to-all-start.4) | async-done | bytes 288 | tf_op jit(solution)/shard_map/all_to_all | solution.py:193
  (180 shorter events, 62.6 us)
Async XLA Ops:
  1.4 11.4 %collective-permute-start = (s32[128,6]{1,0:T(8,128)S(1)}, s32[128,6]{1,0:T(8,128)S(1)}, u32[]{:S(2)}, u32[]{:S(2)}) collective-permute-start(s32[128,6]{1,0:T(8,128)S(1)} %bitcast.308), channel_id=1, source_target_pairs={{0,16},{16,0},{1,17},{17,1},{2,18},{18,2},{3,19},{19,3},{4,20},{20... | collective-permute-start | bytes 9224 | tf_op jit(solution)/shard_map/ppermute | solution.py:14
  2.0 7.5 %collective-permute-start.7 = (s32[128,6]{1,0:T(8,128)S(1)}, s32[128,6]{1,0:T(8,128)S(1)}, u32[]{:S(2)}, u32[]{:S(2)}) collective-permute-start(s32[128,6]{1,0:T(8,128)S(1)} %bitcast.309), channel_id=1, source_target_pairs={{0,20},{20,0},{4,16},{16,4},{1,21},{21,1},{5,17},{17,5},{2,22},{22... | collective-permute-start | bytes 9224 | tf_op jit(solution)/shard_map/ppermute | solution.py:166
  5.7 6.9 %collective-permute-start.6 = (s32[128,6]{1,0:T(8,128)S(1)}, s32[128,6]{1,0:T(8,128)S(1)}, u32[]{:S(2)}, u32[]{:S(2)}) collective-permute-start(s32[128,6]{1,0:T(8,128)S(1)} %bitcast.310), channel_id=1, source_target_pairs={{0,4},{4,0},{1,5},{5,1},{2,6},{6,2},{3,7},{7,3},{8,12},{12,8},{9,1... | collective-permute-start | bytes 9224 | tf_op jit(solution)/shard_map/ppermute | solution.py:47
  5.7 14.3 %collective-permute-start.1 = (f32[2048]{0:T(1024)}, f32[2048]{0:T(1024)S(1)}, u32[]{:S(2)}, u32[]{:S(2)}) collective-permute-start(f32[2048]{0:T(1024)} %bitcast.316), channel_id=1, source_target_pairs={{0,16},{16,0},{1,17},{17,1},{2,18},{18,2},{3,19},{19,3},{4,20},{20... | collective-permute-start | bytes 24584 | tf_op jit(solution)/shard_map/ppermute | solution.py:14
  5.8 60.5 %collective-permute-start.8 = (bf16[4,1024,768]{2,1,0:T(8,128)(2,1)}, bf16[4,1024,768]{2,1,0:T(8,128)(2,1)}, u32[]{:S(2)}, u32[]{:S(2)}) collective-permute-start(bf16[4,1024,768]{2,1,0:T(8,128)(2,1)} %bitcast.284), channel_id=1, source_target_pairs={{0,16},{16,0},{1,17},{17,1},{2,18},{18,2},{3,19},{19,3},{4,20},{20... | collective-permute-start | bytes 18874376 | tf_op jit(solution)/shard_map/ppermute | solution.py:14
  9.5 15.1 %collective-permute-start.5 = (bf16[64,2048]{1,0:T(8,128)(2,1)S(1)}, bf16[64,2048]{1,0:T(8,128)(2,1)S(1)}, u32[]{:S(2)}, u32[]{:S(2)}) collective-permute-start(bf16[64,2048]{1,0:T(8,128)(2,1)S(1)} %get-tuple-element.30), channel_id=1, source_target_pairs={{0,4},{4,0},{1,5},{5,1},{2,6},{6,2},{3,7},{7,3},{8,12},{12,8},{9,1... | collective-permute-start | bytes 786440 | tf_op jit(solution)/shard_map/ppermute | solution.py:47
  12.5 58.6 %collective-permute-start.4 = (bf16[4,1024,768]{2,1,0:T(8,128)(2,1)}, bf16[4,1024,768]{2,1,0:T(8,128)(2,1)}, u32[]{:S(2)}, u32[]{:S(2)}) collective-permute-start(bf16[4,1024,768]{2,1,0:T(8,128)(2,1)} %bitcast.288), channel_id=1, source_target_pairs={{0,16},{16,0},{1,17},{17,1},{2,18},{18,2},{3,19},{19,3},{4,20},{20... | collective-permute-start | bytes 18874376 | tf_op jit(solution)/shard_map/ppermute | solution.py:14
  27.3 35.1 %all-to-all-start = ((bf16[8,112,1024]{2,1,0:T(8,128)(2,1)}), bf16[8,112,1024]{2,1,0:T(8,128)(2,1)}, u32[]{:S(2)}, u32[]{:S(2)}) async-start(bf16[8,112,1024]{2,1,0:T(8,128)(2,1)} %bitcast.19), calls=%async_computation | async-start | bytes 3670016 | tf_op jit(solution)/shard_map/all_to_all | solution.py:93
  32.3 99.0 %collective-permute-start.3 = (bf16[4,768,1024]{2,1,0:T(8,128)(2,1)}, bf16[4,768,1024]{2,1,0:T(8,128)(2,1)}, u32[]{:S(2)}, u32[]{:S(2)}) collective-permute-start(bf16[4,768,1024]{2,1,0:T(8,128)(2,1)} %bitcast.318), channel_id=1, source_target_pairs={{0,16},{16,0},{1,17},{17,1},{2,18},{18,2},{3,19},{19,3},{4,20},{20... | collective-permute-start | bytes 18874376 | tf_op jit(solution)/shard_map/ppermute | solution.py:14
  77.9 31.6 %collective-permute-start.9 = (bf16[8,4,14,1536]{3,0,2,1:T(8,128)(2,1)}, bf16[8,4,14,1536]{3,0,2,1:T(8,128)(2,1)}, u32[]{:S(2)}, u32[]{:S(2)}) collective-permute-start(bf16[8,4,14,1536]{3,0,2,1:T(8,128)(2,1)} %copy.164), channel_id=1, source_target_pairs={{0,8},{8,0},{1,9},{9,1},{2,10},{10,2},{3,11},{11,3},{4,12},{12,4},... | collective-permute-start | bytes 4128776 | tf_op jit(solution)/shard_map/ppermute | solution.py:111
  112.3 17.8 %collective-permute-start.10 = (bf16[8,4,14,768]{3,0,2,1:T(8,128)(2,1)S(1)}, bf16[8,4,14,768]{3,0,2,1:T(8,128)(2,1)S(1)}, u32[]{:S(2)}, u32[]{:S(2)}) collective-permute-start(bf16[8,4,14,768]{3,0,2,1:T(8,128)(2,1)S(1)} %copy.166), channel_id=1, source_target_pairs={{0,8},{8,0},{1,9},{9,1},{2,10},{10,2},{3,11},{11,3},{4,12},{12,4},... | collective-permute-start | bytes 2064392 | tf_op jit(solution)/shard_map/ppermute | solution.py:120
  138.0 47.3 %all-to-all-start.1 = ((bf16[16,56,1024]{2,1,0:T(8,128)(2,1)}), bf16[16,56,1024]{2,1,0:T(8,128)(2,1)S(1)}, u32[]{:S(2)}, u32[]{:S(2)}) async-start(bf16[16,56,1024]{2,1,0:T(8,128)(2,1)} %reshape.268), calls=%async_computation.1 | async-start | bytes 3670016 | tf_op jit(solution)/shard_map/all_to_all | solution.py:131
  143.4 3.2 collective-permute-start.2
  146.7 38.7 %copy-start.9 = (bf16[2048,32]{0,1:T(8,128)(2,1)}, bf16[2048,32]{0,1:T(8,128)(2,1)S(1)}, u32[]{:S(2)}) copy-start(bf16[2048,32]{0,1:T(8,128)(2,1)S(1)} %collective-permute-done.2) | copy-start | bytes 393220
  187.1 14.8 %collective-permute-start.11 = (bf16[64,2048]{1,0:T(8,128)(2,1)S(1)}, bf16[64,2048]{1,0:T(8,128)(2,1)S(1)}, u32[]{:S(2)}, u32[]{:S(2)}) collective-permute-start(bf16[64,2048]{1,0:T(8,128)(2,1)S(1)} %get-tuple-element.47), channel_id=1, source_target_pairs={{0,4},{4,0},{1,5},{5,1},{2,6},{6,2},{3,7},{7,3},{8,12},{12,8},{9,1... | collective-permute-start | bytes 786440 | tf_op jit(solution)/shard_map/ppermute | solution.py:47
  204.7 35.5 %all-to-all-start.2 = ((bf16[8,112,1024]{2,1,0:T(8,128)(2,1)}), bf16[8,112,1024]{2,1,0:T(8,128)(2,1)}, u32[]{:S(2)}, u32[]{:S(2)}) async-start(bf16[8,112,1024]{2,1,0:T(8,128)(2,1)} %bitcast.51), calls=%async_computation.2 | async-start | bytes 3670016 | tf_op jit(solution)/shard_map/all_to_all | solution.py:93
  242.7 39.0 %slice-start.4 = ((s8[6291456]{0:T(1024)(128)(4,1)}), s8[4194304]{0:T(1024)(128)(4,1)S(1)}, s32[]{:S(2)}) async-start(s8[6291456]{0:T(1024)(128)(4,1)} %bitcast.292), calls=%async_computation.9 | async-start | bytes 8388608
  242.7 39.0 %slice-start.6 = ((s8[6291456]{0:T(1024)(128)(4,1)}), s8[4194304]{0:T(1024)(128)(4,1)S(1)}, s32[]{:S(2)}) async-start(s8[6291456]{0:T(1024)(128)(4,1)} %bitcast.294), calls=%async_computation.11 | async-start | bytes 8388608
  243.0 38.7 %slice-start.5 = ((s8[6291456]{0:T(1024)(128)(4,1)}), s8[2097152]{0:T(1024)(128)(4,1)S(1)}, s32[]{:S(2)}) async-start(s8[6291456]{0:T(1024)(128)(4,1)} %bitcast.292), calls=%async_computation.10 | async-start | bytes 4194304
  249.8 31.9 %collective-permute-start.12 = (bf16[8,4,14,1536]{3,0,2,1:T(8,128)(2,1)S(1)}, bf16[8,4,14,1536]{3,0,2,1:T(8,128)(2,1)S(1)}, u32[]{:S(2)}, u32[]{:S(2)}) collective-permute-start(bf16[8,4,14,1536]{3,0,2,1:T(8,128)(2,1)S(1)} %copy.184), channel_id=1, source_target_pairs={{0,8},{8,0},{1,9},{9,1},{2,10},{10,2},{3,11},{11,3},{4,12},{12,4},... | collective-permute-start | bytes 4128776 | tf_op jit(solution)/shard_map/ppermute | solution.py:111
  284.9 16.3 %collective-permute-start.13 = (bf16[8,4,14,768]{3,0,2,1:T(8,128)(2,1)S(1)}, bf16[8,4,14,768]{3,0,2,1:T(8,128)(2,1)S(1)}, u32[]{:S(2)}, u32[]{:S(2)}) collective-permute-start(bf16[8,4,14,768]{3,0,2,1:T(8,128)(2,1)S(1)} %copy.186), channel_id=1, source_target_pairs={{0,8},{8,0},{1,9},{9,1},{2,10},{10,2},{3,11},{11,3},{4,12},{12,4},... | collective-permute-start | bytes 2064392 | tf_op jit(solution)/shard_map/ppermute | solution.py:120
  308.9 45.2 %all-to-all-start.3 = ((bf16[16,56,1024]{2,1,0:T(8,128)(2,1)}), bf16[16,56,1024]{2,1,0:T(8,128)(2,1)S(1)}, u32[]{:S(2)}, u32[]{:S(2)}) async-start(bf16[16,56,1024]{2,1,0:T(8,128)(2,1)} %reshape.269), calls=%async_computation.3 | async-start | bytes 3670016 | tf_op jit(solution)/shard_map/all_to_all | solution.py:131
  357.9 10.2 %all-to-all-start.4 = ((f32[32,1,2]{2,1,0:T(1,128)}), f32[32,1,2]{2,1,0:T(1,128)S(1)}, u32[]{:S(2)}, u32[]{:S(2)}) async-start(f32[32,1,2]{2,1,0:T(1,128)} %broadcast_in_dim.32), calls=%async_computation.4 | async-start | bytes 32768 | tf_op jit(solution)/shard_map/all_to_all | solution.py:193
  361.0 7.7 %collective-permute-start.14 = (bf16[64,1024]{1,0:T(8,128)(2,1)S(1)}, bf16[64,1024]{1,0:T(8,128)(2,1)S(1)}, u32[]{:S(2)}, u32[]{:S(2)}) collective-permute-start(bf16[64,1024]{1,0:T(8,128)(2,1)S(1)} %get-tuple-element.40), channel_id=1, source_target_pairs={{0,16},{16,0},{1,17},{17,1},{2,18},{18,2},{3,19},{19,3},{4,20},{20... | collective-permute-start | bytes 393224 | tf_op jit(solution)/shard_map/ppermute | solution.py:14
  (15 other events, 145.4 us)

commit v6 on v2

--- a/solution.py
+++ b/solution.py
@@ -38,7 +38,11 @@
     onehot = (flat_routes[:, None] == jnp.arange(experts_count, dtype=jnp.int32)[None, :]).astype(
         jnp.int32
     )
-    before = jnp.cumsum(onehot, axis=0) - onehot
+    count = flat_routes.shape[0]
+    earlier = (jnp.arange(count)[:, None] > jnp.arange(count)[None, :]).astype(jnp.bfloat16)
+    before = jnp.dot(
+        earlier, onehot.astype(jnp.bfloat16), preferred_element_type=jnp.float32
+    ).astype(jnp.int32)
     slot_index = jnp.sum(before * onehot, axis=1)
     return (flat_routes * capacity + slot_index).reshape(route_rows.shape)
 
@@ -160,7 +164,9 @@
     own_weights = (w_gate[0], w_up[0], w_down[0])
     other_weights = tuple(other_section(w) for w in own_weights)
     own_small = (norm_gain[0], router[0])
-    other_small = tuple(other_section(v) for v in own_small)
+    packed = jnp.concatenate([own_small[0][:, None], own_small[1].astype(jnp.float32)], axis=1)
+    other_packed = other_section(packed)
+    other_small = (other_packed[:, 0], other_packed[:, 1:].astype(router.dtype))
     own_routes = routes[0]
     section_routes = other_section(own_routes)
     half_routes = other_half(own_routes)

time: 354 us -> 352 us (level)
  waiting for transfers between devices: 198 us -> 203 us
  starting transfers between devices: 33.1 us -> 28.7 us
    all_to_all x2, waiting for transfers between devices: 69.5 us -> 74.4 us  [expert_layer(): lax.all_to_all(sending.reshape(sources, group_slots, chunk), ('fsdp', 'zh...]
    ppermute x7 -> x6, starting transfers between devices: 5.52 us -> 1.28 us  [other_section(): return lax.ppermute(value, 'section', [(0, 1), (1, 0)])]
    another operation x8 -> x0, other arithmetic: 3.68 us -> none
  transfers between devices with their start and end apart: 19 -> 18, of which waited for: 11 -> 11; matrix products, arithmetic and copies ran while one was open for 12% -> 12% of each run, Pallas kernels for 0% -> 0%
where the time goes in v6:
time: 352 us; the launch traced here: 351 us
  waiting for transfers between devices  203 us (58%)
  matrix products  63 us (18%)
  blocking collectives  29.2 us (8%)
  starting transfers between devices  28.7 us (8%)
  local copies, waits for them, and re-layouts  16.4 us (5%)
  other arithmetic  9.44 us (3%)
    all_to_all x2, waiting for transfers between devices, expert_layer(): lax.all_to_all(sending.reshape(sources, group_slots, chunk), ('fsdp', 'zh...  74.4 us
    ppermute x2, waiting for transfers between devices, expert_layer(): lax.ppermute(outgoing_pair, 'fsdp', ring_pairs(fsdp_count, shift))  46.4 us
    all_to_all x1, waiting for transfers between devices, expert_layer(): arrived = lax.all_to_all(outgoing, ('fsdp', 'inner'), 0, 0, tiled=True)  29.3 us
    all_to_all x1, blocking collectives, expert_layer(): arrived = lax.all_to_all(outgoing, ('fsdp', 'inner'), 0, 0, tiled=True)  29.2 us
    ppermute x2, waiting for transfers between devices, expert_layer(): lax.ppermute(inner_act, 'fsdp', ring_pairs(fsdp_count, shift))  25.8 us
    dot_general x4, matrix products, gate_and_up(): jnp.einsum('sjcd,jdh->sjch', rows_in, up_w, preferred_element_type=jnp.fl...  23 us
    dot_general x4, matrix products, gate_and_up(): jnp.einsum('sjcd,jdh->sjch', rows_in, gate_w, preferred_element_type=jnp....  22.1 us
    ppermute x3, waiting for transfers between devices, other_half(): return lax.ppermute(value, 'zhalf', [(0, 1), (1, 0)])  14.8 us
  transfers between devices with their start and end apart: 18, of which 11 were waited for; matrix products, arithmetic and copies ran while one was open for 12% of the time, Pallas kernels for 0%

profile of v6, /device:TPU:0, one launch (start us, length us, event | category | flops | bytes accessed | tf_op | source)
XLA Modules:
  0.0 351.2 jit_solution(1671239485013571456)
XLA Ops:
  12.1 5.8 %collective-permute-done.6 = s32[128,6]{1,0:T(8,128)S(1)} collective-permute-done((s32[128,6]{1,0:T(8,128)S(1)}, s32[128,6]{1,0:T(8,128)S(1)}, u32[]{:S(2)}, u32[]{:S(2)}) %collective-permute-start.6) | collective-permute-done | bytes 3104 | tf_op jit(solution)/shard_map/ppermute | solution.py:173
  25.8 4.5 %all-to-all-start = ((bf16[8,112,1024]{2,1,0:T(8,128)(2,1)}), bf16[8,112,1024]{2,1,0:T(8,128)(2,1)}, u32[]{:S(2)}, u32[]{:S(2)}) async-start(bf16[8,112,1024]{2,1,0:T(8,128)(2,1)} %bitcast.19), calls=%async_computation | async-start | bytes 3670016 | tf_op jit(solution)/shard_map/all_to_all | solution.py:97
  30.5 29.3 %all-to-all-done = bf16[8,112,1024]{2,1,0:T(8,128)(2,1)} async-done(((bf16[8,112,1024]{2,1,0:T(8,128)(2,1)}), bf16[8,112,1024]{2,1,0:T(8,128)(2,1)}, u32[]{:S(2)}, u32[]{:S(2)}) %all-to-all-start) | async-done | bytes 1835040 | tf_op jit(solution)/shard_map/all_to_all | solution.py:97
  62.6 4.6 %fusion.54 = bf16[1,8,4,14,768]{4,3,1,2,0:T(8,128)(2,1)S(1)} fusion(bf16[4,1024,768]{2,1,0:T(8,128)(2,1)} %collective-permute-done.7, pred[]{:T(512)S(6)} %eq.86, bf16[1,8,4,14,1024]{4,3,2,1,0:T(8,128)(2,1)S(1)} %get-tuple-element.21, bf16[1,4,1024,768]{3,2,1,0:T(8,128)(2,1)} %param.13), kind=kOutput, calls=%fused_computation.64 | convolution fusion | flops 708132864 | bytes 14188545 | tf_op jit(solution)/shard_map/sjcd,jdh->sjch/dot_general | solution.py:106
  67.3 4.6 %fusion.57 = bf16[1,8,4,14,768]{4,3,1,2,0:T(8,128)(2,1)S(1)} fusion(bf16[4,1024,768]{2,1,0:T(8,128)(2,1)} %collective-permute-done.3, pred[]{:T(512)S(6)} %eq.86, bf16[1,8,4,14,1024]{4,3,2,1,0:T(8,128)(2,1)S(1)} %get-tuple-element.21, bf16[1,4,1024,768]{3,2,1,0:T(8,128)(2,1)} %param.12), kind=kOutput, calls=%fused_computation.65 | convolution fusion | flops 708132864 | bytes 14188545 | tf_op jit(solution)/shard_map/sjcd,jdh->sjch/dot_general | solution.py:103
  73.2 4.6 %fusion.18 = f32[4,768,8,14]{1,3,2,0:T(8,128)S(1)} fusion(bf16[4,1024,768]{2,1,0:T(8,128)(2,1)} %collective-permute-done.3, pred[]{:T(512)S(6)} %eq.86, bf16[1,8,4,14,1024]{4,3,2,1,0:T(8,128)(2,1)S(1)} %get-tuple-element.22, bf16[1,4,1024,768]{3,2,1,0:T(8,128)(2,1)} %param.12), kind=kOutput, calls=%fused_computation.20 | convolution fusion | flops 707788800 | bytes 14876673 | tf_op jit(solution)/shard_map/sjcd,jdh->sjch/dot_general | solution.py:103
  77.8 26.3 %collective-permute-done.8 = bf16[2,8,4,14,768]{4,1,3,2,0:T(8,128)(2,1)S(1)} collective-permute-done((bf16[2,8,4,14,768]{4,1,3,2,0:T(8,128)(2,1)S(1)}, bf16[2,8,4,14,768]{4,1,3,2,0:T(8,128)(2,1)S(1)}, u32[]{:S(2)}, u32[]{:S(2)}) %collective-permute-start.8) | collective-permute-done | bytes 1376288 | tf_op jit(solution)/shard_map/ppermute | solution.py:115
  104.2 5.0 %fusion.33 = bf16[8,4,14,768]{3,2,0,1:T(8,128)(2,1)S(1)} fusion(f32[4,768,8,14]{1,3,2,0:T(8,128)S(1)} %fusion.18, bf16[1,8,4,14,768]{4,1,3,2,0:T(8,128)(2,1)S(1)} %get-tuple-element.26, bf16[1,8,4,14,768]{4,1,3,2,0:T(8,128)(2,1)S(1)} %get-tuple-element.25, bf16[1,8,4,14,1024]{4,3,2,1,0:T(8,128)(2,1)S(1)} %get-tuple-element.22, ...), kind=kOutput, calls=%fused_computation.48 | convolution fusion | flops 711229440 | bytes 16941056 | tf_op jit(solution)/shard_map/sjcd,jdh->sjch/dot_general | solution.py:106
  110.1 15.4 %collective-permute-done.9 = bf16[8,4,14,768]{3,0,2,1:T(8,128)(2,1)S(1)} collective-permute-done((bf16[8,4,14,768]{3,0,2,1:T(8,128)(2,1)S(1)}, bf16[8,4,14,768]{3,0,2,1:T(8,128)(2,1)S(1)}, u32[]{:S(2)}, u32[]{:S(2)}) %collective-permute-start.9) | collective-permute-done | bytes 688160 | tf_op jit(solution)/shard_map/ppermute | solution.py:125
  126.7 4.7 %convert_bitcast_fusion.1 = bf16[2,2,4,4,14,1024]{5,4,1,2,0,3:T(8,128)(2,1)S(1)} fusion(bf16[4,768,1024]{2,1,0:T(8,128)(2,1)} %collective-permute-done.2, pred[]{:T(512)S(6)} %eq.86, bf16[2,4,2,4,14,768]{5,4,2,1,3,0:T(8,128)(2,1)S(1)} %bitcast.290, bf16[1,4,768,1024]{3,2,1,0:T(8,128)(2,1)} %param.14), kind=kOutput, calls=%fused_computation.35 | convolution fusion | flops 1413349376 | bytes 15794177 | tf_op jit(solution)/shard_map/fipjch,jhd->fpijcd/dot_general | solution.py:133
  133.4 4.3 %all-to-all-start.1 = ((bf16[16,56,1024]{2,1,0:T(8,128)(2,1)}), bf16[16,56,1024]{2,1,0:T(8,128)(2,1)S(1)}, u32[]{:S(2)}, u32[]{:S(2)}) async-start(bf16[16,56,1024]{2,1,0:T(8,128)(2,1)} %reshape.213), calls=%async_computation.1 | async-start | bytes 3670016 | tf_op jit(solution)/shard_map/all_to_all | solution.py:136
  138.4 41.2 %all-to-all-done.1 = bf16[16,56,1024]{2,1,0:T(8,128)(2,1)S(1)} async-done(((bf16[16,56,1024]{2,1,0:T(8,128)(2,1)}), bf16[16,56,1024]{2,1,0:T(8,128)(2,1)S(1)}, u32[]{:S(2)}, u32[]{:S(2)}) %all-to-all-start.1) | async-done | bytes 1835040 | tf_op jit(solution)/shard_map/all_to_all | solution.py:136
  183.4 12.4 %collective-permute-done.10 = bf16[64,2048]{1,0:T(8,128)(2,1)S(1)} collective-permute-done((bf16[64,2048]{1,0:T(8,128)(2,1)S(1)}, bf16[64,2048]{1,0:T(8,128)(2,1)S(1)}, u32[]{:S(2)}, u32[]{:S(2)}) %collective-permute-start.10) | collective-permute-done | bytes 262176 | tf_op jit(solution)/shard_map/ppermute | solution.py:51
  197.3 29.2 %all_to_all.26 = bf16[8,112,1024]{2,1,0:T(8,128)(2,1)} all-to-all(bf16[8,112,1024]{2,1,0:T(8,128)(2,1)S(1)} %bitcast.279), channel_id=1, replica_groups=mesh['section'=2,'fsdp'=2,'zhalf'=2,'inner'=4] {'fsdp','inner'}, dimensions={0} | all-to-all | bytes 3670016 | tf_op jit(solution)/shard_map/all_to_all | solution.py:97
  229.2 6.5 %fusion.51 = bf16[1,8,4,14,768]{4,3,1,2,0:T(8,128)(2,1)S(1)} fusion(bf16[4,1024,768]{2,1,0:T(8,128)(2,1)} %collective-permute-done.3, pred[]{:T(512)S(6)} %eq.196, bf16[1,8,4,14,1024]{4,3,2,1,0:T(8,128)(2,1)S(1)} %get-tuple-element.19, bf16[1,4,1024,768]{3,2,1,0:T(8,128)(2,1)} %param.12), kind=kOutput, calls=%fused_computation.63 | convolution fusion | flops 708132864 | bytes 14188545 | tf_op jit(solution)/shard_map/sjcd,jdh->sjch/dot_general | solution.py:103
  235.7 6.5 %fusion.48 = bf16[1,8,4,14,768]{4,3,1,2,0:T(8,128)(2,1)S(1)} fusion(bf16[4,1024,768]{2,1,0:T(8,128)(2,1)} %collective-permute-done.7, pred[]{:T(512)S(6)} %eq.196, bf16[1,8,4,14,1024]{4,3,2,1,0:T(8,128)(2,1)S(1)} %get-tuple-element.19, bf16[1,4,1024,768]{3,2,1,0:T(8,128)(2,1)} %param.13), kind=kOutput, calls=%fused_computation.62 | convolution fusion | flops 708132864 | bytes 14188545 | tf_op jit(solution)/shard_map/sjcd,jdh->sjch/dot_general | solution.py:106
  243.4 6.4 %fusion.10 = f32[4,768,8,14]{1,3,2,0:T(8,128)S(1)} fusion(bf16[4,1024,768]{2,1,0:T(8,128)(2,1)} %collective-permute-done.3, pred[]{:T(512)S(6)} %eq.196, bf16[1,8,4,14,1024]{4,3,2,1,0:T(8,128)(2,1)S(1)} %get-tuple-element.20, bf16[1,4,1024,768]{3,2,1,0:T(8,128)(2,1)} %param.12), kind=kOutput, calls=%fused_computation.12 | convolution fusion | flops 707788800 | bytes 14876673 | tf_op jit(solution)/shard_map/sjcd,jdh->sjch/dot_general | solution.py:103
  249.8 20.1 %collective-permute-done.11 = bf16[2,8,4,14,768]{4,1,3,2,0:T(8,128)(2,1)S(1)} collective-permute-done((bf16[2,8,4,14,768]{4,1,3,2,0:T(8,128)(2,1)S(1)}, bf16[2,8,4,14,768]{4,1,3,2,0:T(8,128)(2,1)S(1)}, u32[]{:S(2)}, u32[]{:S(2)}) %collective-permute-start.11) | collective-permute-done | bytes 1376288 | tf_op jit(solution)/shard_map/ppermute | solution.py:115
  270.0 6.9 %fusion.31 = bf16[8,4,14,768]{3,2,0,1:T(8,128)(2,1)S(1)} fusion(f32[4,768,8,14]{1,3,2,0:T(8,128)S(1)} %fusion.10, bf16[1,8,4,14,768]{4,1,3,2,0:T(8,128)(2,1)S(1)} %get-tuple-element.24, bf16[1,8,4,14,768]{4,1,3,2,0:T(8,128)(2,1)S(1)} %get-tuple-element.23, bf16[1,8,4,14,1024]{4,3,2,1,0:T(8,128)(2,1)S(1)} %get-tuple-element.20, ...), kind=kOutput, calls=%fused_computation.44 | convolution fusion | flops 711229440 | bytes 16941056 | tf_op jit(solution)/shard_map/sjcd,jdh->sjch/dot_general | solution.py:106
  277.7 10.4 %collective-permute-done.12 = bf16[8,4,14,768]{3,0,2,1:T(8,128)(2,1)S(1)} collective-permute-done((bf16[8,4,14,768]{3,0,2,1:T(8,128)(2,1)S(1)}, bf16[8,4,14,768]{3,0,2,1:T(8,128)(2,1)S(1)}, u32[]{:S(2)}, u32[]{:S(2)}) %collective-permute-start.12) | collective-permute-done | bytes 688160 | tf_op jit(solution)/shard_map/ppermute | solution.py:125
  289.3 6.5 %convert_bitcast_fusion = bf16[2,2,4,4,14,1024]{5,4,1,2,0,3:T(8,128)(2,1)S(1)} fusion(bf16[4,768,1024]{2,1,0:T(8,128)(2,1)} %collective-permute-done.2, pred[]{:T(512)S(6)} %eq.196, bf16[2,4,2,4,14,768]{5,4,2,1,3,0:T(8,128)(2,1)S(1)} %bitcast.291, bf16[1,4,768,1024]{3,2,1,0:T(8,128)(2,1)} %param.14), kind=kOutput, calls=%fused_computation.34 | convolution fusion | flops 1413349376 | bytes 15794177 | tf_op jit(solution)/shard_map/fipjch,jhd->fpijcd/dot_general | solution.py:133
  297.7 4.2 %all-to-all-start.3 = ((bf16[16,56,1024]{2,1,0:T(8,128)(2,1)}), bf16[16,56,1024]{2,1,0:T(8,128)(2,1)S(1)}, u32[]{:S(2)}, u32[]{:S(2)}) async-start(bf16[16,56,1024]{2,1,0:T(8,128)(2,1)} %reshape.214), calls=%async_computation.3 | async-start | bytes 3670016 | tf_op jit(solution)/shard_map/all_to_all | solution.py:136
  302.6 33.2 %all-to-all-done.3 = bf16[16,56,1024]{2,1,0:T(8,128)(2,1)S(1)} async-done(((bf16[16,56,1024]{2,1,0:T(8,128)(2,1)}), bf16[16,56,1024]{2,1,0:T(8,128)(2,1)S(1)}, u32[]{:S(2)}, u32[]{:S(2)}) %all-to-all-start.3) | async-done | bytes 1835040 | tf_op jit(solution)/shard_map/all_to_all | solution.py:136
  343.1 6.7 %all-to-all-done.4 = f32[32,1,2]{2,1,0:T(1,128)S(1)} async-done(((f32[32,1,2]{2,1,0:T(1,128)}), f32[32,1,2]{2,1,0:T(1,128)S(1)}, u32[]{:S(2)}, u32[]{:S(2)}) %all-to-all-start.4) | async-done | bytes 288 | tf_op jit(solution)/shard_map/all_to_all | solution.py:195
  (139 shorter events, 50.6 us)
Async XLA Ops:
  1.4 10.1 %collective-permute-start.5 = (s32[128,6]{1,0:T(8,128)S(1)}, s32[128,6]{1,0:T(8,128)S(1)}, u32[]{:S(2)}, u32[]{:S(2)}) collective-permute-start(s32[128,6]{1,0:T(8,128)S(1)} %bitcast.296), channel_id=1, source_target_pairs={{0,4},{4,0},{1,5},{5,1},{2,6},{6,2},{3,7},{7,3},{8,12},{12,8},{9,1... | collective-permute-start | bytes 9224 | tf_op jit(solution)/shard_map/ppermute | solution.py:51
  5.5 12.3 %collective-permute-start.6 = (s32[128,6]{1,0:T(8,128)S(1)}, s32[128,6]{1,0:T(8,128)S(1)}, u32[]{:S(2)}, u32[]{:S(2)}) collective-permute-start(s32[128,6]{1,0:T(8,128)S(1)} %bitcast.297), channel_id=1, source_target_pairs={{0,20},{20,0},{4,16},{16,4},{1,21},{21,1},{5,17},{17,5},{2,22},{22... | collective-permute-start | bytes 9224 | tf_op jit(solution)/shard_map/ppermute | solution.py:173
  5.5 13.0 %collective-permute-start = (s32[128,6]{1,0:T(8,128)S(1)}, s32[128,6]{1,0:T(8,128)S(1)}, u32[]{:S(2)}, u32[]{:S(2)}) collective-permute-start(s32[128,6]{1,0:T(8,128)S(1)} %bitcast.298), channel_id=1, source_target_pairs={{0,16},{16,0},{1,17},{17,1},{2,18},{18,2},{3,19},{19,3},{4,20},{20... | collective-permute-start | bytes 9224 | tf_op jit(solution)/shard_map/ppermute | solution.py:14
  6.8 16.3 %copy-start.8 = (f32[1,2048]{1,0:T(1,128)S(1)}, f32[1,2048]{1,0:T(1,128)}, u32[]{:S(2)}) copy-start(f32[1,2048]{1,0:T(1,128)} %param.10) | copy-start | bytes 24580
  6.9 16.1 %collective-permute-start.4 = (bf16[64,2048]{1,0:T(8,128)(2,1)S(1)}, bf16[64,2048]{1,0:T(8,128)(2,1)S(1)}, u32[]{:S(2)}, u32[]{:S(2)}) collective-permute-start(bf16[64,2048]{1,0:T(8,128)(2,1)S(1)} %get-tuple-element.18), channel_id=1, source_target_pairs={{0,4},{4,0},{1,5},{5,1},{2,6},{6,2},{3,7},{7,3},{8,12},{12,8},{9,1... | collective-permute-start | bytes 786440 | tf_op jit(solution)/shard_map/ppermute | solution.py:51
  11.4 11.7 %collective-permute-start.1 = (f32[2048,33]{0,1:T(8,128)S(1)}, f32[2048,33]{0,1:T(8,128)S(1)}, u32[]{:S(2)}, u32[]{:S(2)}) collective-permute-start(f32[2048,33]{0,1:T(8,128)S(1)} %pad_maximum_fusion.6), channel_id=1, source_target_pairs={{0,16},{16,0},{1,17},{17,1},{2,18},{18,2},{3,19},{19,3},{4,20},{20... | collective-permute-start | bytes 811016 | tf_op jit(solution)/shard_map/ppermute | solution.py:14
  11.6 51.0 %collective-permute-start.7 = (bf16[4,1024,768]{2,1,0:T(8,128)(2,1)}, bf16[4,1024,768]{2,1,0:T(8,128)(2,1)}, u32[]{:S(2)}, u32[]{:S(2)}) collective-permute-start(bf16[4,1024,768]{2,1,0:T(8,128)(2,1)} %bitcast.306), channel_id=1, source_target_pairs={{0,16},{16,0},{1,17},{17,1},{2,18},{18,2},{3,19},{19,3},{4,20},{20... | collective-permute-start | bytes 18874376 | tf_op jit(solution)/shard_map/ppermute | solution.py:14
  17.9 49.4 %collective-permute-start.3 = (bf16[4,1024,768]{2,1,0:T(8,128)(2,1)}, bf16[4,1024,768]{2,1,0:T(8,128)(2,1)}, u32[]{:S(2)}, u32[]{:S(2)}) collective-permute-start(bf16[4,1024,768]{2,1,0:T(8,128)(2,1)} %bitcast.305), channel_id=1, source_target_pairs={{0,16},{16,0},{1,17},{17,1},{2,18},{18,2},{3,19},{19,3},{4,20},{20... | collective-permute-start | bytes 18874376 | tf_op jit(solution)/shard_map/ppermute | solution.py:14
  18.6 4.6 %copy-start.2 = (s32[64,6]{1,0:T(8,128)}, s32[64,6]{1,0:T(8,128)S(1)}, u32[]{:S(2)}) copy-start(s32[64,6]{1,0:T(8,128)S(1)} %get-tuple-element.35) | copy-start | bytes 4612
  25.8 34.0 %all-to-all-start = ((bf16[8,112,1024]{2,1,0:T(8,128)(2,1)}), bf16[8,112,1024]{2,1,0:T(8,128)(2,1)}, u32[]{:S(2)}, u32[]{:S(2)}) async-start(bf16[8,112,1024]{2,1,0:T(8,128)(2,1)} %bitcast.19), calls=%async_computation | async-start | bytes 3670016 | tf_op jit(solution)/shard_map/all_to_all | solution.py:97
  30.3 96.4 %collective-permute-start.2 = (bf16[4,768,1024]{2,1,0:T(8,128)(2,1)}, bf16[4,768,1024]{2,1,0:T(8,128)(2,1)}, u32[]{:S(2)}, u32[]{:S(2)}) collective-permute-start(bf16[4,768,1024]{2,1,0:T(8,128)(2,1)} %bitcast.307), channel_id=1, source_target_pairs={{0,16},{16,0},{1,17},{17,1},{2,18},{18,2},{3,19},{19,3},{4,20},{20... | collective-permute-start | bytes 18874376 | tf_op jit(solution)/shard_map/ppermute | solution.py:14
  72.6 31.5 %collective-permute-start.8 = (bf16[2,8,4,14,768]{4,1,3,2,0:T(8,128)(2,1)S(1)}, bf16[2,8,4,14,768]{4,1,3,2,0:T(8,128)(2,1)S(1)}, u32[]{:S(2)}, u32[]{:S(2)}) collective-permute-start(bf16[2,8,4,14,768]{4,1,3,2,0:T(8,128)(2,1)S(1)} %copy.150), channel_id=1, source_target_pairs={{0,8},{8,0},{1,9},{9,1},{2,10},{10,2},{3,11},{11,3},{4,12},{12,4},... | collective-permute-start | bytes 4128776 | tf_op jit(solution)/shard_map/ppermute | solution.py:115
  109.4 16.1 %collective-permute-start.9 = (bf16[8,4,14,768]{3,0,2,1:T(8,128)(2,1)S(1)}, bf16[8,4,14,768]{3,0,2,1:T(8,128)(2,1)S(1)}, u32[]{:S(2)}, u32[]{:S(2)}) collective-permute-start(bf16[8,4,14,768]{3,0,2,1:T(8,128)(2,1)S(1)} %copy.153), channel_id=1, source_target_pairs={{0,8},{8,0},{1,9},{9,1},{2,10},{10,2},{3,11},{11,3},{4,12},{12,4},... | collective-permute-start | bytes 2064392 | tf_op jit(solution)/shard_map/ppermute | solution.py:125
  133.4 4.4 %copy-start.6 = (bf16[1,2048,32]{1,2,0:T(8,128)(2,1)S(1)}, bf16[1,2048,32]{1,2,0:T(8,128)(2,1)}, u32[]{:S(2)}) copy-start(bf16[1,2048,32]{1,2,0:T(8,128)(2,1)} %param.11) | copy-start | bytes 393220
  133.4 4.4 %copy-start.10 = (f32[2048,33]{0,1:T(8,128)S(1)}, f32[2048,33]{0,1:T(8,128)}, u32[]{:S(2)}) copy-start(f32[2048,33]{0,1:T(8,128)} %copy-done.9) | copy-start | bytes 811012
  133.4 46.2 %all-to-all-start.1 = ((bf16[16,56,1024]{2,1,0:T(8,128)(2,1)}), bf16[16,56,1024]{2,1,0:T(8,128)(2,1)S(1)}, u32[]{:S(2)}, u32[]{:S(2)}) async-start(bf16[16,56,1024]{2,1,0:T(8,128)(2,1)} %reshape.213), calls=%async_computation.1 | async-start | bytes 3670016 | tf_op jit(solution)/shard_map/all_to_all | solution.py:136
  181.5 15.6 %copy-start = (bf16[64,2048]{1,0:T(8,128)(2,1)}, bf16[64,2048]{1,0:T(8,128)(2,1)S(1)}, u32[]{:S(2)}) copy-start(bf16[64,2048]{1,0:T(8,128)(2,1)S(1)} %get-tuple-element.39) | copy-start | bytes 786436
  181.5 14.3 %collective-permute-start.10 = (bf16[64,2048]{1,0:T(8,128)(2,1)S(1)}, bf16[64,2048]{1,0:T(8,128)(2,1)S(1)}, u32[]{:S(2)}, u32[]{:S(2)}) collective-permute-start(bf16[64,2048]{1,0:T(8,128)(2,1)S(1)} %get-tuple-element.39), channel_id=1, source_target_pairs={{0,4},{4,0},{1,5},{5,1},{2,6},{6,2},{3,7},{7,3},{8,12},{12,8},{9,1... | collective-permute-start | bytes 786440 | tf_op jit(solution)/shard_map/ppermute | solution.py:51
  242.8 27.1 %collective-permute-start.11 = (bf16[2,8,4,14,768]{4,1,3,2,0:T(8,128)(2,1)S(1)}, bf16[2,8,4,14,768]{4,1,3,2,0:T(8,128)(2,1)S(1)}, u32[]{:S(2)}, u32[]{:S(2)}) collective-permute-start(bf16[2,8,4,14,768]{4,1,3,2,0:T(8,128)(2,1)S(1)} %copy.169), channel_id=1, source_target_pairs={{0,8},{8,0},{1,9},{9,1},{2,10},{10,2},{3,11},{11,3},{4,12},{12,4},... | collective-permute-start | bytes 4128776 | tf_op jit(solution)/shard_map/ppermute | solution.py:115
  277.1 11.0 %collective-permute-start.12 = (bf16[8,4,14,768]{3,0,2,1:T(8,128)(2,1)S(1)}, bf16[8,4,14,768]{3,0,2,1:T(8,128)(2,1)S(1)}, u32[]{:S(2)}, u32[]{:S(2)}) collective-permute-start(bf16[8,4,14,768]{3,0,2,1:T(8,128)(2,1)S(1)} %copy.172), channel_id=1, source_target_pairs={{0,8},{8,0},{1,9},{9,1},{2,10},{10,2},{3,11},{11,3},{4,12},{12,4},... | collective-permute-start | bytes 2064392 | tf_op jit(solution)/shard_map/ppermute | solution.py:125
  297.6 4.4 %copy-start.11 = (f32[2048,33]{0,1:T(8,128)S(1)}, f32[2048,33]{0,1:T(8,128)}, u32[]{:S(2)}) copy-start(f32[2048,33]{0,1:T(8,128)} %copy-done.9) | copy-start | bytes 811012
  297.7 38.1 %all-to-all-start.3 = ((bf16[16,56,1024]{2,1,0:T(8,128)(2,1)}), bf16[16,56,1024]{2,1,0:T(8,128)(2,1)S(1)}, u32[]{:S(2)}, u32[]{:S(2)}) async-start(bf16[16,56,1024]{2,1,0:T(8,128)(2,1)} %reshape.214), calls=%async_computation.3 | async-start | bytes 3670016 | tf_op jit(solution)/shard_map/all_to_all | solution.py:136
  339.7 10.2 %all-to-all-start.4 = ((f32[32,1,2]{2,1,0:T(1,128)}), f32[32,1,2]{2,1,0:T(1,128)S(1)}, u32[]{:S(2)}, u32[]{:S(2)}) async-start(f32[32,1,2]{2,1,0:T(1,128)} %broadcast_in_dim.28), calls=%async_computation.4 | async-start | bytes 32768 | tf_op jit(solution)/shard_map/all_to_all | solution.py:195
  342.8 7.7 %collective-permute-start.13 = (bf16[64,1024]{1,0:T(8,128)(2,1)S(1)}, bf16[64,1024]{1,0:T(8,128)(2,1)S(1)}, u32[]{:S(2)}, u32[]{:S(2)}) collective-permute-start(bf16[64,1024]{1,0:T(8,128)(2,1)S(1)} %get-tuple-element.34), channel_id=1, source_target_pairs={{0,16},{16,0},{1,17},{17,1},{2,18},{18,2},{3,19},{19,3},{4,20},{20... | collective-permute-start | bytes 393224 | tf_op jit(solution)/shard_map/ppermute | solution.py:14
  (6 other events, 23.3 us)

commit v7 on v6

--- a/solution.py
+++ b/solution.py
@@ -162,7 +162,6 @@
     block_capacity = (7 * BLOCK * TOP + 6 * experts_count - 1) // (6 * experts_count)
     capacity = block_capacity * (piece // BLOCK)
     own_weights = (w_gate[0], w_up[0], w_down[0])
-    other_weights = tuple(other_section(w) for w in own_weights)
     own_small = (norm_gain[0], router[0])
     packed = jnp.concatenate([own_small[0][:, None], own_small[1].astype(jnp.float32)], axis=1)
     other_packed = other_section(packed)
@@ -173,6 +172,8 @@
     diagonal_routes = lax.ppermute(
         own_routes, ("section", "zhalf"), [(0, 3), (3, 0), (1, 2), (2, 1)]
     )
+    held = lax.optimization_barrier((own_weights, section_routes, half_routes, diagonal_routes))
+    other_weights = tuple(other_section(w) for w in held[0])
     hidden = lax.dynamic_slice_in_dim(tokens, section_index * piece, piece, 0)
     squares = []
     for layer in range(sections):

time: 352 us -> 352 us (level)
  no operation moved by 1% of the time
where the time goes in v7:
time: 352 us; the launch traced here: 351 us
  waiting for transfers between devices  203 us (58%)
  matrix products  63 us (18%)
  blocking collectives  29.2 us (8%)
  starting transfers between devices  28.8 us (8%)
  local copies, waits for them, and re-layouts  16.4 us (5%)
  other arithmetic  9.4 us (3%)
    all_to_all x2, waiting for transfers between devices, expert_layer(): lax.all_to_all(sending.reshape(sources, group_slots, chunk), ('fsdp', 'zh...  74.4 us
    ppermute x2, waiting for transfers between devices, expert_layer(): lax.ppermute(outgoing_pair, 'fsdp', ring_pairs(fsdp_count, shift))  46.4 us
    all_to_all x1, waiting for transfers between devices, expert_layer(): arrived = lax.all_to_all(outgoing, ('fsdp', 'inner'), 0, 0, tiled=True)  29.3 us
    all_to_all x1, blocking collectives, expert_layer(): arrived = lax.all_to_all(outgoing, ('fsdp', 'inner'), 0, 0, tiled=True)  29.2 us
    ppermute x2, waiting for transfers between devices, expert_layer(): lax.ppermute(inner_act, 'fsdp', ring_pairs(fsdp_count, shift))  25.8 us
    dot_general x4, matrix products, gate_and_up(): jnp.einsum('sjcd,jdh->sjch', rows_in, up_w, preferred_element_type=jnp.fl...  23 us
    dot_general x4, matrix products, gate_and_up(): jnp.einsum('sjcd,jdh->sjch', rows_in, gate_w, preferred_element_type=jnp....  22.1 us
    ppermute x3, waiting for transfers between devices, other_half(): return lax.ppermute(value, 'zhalf', [(0, 1), (1, 0)])  14.3 us
  transfers between devices with their start and end apart: 18, of which 11 were waited for; matrix products, arithmetic and copies ran while one was open for 12% of the time, Pallas kernels for 0%

profile of v7, /device:TPU:0, one launch (start us, length us, event | category | flops | bytes accessed | tf_op | source)
XLA Modules:
  0.0 351.2 jit_solution(8447565453939605025)
XLA Ops:
  11.6 6.3 %collective-permute-done.3 = s32[128,6]{1,0:T(8,128)S(1)} collective-permute-done((s32[128,6]{1,0:T(8,128)S(1)}, s32[128,6]{1,0:T(8,128)S(1)}, u32[]{:S(2)}, u32[]{:S(2)}) %collective-permute-start.3) | collective-permute-done | bytes 3104 | tf_op jit(solution)/shard_map/ppermute | solution.py:172
  25.8 4.5 %all-to-all-start = ((bf16[8,112,1024]{2,1,0:T(8,128)(2,1)}), bf16[8,112,1024]{2,1,0:T(8,128)(2,1)}, u32[]{:S(2)}, u32[]{:S(2)}) async-start(bf16[8,112,1024]{2,1,0:T(8,128)(2,1)} %bitcast.20), calls=%async_computation | async-start | bytes 3670016 | tf_op jit(solution)/shard_map/all_to_all | solution.py:97
  30.5 29.3 %all-to-all-done = bf16[8,112,1024]{2,1,0:T(8,128)(2,1)} async-done(((bf16[8,112,1024]{2,1,0:T(8,128)(2,1)}), bf16[8,112,1024]{2,1,0:T(8,128)(2,1)}, u32[]{:S(2)}, u32[]{:S(2)}) %all-to-all-start) | async-done | bytes 1835040 | tf_op jit(solution)/shard_map/all_to_all | solution.py:97
  62.6 4.6 %fusion.54 = bf16[1,8,4,14,768]{4,3,1,2,0:T(8,128)(2,1)S(1)} fusion(bf16[4,1024,768]{2,1,0:T(8,128)(2,1)} %collective-permute-done.7, pred[]{:T(512)S(6)} %eq.86, bf16[1,8,4,14,1024]{4,3,2,1,0:T(8,128)(2,1)S(1)} %get-tuple-element.27, bf16[1,4,1024,768]{3,2,1,0:T(8,128)(2,1)} %param.13), kind=kOutput, calls=%fused_computation.64 | convolution fusion | flops 708132864 | bytes 14188545 | tf_op jit(solution)/shard_map/sjcd,jdh->sjch/dot_general | solution.py:106
  67.3 4.6 %fusion.57 = bf16[1,8,4,14,768]{4,3,1,2,0:T(8,128)(2,1)S(1)} fusion(bf16[4,1024,768]{2,1,0:T(8,128)(2,1)} %collective-permute-done.5, pred[]{:T(512)S(6)} %eq.86, bf16[1,8,4,14,1024]{4,3,2,1,0:T(8,128)(2,1)S(1)} %get-tuple-element.27, bf16[1,4,1024,768]{3,2,1,0:T(8,128)(2,1)} %param.12), kind=kOutput, calls=%fused_computation.65 | convolution fusion | flops 708132864 | bytes 14188545 | tf_op jit(solution)/shard_map/sjcd,jdh->sjch/dot_general | solution.py:103
  73.2 4.6 %fusion.18 = f32[4,768,8,14]{1,3,2,0:T(8,128)S(1)} fusion(bf16[4,1024,768]{2,1,0:T(8,128)(2,1)} %collective-permute-done.5, pred[]{:T(512)S(6)} %eq.86, bf16[1,8,4,14,1024]{4,3,2,1,0:T(8,128)(2,1)S(1)} %get-tuple-element.28, bf16[1,4,1024,768]{3,2,1,0:T(8,128)(2,1)} %param.12), kind=kOutput, calls=%fused_computation.20 | convolution fusion | flops 707788800 | bytes 14876673 | tf_op jit(solution)/shard_map/sjcd,jdh->sjch/dot_general | solution.py:103
  77.8 26.3 %collective-permute-done.8 = bf16[2,8,4,14,768]{4,1,3,2,0:T(8,128)(2,1)S(1)} collective-permute-done((bf16[2,8,4,14,768]{4,1,3,2,0:T(8,128)(2,1)S(1)}, bf16[2,8,4,14,768]{4,1,3,2,0:T(8,128)(2,1)S(1)}, u32[]{:S(2)}, u32[]{:S(2)}) %collective-permute-start.8) | collective-permute-done | bytes 1376288 | tf_op jit(solution)/shard_map/ppermute | solution.py:115
  104.2 5.0 %fusion.33 = bf16[8,4,14,768]{3,2,0,1:T(8,128)(2,1)S(1)} fusion(f32[4,768,8,14]{1,3,2,0:T(8,128)S(1)} %fusion.18, bf16[1,8,4,14,768]{4,1,3,2,0:T(8,128)(2,1)S(1)} %get-tuple-element.32, bf16[1,8,4,14,768]{4,1,3,2,0:T(8,128)(2,1)S(1)} %get-tuple-element.31, bf16[1,8,4,14,1024]{4,3,2,1,0:T(8,128)(2,1)S(1)} %get-tuple-element.28, ...), kind=kOutput, calls=%fused_computation.48 | convolution fusion | flops 711229440 | bytes 16941056 | tf_op jit(solution)/shard_map/sjcd,jdh->sjch/dot_general | solution.py:106
  110.1 15.4 %collective-permute-done.9 = bf16[8,4,14,768]{3,0,2,1:T(8,128)(2,1)S(1)} collective-permute-done((bf16[8,4,14,768]{3,0,2,1:T(8,128)(2,1)S(1)}, bf16[8,4,14,768]{3,0,2,1:T(8,128)(2,1)S(1)}, u32[]{:S(2)}, u32[]{:S(2)}) %collective-permute-start.9) | collective-permute-done | bytes 688160 | tf_op jit(solution)/shard_map/ppermute | solution.py:125
  126.7 4.7 %convert_bitcast_fusion.1 = bf16[2,2,4,4,14,1024]{5,4,1,2,0,3:T(8,128)(2,1)S(1)} fusion(bf16[4,768,1024]{2,1,0:T(8,128)(2,1)} %collective-permute-done.4, pred[]{:T(512)S(6)} %eq.86, bf16[2,4,2,4,14,768]{5,4,2,1,3,0:T(8,128)(2,1)S(1)} %bitcast.290, bf16[1,4,768,1024]{3,2,1,0:T(8,128)(2,1)} %param.14), kind=kOutput, calls=%fused_computation.35 | convolution fusion | flops 1413349376 | bytes 15794177 | tf_op jit(solution)/shard_map/fipjch,jhd->fpijcd/dot_general | solution.py:133
  133.4 4.3 %all-to-all-start.1 = ((bf16[16,56,1024]{2,1,0:T(8,128)(2,1)}), bf16[16,56,1024]{2,1,0:T(8,128)(2,1)S(1)}, u32[]{:S(2)}, u32[]{:S(2)}) async-start(bf16[16,56,1024]{2,1,0:T(8,128)(2,1)} %reshape.213), calls=%async_computation.1 | async-start | bytes 3670016 | tf_op jit(solution)/shard_map/all_to_all | solution.py:136
  138.4 41.2 %all-to-all-done.1 = bf16[16,56,1024]{2,1,0:T(8,128)(2,1)S(1)} async-done(((bf16[16,56,1024]{2,1,0:T(8,128)(2,1)}), bf16[16,56,1024]{2,1,0:T(8,128)(2,1)S(1)}, u32[]{:S(2)}, u32[]{:S(2)}) %all-to-all-start.1) | async-done | bytes 1835040 | tf_op jit(solution)/shard_map/all_to_all | solution.py:136
  183.4 12.4 %collective-permute-done.10 = bf16[64,2048]{1,0:T(8,128)(2,1)S(1)} collective-permute-done((bf16[64,2048]{1,0:T(8,128)(2,1)S(1)}, bf16[64,2048]{1,0:T(8,128)(2,1)S(1)}, u32[]{:S(2)}, u32[]{:S(2)}) %collective-permute-start.10) | collective-permute-done | bytes 262176 | tf_op jit(solution)/shard_map/ppermute | solution.py:51
  197.3 29.2 %all_to_all.26 = bf16[8,112,1024]{2,1,0:T(8,128)(2,1)} all-to-all(bf16[8,112,1024]{2,1,0:T(8,128)(2,1)S(1)} %bitcast.279), channel_id=1, replica_groups=mesh['section'=2,'fsdp'=2,'zhalf'=2,'inner'=4] {'fsdp','inner'}, dimensions={0} | all-to-all | bytes 3670016 | tf_op jit(solution)/shard_map/all_to_all | solution.py:97
  229.2 6.5 %fusion.51 = bf16[1,8,4,14,768]{4,3,1,2,0:T(8,128)(2,1)S(1)} fusion(bf16[4,1024,768]{2,1,0:T(8,128)(2,1)} %collective-permute-done.5, pred[]{:T(512)S(6)} %eq.196, bf16[1,8,4,14,1024]{4,3,2,1,0:T(8,128)(2,1)S(1)} %get-tuple-element.25, bf16[1,4,1024,768]{3,2,1,0:T(8,128)(2,1)} %param.12), kind=kOutput, calls=%fused_computation.63 | convolution fusion | flops 708132864 | bytes 14188545 | tf_op jit(solution)/shard_map/sjcd,jdh->sjch/dot_general | solution.py:103
  235.7 6.5 %fusion.48 = bf16[1,8,4,14,768]{4,3,1,2,0:T(8,128)(2,1)S(1)} fusion(bf16[4,1024,768]{2,1,0:T(8,128)(2,1)} %collective-permute-done.7, pred[]{:T(512)S(6)} %eq.196, bf16[1,8,4,14,1024]{4,3,2,1,0:T(8,128)(2,1)S(1)} %get-tuple-element.25, bf16[1,4,1024,768]{3,2,1,0:T(8,128)(2,1)} %param.13), kind=kOutput, calls=%fused_computation.62 | convolution fusion | flops 708132864 | bytes 14188545 | tf_op jit(solution)/shard_map/sjcd,jdh->sjch/dot_general | solution.py:106
  243.4 6.4 %fusion.10 = f32[4,768,8,14]{1,3,2,0:T(8,128)S(1)} fusion(bf16[4,1024,768]{2,1,0:T(8,128)(2,1)} %collective-permute-done.5, pred[]{:T(512)S(6)} %eq.196, bf16[1,8,4,14,1024]{4,3,2,1,0:T(8,128)(2,1)S(1)} %get-tuple-element.26, bf16[1,4,1024,768]{3,2,1,0:T(8,128)(2,1)} %param.12), kind=kOutput, calls=%fused_computation.12 | convolution fusion | flops 707788800 | bytes 14876673 | tf_op jit(solution)/shard_map/sjcd,jdh->sjch/dot_general | solution.py:103
  249.8 20.1 %collective-permute-done.11 = bf16[2,8,4,14,768]{4,1,3,2,0:T(8,128)(2,1)S(1)} collective-permute-done((bf16[2,8,4,14,768]{4,1,3,2,0:T(8,128)(2,1)S(1)}, bf16[2,8,4,14,768]{4,1,3,2,0:T(8,128)(2,1)S(1)}, u32[]{:S(2)}, u32[]{:S(2)}) %collective-permute-start.11) | collective-permute-done | bytes 1376288 | tf_op jit(solution)/shard_map/ppermute | solution.py:115
  270.0 6.9 %fusion.31 = bf16[8,4,14,768]{3,2,0,1:T(8,128)(2,1)S(1)} fusion(f32[4,768,8,14]{1,3,2,0:T(8,128)S(1)} %fusion.10, bf16[1,8,4,14,768]{4,1,3,2,0:T(8,128)(2,1)S(1)} %get-tuple-element.30, bf16[1,8,4,14,768]{4,1,3,2,0:T(8,128)(2,1)S(1)} %get-tuple-element.29, bf16[1,8,4,14,1024]{4,3,2,1,0:T(8,128)(2,1)S(1)} %get-tuple-element.26, ...), kind=kOutput, calls=%fused_computation.44 | convolution fusion | flops 711229440 | bytes 16941056 | tf_op jit(solution)/shard_map/sjcd,jdh->sjch/dot_general | solution.py:106
  277.7 10.4 %collective-permute-done.12 = bf16[8,4,14,768]{3,0,2,1:T(8,128)(2,1)S(1)} collective-permute-done((bf16[8,4,14,768]{3,0,2,1:T(8,128)(2,1)S(1)}, bf16[8,4,14,768]{3,0,2,1:T(8,128)(2,1)S(1)}, u32[]{:S(2)}, u32[]{:S(2)}) %collective-permute-start.12) | collective-permute-done | bytes 688160 | tf_op jit(solution)/shard_map/ppermute | solution.py:125
  289.3 6.5 %convert_bitcast_fusion = bf16[2,2,4,4,14,1024]{5,4,1,2,0,3:T(8,128)(2,1)S(1)} fusion(bf16[4,768,1024]{2,1,0:T(8,128)(2,1)} %collective-permute-done.4, pred[]{:T(512)S(6)} %eq.196, bf16[2,4,2,4,14,768]{5,4,2,1,3,0:T(8,128)(2,1)S(1)} %bitcast.291, bf16[1,4,768,1024]{3,2,1,0:T(8,128)(2,1)} %param.14), kind=kOutput, calls=%fused_computation.34 | convolution fusion | flops 1413349376 | bytes 15794177 | tf_op jit(solution)/shard_map/fipjch,jhd->fpijcd/dot_general | solution.py:133
  297.7 4.2 %all-to-all-start.3 = ((bf16[16,56,1024]{2,1,0:T(8,128)(2,1)}), bf16[16,56,1024]{2,1,0:T(8,128)(2,1)S(1)}, u32[]{:S(2)}, u32[]{:S(2)}) async-start(bf16[16,56,1024]{2,1,0:T(8,128)(2,1)} %reshape.214), calls=%async_computation.3 | async-start | bytes 3670016 | tf_op jit(solution)/shard_map/all_to_all | solution.py:136
  302.6 33.2 %all-to-all-done.3 = bf16[16,56,1024]{2,1,0:T(8,128)(2,1)S(1)} async-done(((bf16[16,56,1024]{2,1,0:T(8,128)(2,1)}), bf16[16,56,1024]{2,1,0:T(8,128)(2,1)S(1)}, u32[]{:S(2)}, u32[]{:S(2)}) %all-to-all-start.3) | async-done | bytes 1835040 | tf_op jit(solution)/shard_map/all_to_all | solution.py:136
  343.1 6.7 %all-to-all-done.4 = f32[32,1,2]{2,1,0:T(1,128)S(1)} async-done(((f32[32,1,2]{2,1,0:T(1,128)}), f32[32,1,2]{2,1,0:T(1,128)S(1)}, u32[]{:S(2)}, u32[]{:S(2)}) %all-to-all-start.4) | async-done | bytes 288 | tf_op jit(solution)/shard_map/all_to_all | solution.py:196
  (139 shorter events, 50.1 us)
Async XLA Ops:
  1.4 10.1 %collective-permute-start.2 = (s32[128,6]{1,0:T(8,128)S(1)}, s32[128,6]{1,0:T(8,128)S(1)}, u32[]{:S(2)}, u32[]{:S(2)}) collective-permute-start(s32[128,6]{1,0:T(8,128)S(1)} %bitcast.296), channel_id=1, source_target_pairs={{0,4},{4,0},{1,5},{5,1},{2,6},{6,2},{3,7},{7,3},{8,12},{12,8},{9,1... | collective-permute-start | bytes 9224 | tf_op jit(solution)/shard_map/ppermute | solution.py:51
  5.5 12.3 %collective-permute-start.3 = (s32[128,6]{1,0:T(8,128)S(1)}, s32[128,6]{1,0:T(8,128)S(1)}, u32[]{:S(2)}, u32[]{:S(2)}) collective-permute-start(s32[128,6]{1,0:T(8,128)S(1)} %bitcast.297), channel_id=1, source_target_pairs={{0,20},{20,0},{4,16},{16,4},{1,21},{21,1},{5,17},{17,5},{2,22},{22... | collective-permute-start | bytes 9224 | tf_op jit(solution)/shard_map/ppermute | solution.py:172
  5.5 13.0 %collective-permute-start = (s32[128,6]{1,0:T(8,128)S(1)}, s32[128,6]{1,0:T(8,128)S(1)}, u32[]{:S(2)}, u32[]{:S(2)}) collective-permute-start(s32[128,6]{1,0:T(8,128)S(1)} %bitcast.298), channel_id=1, source_target_pairs={{0,16},{16,0},{1,17},{17,1},{2,18},{18,2},{3,19},{19,3},{4,20},{20... | collective-permute-start | bytes 9224 | tf_op jit(solution)/shard_map/ppermute | solution.py:14
  6.8 16.3 %copy-start.8 = (f32[1,2048]{1,0:T(1,128)S(1)}, f32[1,2048]{1,0:T(1,128)}, u32[]{:S(2)}) copy-start(f32[1,2048]{1,0:T(1,128)} %param.10) | copy-start | bytes 24580
  6.9 16.1 %collective-permute-start.6 = (bf16[64,2048]{1,0:T(8,128)(2,1)S(1)}, bf16[64,2048]{1,0:T(8,128)(2,1)S(1)}, u32[]{:S(2)}, u32[]{:S(2)}) collective-permute-start(bf16[64,2048]{1,0:T(8,128)(2,1)S(1)} %get-tuple-element.24), channel_id=1, source_target_pairs={{0,4},{4,0},{1,5},{5,1},{2,6},{6,2},{3,7},{7,3},{8,12},{12,8},{9,1... | collective-permute-start | bytes 786440 | tf_op jit(solution)/shard_map/ppermute | solution.py:51
  11.4 11.7 %collective-permute-start.1 = (f32[2048,33]{0,1:T(8,128)S(1)}, f32[2048,33]{0,1:T(8,128)S(1)}, u32[]{:S(2)}, u32[]{:S(2)}) collective-permute-start(f32[2048,33]{0,1:T(8,128)S(1)} %pad_maximum_fusion.6), channel_id=1, source_target_pairs={{0,16},{16,0},{1,17},{17,1},{2,18},{18,2},{3,19},{19,3},{4,20},{20... | collective-permute-start | bytes 811016 | tf_op jit(solution)/shard_map/ppermute | solution.py:14
  18.6 4.6 %copy-start.2 = (s32[64,6]{1,0:T(8,128)}, s32[64,6]{1,0:T(8,128)S(1)}, u32[]{:S(2)}) copy-start(s32[64,6]{1,0:T(8,128)S(1)} %get-tuple-element.41) | copy-start | bytes 4612
  18.8 43.8 %collective-permute-start.7 = (bf16[4,1024,768]{2,1,0:T(8,128)(2,1)}, bf16[4,1024,768]{2,1,0:T(8,128)(2,1)}, u32[]{:S(2)}, u32[]{:S(2)}) collective-permute-start(bf16[4,1024,768]{2,1,0:T(8,128)(2,1)} %bitcast.306), channel_id=1, source_target_pairs={{0,16},{16,0},{1,17},{17,1},{2,18},{18,2},{3,19},{19,3},{4,20},{20... | collective-permute-start | bytes 18874376 | tf_op jit(solution)/shard_map/ppermute | solution.py:14
  20.3 46.9 %collective-permute-start.5 = (bf16[4,1024,768]{2,1,0:T(8,128)(2,1)}, bf16[4,1024,768]{2,1,0:T(8,128)(2,1)}, u32[]{:S(2)}, u32[]{:S(2)}) collective-permute-start(bf16[4,1024,768]{2,1,0:T(8,128)(2,1)} %bitcast.305), channel_id=1, source_target_pairs={{0,16},{16,0},{1,17},{17,1},{2,18},{18,2},{3,19},{19,3},{4,20},{20... | collective-permute-start | bytes 18874376 | tf_op jit(solution)/shard_map/ppermute | solution.py:14
  25.8 34.0 %all-to-all-start = ((bf16[8,112,1024]{2,1,0:T(8,128)(2,1)}), bf16[8,112,1024]{2,1,0:T(8,128)(2,1)}, u32[]{:S(2)}, u32[]{:S(2)}) async-start(bf16[8,112,1024]{2,1,0:T(8,128)(2,1)} %bitcast.20), calls=%async_computation | async-start | bytes 3670016 | tf_op jit(solution)/shard_map/all_to_all | solution.py:97
  30.3 96.4 %collective-permute-start.4 = (bf16[4,768,1024]{2,1,0:T(8,128)(2,1)}, bf16[4,768,1024]{2,1,0:T(8,128)(2,1)}, u32[]{:S(2)}, u32[]{:S(2)}) collective-permute-start(bf16[4,768,1024]{2,1,0:T(8,128)(2,1)} %bitcast.307), channel_id=1, source_target_pairs={{0,16},{16,0},{1,17},{17,1},{2,18},{18,2},{3,19},{19,3},{4,20},{20... | collective-permute-start | bytes 18874376 | tf_op jit(solution)/shard_map/ppermute | solution.py:14
  72.6 31.5 %collective-permute-start.8 = (bf16[2,8,4,14,768]{4,1,3,2,0:T(8,128)(2,1)S(1)}, bf16[2,8,4,14,768]{4,1,3,2,0:T(8,128)(2,1)S(1)}, u32[]{:S(2)}, u32[]{:S(2)}) collective-permute-start(bf16[2,8,4,14,768]{4,1,3,2,0:T(8,128)(2,1)S(1)} %copy.150), channel_id=1, source_target_pairs={{0,8},{8,0},{1,9},{9,1},{2,10},{10,2},{3,11},{11,3},{4,12},{12,4},... | collective-permute-start | bytes 4128776 | tf_op jit(solution)/shard_map/ppermute | solution.py:115
  109.4 16.1 %collective-permute-start.9 = (bf16[8,4,14,768]{3,0,2,1:T(8,128)(2,1)S(1)}, bf16[8,4,14,768]{3,0,2,1:T(8,128)(2,1)S(1)}, u32[]{:S(2)}, u32[]{:S(2)}) collective-permute-start(bf16[8,4,14,768]{3,0,2,1:T(8,128)(2,1)S(1)} %copy.153), channel_id=1, source_target_pairs={{0,8},{8,0},{1,9},{9,1},{2,10},{10,2},{3,11},{11,3},{4,12},{12,4},... | collective-permute-start | bytes 2064392 | tf_op jit(solution)/shard_map/ppermute | solution.py:125
  133.4 4.4 %copy-start.6 = (bf16[1,2048,32]{1,2,0:T(8,128)(2,1)S(1)}, bf16[1,2048,32]{1,2,0:T(8,128)(2,1)}, u32[]{:S(2)}) copy-start(bf16[1,2048,32]{1,2,0:T(8,128)(2,1)} %param.11) | copy-start | bytes 393220
  133.4 4.4 %copy-start.10 = (f32[2048,33]{0,1:T(8,128)S(1)}, f32[2048,33]{0,1:T(8,128)}, u32[]{:S(2)}) copy-start(f32[2048,33]{0,1:T(8,128)} %copy-done.9) | copy-start | bytes 811012
  133.4 46.2 %all-to-all-start.1 = ((bf16[16,56,1024]{2,1,0:T(8,128)(2,1)}), bf16[16,56,1024]{2,1,0:T(8,128)(2,1)S(1)}, u32[]{:S(2)}, u32[]{:S(2)}) async-start(bf16[16,56,1024]{2,1,0:T(8,128)(2,1)} %reshape.213), calls=%async_computation.1 | async-start | bytes 3670016 | tf_op jit(solution)/shard_map/all_to_all | solution.py:136
  181.5 15.6 %copy-start = (bf16[64,2048]{1,0:T(8,128)(2,1)}, bf16[64,2048]{1,0:T(8,128)(2,1)S(1)}, u32[]{:S(2)}) copy-start(bf16[64,2048]{1,0:T(8,128)(2,1)S(1)} %get-tuple-element.45) | copy-start | bytes 786436
  181.5 14.3 %collective-permute-start.10 = (bf16[64,2048]{1,0:T(8,128)(2,1)S(1)}, bf16[64,2048]{1,0:T(8,128)(2,1)S(1)}, u32[]{:S(2)}, u32[]{:S(2)}) collective-permute-start(bf16[64,2048]{1,0:T(8,128)(2,1)S(1)} %get-tuple-element.45), channel_id=1, source_target_pairs={{0,4},{4,0},{1,5},{5,1},{2,6},{6,2},{3,7},{7,3},{8,12},{12,8},{9,1... | collective-permute-start | bytes 786440 | tf_op jit(solution)/shard_map/ppermute | solution.py:51
  242.8 27.1 %collective-permute-start.11 = (bf16[2,8,4,14,768]{4,1,3,2,0:T(8,128)(2,1)S(1)}, bf16[2,8,4,14,768]{4,1,3,2,0:T(8,128)(2,1)S(1)}, u32[]{:S(2)}, u32[]{:S(2)}) collective-permute-start(bf16[2,8,4,14,768]{4,1,3,2,0:T(8,128)(2,1)S(1)} %copy.169), channel_id=1, source_target_pairs={{0,8},{8,0},{1,9},{9,1},{2,10},{10,2},{3,11},{11,3},{4,12},{12,4},... | collective-permute-start | bytes 4128776 | tf_op jit(solution)/shard_map/ppermute | solution.py:115
  277.1 11.0 %collective-permute-start.12 = (bf16[8,4,14,768]{3,0,2,1:T(8,128)(2,1)S(1)}, bf16[8,4,14,768]{3,0,2,1:T(8,128)(2,1)S(1)}, u32[]{:S(2)}, u32[]{:S(2)}) collective-permute-start(bf16[8,4,14,768]{3,0,2,1:T(8,128)(2,1)S(1)} %copy.172), channel_id=1, source_target_pairs={{0,8},{8,0},{1,9},{9,1},{2,10},{10,2},{3,11},{11,3},{4,12},{12,4},... | collective-permute-start | bytes 2064392 | tf_op jit(solution)/shard_map/ppermute | solution.py:125
  297.6 4.4 %copy-start.11 = (f32[2048,33]{0,1:T(8,128)S(1)}, f32[2048,33]{0,1:T(8,128)}, u32[]{:S(2)}) copy-start(f32[2048,33]{0,1:T(8,128)} %copy-done.9) | copy-start | bytes 811012
  297.7 38.1 %all-to-all-start.3 = ((bf16[16,56,1024]{2,1,0:T(8,128)(2,1)}), bf16[16,56,1024]{2,1,0:T(8,128)(2,1)S(1)}, u32[]{:S(2)}, u32[]{:S(2)}) async-start(bf16[16,56,1024]{2,1,0:T(8,128)(2,1)} %reshape.214), calls=%async_computation.3 | async-start | bytes 3670016 | tf_op jit(solution)/shard_map/all_to_all | solution.py:136
  339.7 10.2 %all-to-all-start.4 = ((f32[32,1,2]{2,1,0:T(1,128)}), f32[32,1,2]{2,1,0:T(1,128)S(1)}, u32[]{:S(2)}, u32[]{:S(2)}) async-start(f32[32,1,2]{2,1,0:T(1,128)} %broadcast_in_dim.28), calls=%async_computation.4 | async-start | bytes 32768 | tf_op jit(solution)/shard_map/all_to_all | solution.py:196
  342.8 7.7 %collective-permute-start.13 = (bf16[64,1024]{1,0:T(8,128)(2,1)S(1)}, bf16[64,1024]{1,0:T(8,128)(2,1)S(1)}, u32[]{:S(2)}, u32[]{:S(2)}) collective-permute-start(bf16[64,1024]{1,0:T(8,128)(2,1)S(1)} %get-tuple-element.40), channel_id=1, source_target_pairs={{0,16},{16,0},{1,17},{17,1},{2,18},{18,2},{3,19},{19,3},{4,20},{20... | collective-permute-start | bytes 393224 | tf_op jit(solution)/shard_map/ppermute | solution.py:14
  (6 other events, 23.3 us)

commit v8 on v6

--- a/solution.py
+++ b/solution.py
@@ -178,7 +178,12 @@
     for layer in range(sections):
         mine = section_index == layer
         gain_row, router_weight = [jnp.where(mine, a, b) for a, b in zip(own_small, other_small)]
-        weights = tuple(jnp.where(mine, a, b) for a, b in zip(own_weights, other_weights))
+        pairs = (own_weights, other_weights)
+        if layer > 0:
+            pairs = lax.optimization_barrier((own_weights, other_weights, hidden))[:2]
+        weights = tuple(jnp.where(mine, a, b) for a, b in zip(*pairs))
+        if layer > 0:
+            weights = lax.optimization_barrier(weights)
         route_all = jnp.where(mine, own_routes, section_routes)
         partner_all = jnp.where(mine, half_routes, diagonal_routes)
         route_rows = lax.dynamic_slice_in_dim(route_all, section_index * piece, piece, 0)

time: 352 us -> 360 us (1.023)
  waiting for transfers between devices: 203 us -> 239 us
  blocking collectives: 29.2 us -> 0 us
  matrix products: 63 us -> 38.3 us
  other arithmetic: 9.44 us -> 27.6 us
  starting transfers between devices: 28.7 us -> 32.8 us
    all_to_all x1 -> x0, blocking collectives: 29.2 us -> none  [expert_layer(): arrived = lax.all_to_all(outgoing, ('fsdp', 'inner'), 0, 0, tiled=True)]
    select_n x0 -> x2, other arithmetic: none -> 16.9 us  [body(): weights = tuple((jnp.where(mine, a, b) for a, b in zip(*pairs)))]
    dot_general x4, matrix products: 22.1 us -> 8.21 us  [gate_and_up(): jnp.einsum('sjcd,jdh->sjch', rows_in, gate_w, preferred_element_type=jnp....]
    all_to_all x1 -> x2, waiting for transfers between devices: 29.3 us -> 41.8 us  [expert_layer(): arrived = lax.all_to_all(outgoing, ('fsdp', 'inner'), 0, 0, tiled=True)]
    ppermute x2, waiting for transfers between devices: 46.4 us -> 57.2 us  [expert_layer(): lax.ppermute(outgoing_pair, 'fsdp', ring_pairs(fsdp_count, shift))]
    dot_general x4, matrix products: 23 us -> 14.1 us  [gate_and_up(): jnp.einsum('sjcd,jdh->sjch', rows_in, up_w, preferred_element_type=jnp.fl...]
    all_to_all x2, waiting for transfers between devices: 74.4 us -> 81.5 us  [expert_layer(): lax.all_to_all(sending.reshape(sources, group_slots, chunk), ('fsdp', 'zh...]
    ppermute x3, waiting for transfers between devices: 14.8 us -> 21 us  [other_half(): return lax.ppermute(value, 'zhalf', [(0, 1), (1, 0)])]
  transfers between devices with their start and end apart: 18 -> 19, of which waited for: 11 -> 12; matrix products, arithmetic and copies ran while one was open for 12% -> 14% of each run, Pallas kernels for 0% -> 0%
where the time goes in v8:
time: 360 us; the launch traced here: 359 us
  waiting for transfers between devices  239 us (66%)
  matrix products  38.3 us (11%)
  starting transfers between devices  32.8 us (9%)
  other arithmetic  27.6 us (8%)
  local copies, waits for them, and re-layouts  19.8 us (6%)
    all_to_all x2, waiting for transfers between devices, expert_layer(): lax.all_to_all(sending.reshape(sources, group_slots, chunk), ('fsdp', 'zh...  81.5 us
    ppermute x2, waiting for transfers between devices, expert_layer(): lax.ppermute(outgoing_pair, 'fsdp', ring_pairs(fsdp_count, shift))  57.2 us
    all_to_all x2, waiting for transfers between devices, expert_layer(): arrived = lax.all_to_all(outgoing, ('fsdp', 'inner'), 0, 0, tiled=True)  41.8 us
    ppermute x2, waiting for transfers between devices, expert_layer(): lax.ppermute(inner_act, 'fsdp', ring_pairs(fsdp_count, shift))  31.3 us
    ppermute x3, waiting for transfers between devices, other_half(): return lax.ppermute(value, 'zhalf', [(0, 1), (1, 0)])  21 us
    select_n x2, other arithmetic, body(): weights = tuple((jnp.where(mine, a, b) for a, b in zip(*pairs)))  16.9 us
    dot_general x4, matrix products, gate_and_up(): jnp.einsum('sjcd,jdh->sjch', rows_in, up_w, preferred_element_type=jnp.fl...  14.1 us
    dot_general x2, matrix products, expert_layer(): jnp.einsum('fipjch,jhd->fpijcd', inner_all, down_w, preferred_element_typ...  9.35 us
  transfers between devices with their start and end apart: 19, of which 12 were waited for; matrix products, arithmetic and copies ran while one was open for 14% of the time, Pallas kernels for 0%

profile of v8, /device:TPU:0, one launch (start us, length us, event | category | flops | bytes accessed | tf_op | source)
XLA Modules:
  0.0 359.4 jit_solution(6089482231748115596)
XLA Ops:
  1.4 3.6 collective-permute-start.6
  11.8 6.1 %collective-permute-done.5 = s32[128,6]{1,0:T(8,128)S(1)} collective-permute-done((s32[128,6]{1,0:T(8,128)S(1)}, s32[128,6]{1,0:T(8,128)S(1)}, u32[]{:S(2)}, u32[]{:S(2)}) %collective-permute-start.5) | collective-permute-done | bytes 3104 | tf_op jit(solution)/shard_map/ppermute | solution.py:51
  26.1 4.5 %all-to-all-start = ((bf16[8,112,1024]{2,1,0:T(8,128)(2,1)}), bf16[8,112,1024]{2,1,0:T(8,128)(2,1)}, u32[]{:S(2)}, u32[]{:S(2)}) async-start(bf16[8,112,1024]{2,1,0:T(8,128)(2,1)} %bitcast.19), calls=%async_computation | async-start | bytes 3670016 | tf_op jit(solution)/shard_map/all_to_all | solution.py:97
  30.7 29.0 %all-to-all-done = bf16[8,112,1024]{2,1,0:T(8,128)(2,1)} async-done(((bf16[8,112,1024]{2,1,0:T(8,128)(2,1)}), bf16[8,112,1024]{2,1,0:T(8,128)(2,1)}, u32[]{:S(2)}, u32[]{:S(2)}) %all-to-all-start) | async-done | bytes 1835040 | tf_op jit(solution)/shard_map/all_to_all | solution.py:97
  63.5 5.0 %fusion.46 = bf16[1,8,4,14,768]{4,3,1,2,0:T(8,128)(2,1)S(1)} fusion(bf16[4,1024,768]{2,1,0:T(8,128)(2,1)} %collective-permute-done.7, pred[]{:T(512)S(6)} %eq.86, bf16[1,8,4,14,1024]{4,3,2,1,0:T(8,128)(2,1)S(1)} %get-tuple-element.39, bf16[1,4,1024,768]{3,2,1,0:T(8,128)(2,1)} %param.13), kind=kOutput, calls=%fused_computation.61 | convolution fusion | flops 708132864 | bytes 14188545 | tf_op jit(solution)/shard_map/sjcd,jdh->sjch/dot_general | solution.py:106
  72.7 4.4 %fusion.18 = f32[4,768,8,14]{1,3,2,0:T(8,128)} fusion(bf16[4,1024,768]{2,1,0:T(8,128)(2,1)} %collective-permute-done.3, pred[]{:T(512)S(6)} %eq.86, bf16[1,8,4,14,1024]{4,3,2,1,0:T(8,128)(2,1)} %get-tuple-element.40, bf16[1,4,1024,768]{3,2,1,0:T(8,128)(2,1)S(1)} %bitcast.261), kind=kOutput, calls=%fused_computation.20 | convolution fusion | flops 707788800 | bytes 14876673 | tf_op jit(solution)/shard_map/sjcd,jdh->sjch/dot_general | solution.py:103
  77.0 26.0 %collective-permute-done.8 = bf16[2,8,4,14,768]{4,1,3,2,0:T(8,128)(2,1)S(1)} collective-permute-done((bf16[2,8,4,14,768]{4,1,3,2,0:T(8,128)(2,1)}, bf16[2,8,4,14,768]{4,1,3,2,0:T(8,128)(2,1)S(1)}, u32[]{:S(2)}, u32[]{:S(2)}) %collective-permute-start.8) | collective-permute-done | bytes 1376288 | tf_op jit(solution)/shard_map/ppermute | solution.py:115
  104.0 3.8 %fusion.31 = bf16[8,4,14,768]{3,2,0,1:T(8,128)(2,1)S(1)} fusion(f32[4,768,8,14]{1,3,2,0:T(8,128)} %fusion.18, bf16[1,8,4,14,768]{4,1,3,2,0:T(8,128)(2,1)} %get-tuple-element.44, bf16[1,8,4,14,768]{4,1,3,2,0:T(8,128)(2,1)S(1)} %get-tuple-element.43, bf16[1,8,4,14,1024]{4,3,2,1,0:T(8,128)(2,1)S(1)} %copy-done.2, ...), kind=kOutput, calls=%fused_computation.47 | convolution fusion | flops 711229440 | bytes 16941056 | tf_op jit(solution)/shard_map/sjcd,jdh->sjch/dot_general | solution.py:106
  108.6 14.7 %collective-permute-done.9 = bf16[8,4,14,768]{3,0,2,1:T(8,128)(2,1)S(1)} collective-permute-done((bf16[8,4,14,768]{3,0,2,1:T(8,128)(2,1)S(1)}, bf16[8,4,14,768]{3,0,2,1:T(8,128)(2,1)S(1)}, u32[]{:S(2)}, u32[]{:S(2)}) %collective-permute-start.9) | collective-permute-done | bytes 688160 | tf_op jit(solution)/shard_map/ppermute | solution.py:125
  124.6 4.7 %convert_bitcast_fusion.1 = bf16[2,2,4,4,14,1024]{5,4,1,2,0,3:T(8,128)(2,1)S(1)} fusion(bf16[4,768,1024]{2,1,0:T(8,128)(2,1)} %collective-permute-done.2, pred[]{:T(512)S(6)} %eq.86, bf16[2,4,2,4,14,768]{5,4,2,1,3,0:T(8,128)(2,1)S(1)} %bitcast.283, bf16[1,4,768,1024]{3,2,1,0:T(8,128)(2,1)} %param.14), kind=kOutput, calls=%fused_computation.34 | convolution fusion | flops 1413349376 | bytes 15794177 | tf_op jit(solution)/shard_map/fipjch,jhd->fpijcd/dot_general | solution.py:133
  131.2 4.9 %all-to-all-start.1 = ((bf16[16,56,1024]{2,1,0:T(8,128)(2,1)}), bf16[16,56,1024]{2,1,0:T(8,128)(2,1)S(1)}, u32[]{:S(2)}, u32[]{:S(2)}) async-start(bf16[16,56,1024]{2,1,0:T(8,128)(2,1)} %reshape.213), calls=%async_computation.1 | async-start | bytes 3670016 | tf_op jit(solution)/shard_map/all_to_all | solution.py:136
  136.9 40.3 %all-to-all-done.1 = bf16[16,56,1024]{2,1,0:T(8,128)(2,1)S(1)} async-done(((bf16[16,56,1024]{2,1,0:T(8,128)(2,1)}), bf16[16,56,1024]{2,1,0:T(8,128)(2,1)S(1)}, u32[]{:S(2)}, u32[]{:S(2)}) %all-to-all-start.1) | async-done | bytes 1835040 | tf_op jit(solution)/shard_map/all_to_all | solution.py:136
  180.6 12.2 %collective-permute-done.10 = bf16[64,2048]{1,0:T(8,128)(2,1)S(1)} collective-permute-done((bf16[64,2048]{1,0:T(8,128)(2,1)S(1)}, bf16[64,2048]{1,0:T(8,128)(2,1)S(1)}, u32[]{:S(2)}, u32[]{:S(2)}) %collective-permute-start.10) | collective-permute-done | bytes 262176 | tf_op jit(solution)/shard_map/ppermute | solution.py:51
  195.5 4.5 %all-to-all-start.2 = ((bf16[8,112,1024]{2,1,0:T(8,128)(2,1)}), bf16[8,112,1024]{2,1,0:T(8,128)(2,1)}, u32[]{:S(2)}, u32[]{:S(2)}) async-start(bf16[8,112,1024]{2,1,0:T(8,128)(2,1)} %bitcast.54), calls=%async_computation.2 | async-start | bytes 3670016 | tf_op jit(solution)/shard_map/all_to_all | solution.py:97
  199.9 6.2 %broadcast_select_fusion = bf16[4,768,1024]{2,1,0:T(8,128)(2,1)} fusion(bf16[4,768,1024]{2,1,0:T(8,128)(2,1)} %bitcast.274, bf16[4,768,1024]{2,1,0:T(8,128)(2,1)} %collective-permute-done.2, pred[]{:T(512)S(6)} %eq.196), kind=kLoop, calls=%fused_computation.23 | loop fusion | flops 3145728 | bytes 18874368 | tf_op jit(solution)/shard_map/jit(_where)/select_n | solution.py:184
  206.1 10.7 %broadcast_select_fusion.1 = (bf16[4,1024,768]{2,1,0:T(8,128)(2,1)}, bf16[4,1024,768]{2,1,0:T(8,128)(2,1)}) fusion(bf16[4,1024,768]{2,1,0:T(8,128)(2,1)} %bitcast.266, bf16[4,1024,768]{2,1,0:T(8,128)(2,1)} %collective-permute-done.7, pred[]{:T(512)S(6)} %eq.196, bf16[4,1024,768]{2,1,0:T(8,128)(2,1)S(1)} %bitcast.264, ...), kind=kLoop, calls=%fused_computation.24 | loop fusion | flops 6291456 | bytes 37748736 | tf_op jit(solution)/shard_map/jit(_where)/select_n | solution.py:184
  216.9 12.8 %all-to-all-done.2 = bf16[8,112,1024]{2,1,0:T(8,128)(2,1)} async-done(((bf16[8,112,1024]{2,1,0:T(8,128)(2,1)}), bf16[8,112,1024]{2,1,0:T(8,128)(2,1)}, u32[]{:S(2)}, u32[]{:S(2)}) %all-to-all-start.2) | async-done | bytes 1835040 | tf_op jit(solution)/shard_map/all_to_all | solution.py:97
  232.5 3.9 %fusion.52 = bf16[1,8,4,14,768]{4,3,1,2,0:T(8,128)(2,1)S(1)} fusion(bf16[4,1024,768]{2,1,0:T(8,128)(2,1)} %get-tuple-element.20, bf16[1,8,4,14,1024]{4,3,2,1,0:T(8,128)(2,1)S(1)} %get-tuple-element.37), kind=kOutput, calls=%fused_computation.63 | convolution fusion | flops 704987136 | bytes 7897088 | tf_op jit(solution)/shard_map/sjcd,jdh->sjch/dot_general | solution.py:106
  240.3 31.2 %collective-permute-done.11 = bf16[2,8,4,14,768]{4,1,3,2,0:T(8,128)(2,1)S(1)} collective-permute-done((bf16[2,8,4,14,768]{4,1,3,2,0:T(8,128)(2,1)S(1)}, bf16[2,8,4,14,768]{4,1,3,2,0:T(8,128)(2,1)S(1)}, u32[]{:S(2)}, u32[]{:S(2)}) %collective-permute-start.11) | collective-permute-done | bytes 1376288 | tf_op jit(solution)/shard_map/ppermute | solution.py:115
  273.8 16.6 %collective-permute-done.12 = bf16[8,4,14,768]{3,0,2,1:T(8,128)(2,1)S(1)} collective-permute-done((bf16[8,4,14,768]{3,0,2,1:T(8,128)(2,1)S(1)}, bf16[8,4,14,768]{3,0,2,1:T(8,128)(2,1)S(1)}, u32[]{:S(2)}, u32[]{:S(2)}) %collective-permute-start.12) | collective-permute-done | bytes 688160 | tf_op jit(solution)/shard_map/ppermute | solution.py:125
  291.6 4.6 %convert_bitcast_fusion = bf16[2,2,4,4,14,1024]{5,4,1,2,0,3:T(8,128)(2,1)S(1)} fusion(bf16[4,768,1024]{2,1,0:T(8,128)(2,1)} %broadcast_select_fusion, bf16[2,4,2,4,14,768]{5,4,2,1,3,0:T(8,128)(2,1)S(1)} %bitcast.284), kind=kOutput, calls=%fused_computation.33 | convolution fusion | flops 1410203648 | bytes 9502720 | tf_op jit(solution)/shard_map/fipjch,jhd->fpijcd/dot_general | solution.py:133
  297.9 3.9 %all-to-all-start.3 = ((bf16[16,56,1024]{2,1,0:T(8,128)(2,1)}), bf16[16,56,1024]{2,1,0:T(8,128)(2,1)S(1)}, u32[]{:S(2)}, u32[]{:S(2)}) async-start(bf16[16,56,1024]{2,1,0:T(8,128)(2,1)} %reshape.214), calls=%async_computation.3 | async-start | bytes 3670016 | tf_op jit(solution)/shard_map/all_to_all | solution.py:136
  302.5 41.2 %all-to-all-done.3 = bf16[16,56,1024]{2,1,0:T(8,128)(2,1)S(1)} async-done(((bf16[16,56,1024]{2,1,0:T(8,128)(2,1)}), bf16[16,56,1024]{2,1,0:T(8,128)(2,1)S(1)}, u32[]{:S(2)}, u32[]{:S(2)}) %all-to-all-start.3) | async-done | bytes 1835040 | tf_op jit(solution)/shard_map/all_to_all | solution.py:136
  351.2 6.7 %all-to-all-done.4 = f32[32,1,2]{2,1,0:T(1,128)S(1)} async-done(((f32[32,1,2]{2,1,0:T(1,128)}), f32[32,1,2]{2,1,0:T(1,128)S(1)}, u32[]{:S(2)}, u32[]{:S(2)}) %all-to-all-start.4) | async-done | bytes 288 | tf_op jit(solution)/shard_map/all_to_all | solution.py:200
  (170 shorter events, 56.6 us)
Async XLA Ops:
  1.4 9.8 %collective-permute-start.6 = (s32[128,6]{1,0:T(8,128)S(1)}, s32[128,6]{1,0:T(8,128)S(1)}, u32[]{:S(2)}, u32[]{:S(2)}) collective-permute-start(s32[128,6]{1,0:T(8,128)S(1)} %bitcast.289), channel_id=1, source_target_pairs={{0,20},{20,0},{4,16},{16,4},{1,21},{21,1},{5,17},{17,5},{2,22},{22... | collective-permute-start | bytes 9224 | tf_op jit(solution)/shard_map/ppermute | solution.py:173
  5.0 12.9 %collective-permute-start.5 = (s32[128,6]{1,0:T(8,128)S(1)}, s32[128,6]{1,0:T(8,128)S(1)}, u32[]{:S(2)}, u32[]{:S(2)}) collective-permute-start(s32[128,6]{1,0:T(8,128)S(1)} %bitcast.290), channel_id=1, source_target_pairs={{0,4},{4,0},{1,5},{5,1},{2,6},{6,2},{3,7},{7,3},{8,12},{12,8},{9,1... | collective-permute-start | bytes 9224 | tf_op jit(solution)/shard_map/ppermute | solution.py:51
  5.6 12.9 %collective-permute-start = (s32[128,6]{1,0:T(8,128)S(1)}, s32[128,6]{1,0:T(8,128)S(1)}, u32[]{:S(2)}, u32[]{:S(2)}) collective-permute-start(s32[128,6]{1,0:T(8,128)S(1)} %bitcast.291), channel_id=1, source_target_pairs={{0,16},{16,0},{1,17},{17,1},{2,18},{18,2},{3,19},{19,3},{4,20},{20... | collective-permute-start | bytes 9224 | tf_op jit(solution)/shard_map/ppermute | solution.py:14
  6.8 16.5 %collective-permute-start.4 = (bf16[64,2048]{1,0:T(8,128)(2,1)S(1)}, bf16[64,2048]{1,0:T(8,128)(2,1)S(1)}, u32[]{:S(2)}, u32[]{:S(2)}) collective-permute-start(bf16[64,2048]{1,0:T(8,128)(2,1)S(1)} %get-tuple-element.36), channel_id=1, source_target_pairs={{0,4},{4,0},{1,5},{5,1},{2,6},{6,2},{3,7},{7,3},{8,12},{12,8},{9,1... | collective-permute-start | bytes 786440 | tf_op jit(solution)/shard_map/ppermute | solution.py:51
  11.1 12.3 %collective-permute-start.1 = (f32[2048,33]{0,1:T(8,128)S(1)}, f32[2048,33]{0,1:T(8,128)S(1)}, u32[]{:S(2)}, u32[]{:S(2)}) collective-permute-start(f32[2048,33]{0,1:T(8,128)S(1)} %pad_maximum_fusion.6), channel_id=1, source_target_pairs={{0,16},{16,0},{1,17},{17,1},{2,18},{18,2},{3,19},{19,3},{4,20},{20... | collective-permute-start | bytes 811016 | tf_op jit(solution)/shard_map/ppermute | solution.py:14
  11.3 52.2 %collective-permute-start.7 = (bf16[4,1024,768]{2,1,0:T(8,128)(2,1)}, bf16[4,1024,768]{2,1,0:T(8,128)(2,1)}, u32[]{:S(2)}, u32[]{:S(2)}) collective-permute-start(bf16[4,1024,768]{2,1,0:T(8,128)(2,1)} %bitcast.265), channel_id=1, source_target_pairs={{0,16},{16,0},{1,17},{17,1},{2,18},{18,2},{3,19},{19,3},{4,20},{20... | collective-permute-start | bytes 18874376 | tf_op jit(solution)/shard_map/ppermute | solution.py:14
  17.9 50.6 %collective-permute-start.3 = (bf16[4,1024,768]{2,1,0:T(8,128)(2,1)}, bf16[4,1024,768]{2,1,0:T(8,128)(2,1)}, u32[]{:S(2)}, u32[]{:S(2)}) collective-permute-start(bf16[4,1024,768]{2,1,0:T(8,128)(2,1)} %bitcast.259), channel_id=1, source_target_pairs={{0,16},{16,0},{1,17},{17,1},{2,18},{18,2},{3,19},{19,3},{4,20},{20... | collective-permute-start | bytes 18874376 | tf_op jit(solution)/shard_map/ppermute | solution.py:14
  26.1 33.6 %all-to-all-start = ((bf16[8,112,1024]{2,1,0:T(8,128)(2,1)}), bf16[8,112,1024]{2,1,0:T(8,128)(2,1)}, u32[]{:S(2)}, u32[]{:S(2)}) async-start(bf16[8,112,1024]{2,1,0:T(8,128)(2,1)} %bitcast.19), calls=%async_computation | async-start | bytes 3670016 | tf_op jit(solution)/shard_map/all_to_all | solution.py:97
  30.6 94.0 %collective-permute-start.2 = (bf16[4,768,1024]{2,1,0:T(8,128)(2,1)}, bf16[4,768,1024]{2,1,0:T(8,128)(2,1)}, u32[]{:S(2)}, u32[]{:S(2)}) collective-permute-start(bf16[4,768,1024]{2,1,0:T(8,128)(2,1)} %bitcast.273), channel_id=1, source_target_pairs={{0,16},{16,0},{1,17},{17,1},{2,18},{18,2},{3,19},{19,3},{4,20},{20... | collective-permute-start | bytes 18874376 | tf_op jit(solution)/shard_map/ppermute | solution.py:14
  70.6 33.4 %slice-start.4 = ((s8[6291456]{0:T(1024)(128)(4,1)}), s8[4194304]{0:T(1024)(128)(4,1)S(1)}, s32[]{:S(2)}) async-start(s8[6291456]{0:T(1024)(128)(4,1)} %bitcast.267), calls=%async_computation.9 | async-start | bytes 8388608
  72.2 30.9 %collective-permute-start.8 = (bf16[2,8,4,14,768]{4,1,3,2,0:T(8,128)(2,1)}, bf16[2,8,4,14,768]{4,1,3,2,0:T(8,128)(2,1)S(1)}, u32[]{:S(2)}, u32[]{:S(2)}) collective-permute-start(bf16[2,8,4,14,768]{4,1,3,2,0:T(8,128)(2,1)} %copy.150), channel_id=1, source_target_pairs={{0,8},{8,0},{1,9},{9,1},{2,10},{10,2},{3,11},{11,3},{4,12},{12,4},... | collective-permute-start | bytes 4128776 | tf_op jit(solution)/shard_map/ppermute | solution.py:115
  72.7 31.3 %slice-start.5 = ((s8[6291456]{0:T(1024)(128)(4,1)}), s8[2097152]{0:T(1024)(128)(4,1)S(1)}, s32[]{:S(2)}) async-start(s8[6291456]{0:T(1024)(128)(4,1)} %bitcast.267), calls=%async_computation.10 | async-start | bytes 4194304
  77.0 26.9 %copy-start.2 = (bf16[1,8,4,14,1024]{4,3,2,1,0:T(8,128)(2,1)S(1)}, bf16[1,8,4,14,1024]{4,3,2,1,0:T(8,128)(2,1)}, u32[]{:S(2)}) copy-start(bf16[1,8,4,14,1024]{4,3,2,1,0:T(8,128)(2,1)} %get-tuple-element.40) | copy-start | bytes 2752516
  108.0 15.3 %collective-permute-start.9 = (bf16[8,4,14,768]{3,0,2,1:T(8,128)(2,1)S(1)}, bf16[8,4,14,768]{3,0,2,1:T(8,128)(2,1)S(1)}, u32[]{:S(2)}, u32[]{:S(2)}) collective-permute-start(bf16[8,4,14,768]{3,0,2,1:T(8,128)(2,1)S(1)} %copy.153), channel_id=1, source_target_pairs={{0,8},{8,0},{1,9},{9,1},{2,10},{10,2},{3,11},{11,3},{4,12},{12,4},... | collective-permute-start | bytes 2064392 | tf_op jit(solution)/shard_map/ppermute | solution.py:125
  131.2 46.0 %all-to-all-start.1 = ((bf16[16,56,1024]{2,1,0:T(8,128)(2,1)}), bf16[16,56,1024]{2,1,0:T(8,128)(2,1)S(1)}, u32[]{:S(2)}, u32[]{:S(2)}) async-start(bf16[16,56,1024]{2,1,0:T(8,128)(2,1)} %reshape.213), calls=%async_computation.1 | async-start | bytes 3670016 | tf_op jit(solution)/shard_map/all_to_all | solution.py:136
  179.0 13.7 %collective-permute-start.10 = (bf16[64,2048]{1,0:T(8,128)(2,1)S(1)}, bf16[64,2048]{1,0:T(8,128)(2,1)S(1)}, u32[]{:S(2)}, u32[]{:S(2)}) collective-permute-start(bf16[64,2048]{1,0:T(8,128)(2,1)S(1)} %get-tuple-element.57), channel_id=1, source_target_pairs={{0,4},{4,0},{1,5},{5,1},{2,6},{6,2},{3,7},{7,3},{8,12},{12,8},{9,1... | collective-permute-start | bytes 786440 | tf_op jit(solution)/shard_map/ppermute | solution.py:51
  195.5 34.2 %all-to-all-start.2 = ((bf16[8,112,1024]{2,1,0:T(8,128)(2,1)}), bf16[8,112,1024]{2,1,0:T(8,128)(2,1)}, u32[]{:S(2)}, u32[]{:S(2)}) async-start(bf16[8,112,1024]{2,1,0:T(8,128)(2,1)} %bitcast.54), calls=%async_computation.2 | async-start | bytes 3670016 | tf_op jit(solution)/shard_map/all_to_all | solution.py:97
  238.2 33.3 %slice-start.6 = ((s8[6291456]{0:T(1024)(128)(4,1)}), s8[4194304]{0:T(1024)(128)(4,1)S(1)}, s32[]{:S(2)}) async-start(s8[6291456]{0:T(1024)(128)(4,1)} %bitcast.269), calls=%async_computation.11 | async-start | bytes 8388608
  238.7 32.8 %collective-permute-start.11 = (bf16[2,8,4,14,768]{4,1,3,2,0:T(8,128)(2,1)S(1)}, bf16[2,8,4,14,768]{4,1,3,2,0:T(8,128)(2,1)S(1)}, u32[]{:S(2)}, u32[]{:S(2)}) collective-permute-start(bf16[2,8,4,14,768]{4,1,3,2,0:T(8,128)(2,1)S(1)} %copy.169), channel_id=1, source_target_pairs={{0,8},{8,0},{1,9},{9,1},{2,10},{10,2},{3,11},{11,3},{4,12},{12,4},... | collective-permute-start | bytes 4128776 | tf_op jit(solution)/shard_map/ppermute | solution.py:115
  239.3 32.3 %slice-start.7 = ((s8[6291456]{0:T(1024)(128)(4,1)}), s8[2097152]{0:T(1024)(128)(4,1)S(1)}, s32[]{:S(2)}) async-start(s8[6291456]{0:T(1024)(128)(4,1)} %bitcast.269), calls=%async_computation.12 | async-start | bytes 4194304
  273.2 17.2 %collective-permute-start.12 = (bf16[8,4,14,768]{3,0,2,1:T(8,128)(2,1)S(1)}, bf16[8,4,14,768]{3,0,2,1:T(8,128)(2,1)S(1)}, u32[]{:S(2)}, u32[]{:S(2)}) collective-permute-start(bf16[8,4,14,768]{3,0,2,1:T(8,128)(2,1)S(1)} %copy.172), channel_id=1, source_target_pairs={{0,8},{8,0},{1,9},{9,1},{2,10},{10,2},{3,11},{11,3},{4,12},{12,4},... | collective-permute-start | bytes 2064392 | tf_op jit(solution)/shard_map/ppermute | solution.py:125
  297.9 45.8 %all-to-all-start.3 = ((bf16[16,56,1024]{2,1,0:T(8,128)(2,1)}), bf16[16,56,1024]{2,1,0:T(8,128)(2,1)S(1)}, u32[]{:S(2)}, u32[]{:S(2)}) async-start(bf16[16,56,1024]{2,1,0:T(8,128)(2,1)} %reshape.214), calls=%async_computation.3 | async-start | bytes 3670016 | tf_op jit(solution)/shard_map/all_to_all | solution.py:136
  347.5 10.4 %all-to-all-start.4 = ((f32[32,1,2]{2,1,0:T(1,128)}), f32[32,1,2]{2,1,0:T(1,128)S(1)}, u32[]{:S(2)}, u32[]{:S(2)}) async-start(f32[32,1,2]{2,1,0:T(1,128)} %broadcast_in_dim.28), calls=%async_computation.4 | async-start | bytes 32768 | tf_op jit(solution)/shard_map/all_to_all | solution.py:200
  350.9 7.7 %collective-permute-start.13 = (bf16[64,1024]{1,0:T(8,128)(2,1)S(1)}, bf16[64,1024]{1,0:T(8,128)(2,1)S(1)}, u32[]{:S(2)}, u32[]{:S(2)}) collective-permute-start(bf16[64,1024]{1,0:T(8,128)(2,1)S(1)} %get-tuple-element.52), channel_id=1, source_target_pairs={{0,16},{16,0},{1,17},{17,1},{2,18},{18,2},{3,19},{19,3},{4,20},{20... | collective-permute-start | bytes 393224 | tf_op jit(solution)/shard_map/ppermute | solution.py:14
  (18 other events, 109.7 us)

commit v9 on v6

--- a/solution.py
+++ b/solution.py
@@ -143,13 +143,16 @@
     slot_ids = jnp.arange(experts_count * capacity, dtype=jnp.int32)
     hits = positions[:, :, None] == slot_ids[None, None, :]
     combining = jnp.sum(jnp.where(hits, mix_weights[:, :, None], 0.0), axis=1)
-    branch_sum = jnp.einsum(
-        "rs,fsd->rfd",
-        combining,
-        returned.reshape(fsdp_count, experts_count * capacity, chunk).astype(jnp.float32),
-        precision=lax.Precision.HIGHEST,
-        preferred_element_type=jnp.float32,
-    ).reshape(rows, width)
+    outputs_in = returned.reshape(fsdp_count, experts_count * capacity, chunk)
+    branch_sum = jnp.zeros((rows, fsdp_count, chunk), jnp.float32)
+    remainder = combining
+    for _ in range(3):
+        term = remainder.astype(jnp.bfloat16)
+        remainder = remainder - term.astype(jnp.float32)
+        branch_sum = branch_sum + jnp.einsum(
+            "rs,fsd->rfd", term, outputs_in, preferred_element_type=jnp.float32
+        )
+    branch_sum = branch_sum.reshape(rows, width)
     return (entering.astype(jnp.float32) + branch_sum).astype(jnp.bfloat16)
 
 

time: 352 us -> 353 us (level)
  transfers between devices with their start and end apart: 18 -> 18, of which waited for: 11 -> 11; matrix products, arithmetic and copies ran while one was open for 12% -> 11% of each run, Pallas kernels for 0% -> 0%
where the time goes in v9:
time: 353 us; the launch traced here: 352 us
  waiting for transfers between devices  203 us (58%)
  matrix products  62.3 us (18%)
  blocking collectives  29.2 us (8%)
  starting transfers between devices  28.7 us (8%)
  local copies, waits for them, and re-layouts  16 us (5%)
  other arithmetic  11 us (3%)
    all_to_all x2, waiting for transfers between devices, expert_layer(): lax.all_to_all(sending.reshape(sources, group_slots, chunk), ('fsdp', 'zh...  74.4 us
    ppermute x2, waiting for transfers between devices, expert_layer(): lax.ppermute(outgoing_pair, 'fsdp', ring_pairs(fsdp_count, shift))  46.4 us
    all_to_all x1, waiting for transfers between devices, expert_layer(): arrived = lax.all_to_all(outgoing, ('fsdp', 'inner'), 0, 0, tiled=True)  29.3 us
    all_to_all x1, blocking collectives, expert_layer(): arrived = lax.all_to_all(outgoing, ('fsdp', 'inner'), 0, 0, tiled=True)  29.2 us
    ppermute x2, waiting for transfers between devices, expert_layer(): lax.ppermute(inner_act, 'fsdp', ring_pairs(fsdp_count, shift))  25.8 us
    dot_general x4, matrix products, gate_and_up(): jnp.einsum('sjcd,jdh->sjch', rows_in, up_w, preferred_element_type=jnp.fl...  23 us
    dot_general x4, matrix products, gate_and_up(): jnp.einsum('sjcd,jdh->sjch', rows_in, gate_w, preferred_element_type=jnp....  22.1 us
    ppermute x3, waiting for transfers between devices, other_half(): return lax.ppermute(value, 'zhalf', [(0, 1), (1, 0)])  14.8 us
  transfers between devices with their start and end apart: 18, of which 11 were waited for; matrix products, arithmetic and copies ran while one was open for 11% of the time, Pallas kernels for 0%

profile of v9, /device:TPU:0, one launch (start us, length us, event | category | flops | bytes accessed | tf_op | source)
XLA Modules:
  0.0 351.7 jit_solution(2246865229564332414)
XLA Ops:
  12.1 5.8 %collective-permute-done.6 = s32[128,6]{1,0:T(8,128)S(1)} collective-permute-done((s32[128,6]{1,0:T(8,128)S(1)}, s32[128,6]{1,0:T(8,128)S(1)}, u32[]{:S(2)}, u32[]{:S(2)}) %collective-permute-start.6) | collective-permute-done | bytes 3104 | tf_op jit(solution)/shard_map/ppermute | solution.py:176
  25.8 4.5 %all-to-all-start = ((bf16[8,112,1024]{2,1,0:T(8,128)(2,1)}), bf16[8,112,1024]{2,1,0:T(8,128)(2,1)}, u32[]{:S(2)}, u32[]{:S(2)}) async-start(bf16[8,112,1024]{2,1,0:T(8,128)(2,1)} %bitcast.20), calls=%async_computation | async-start | bytes 3670016 | tf_op jit(solution)/shard_map/all_to_all | solution.py:97
  30.5 29.3 %all-to-all-done = bf16[8,112,1024]{2,1,0:T(8,128)(2,1)} async-done(((bf16[8,112,1024]{2,1,0:T(8,128)(2,1)}), bf16[8,112,1024]{2,1,0:T(8,128)(2,1)}, u32[]{:S(2)}, u32[]{:S(2)}) %all-to-all-start) | async-done | bytes 1835040 | tf_op jit(solution)/shard_map/all_to_all | solution.py:97
  62.5 4.6 %fusion.52 = bf16[1,8,4,14,768]{4,3,1,2,0:T(8,128)(2,1)S(1)} fusion(bf16[4,1024,768]{2,1,0:T(8,128)(2,1)} %collective-permute-done.7, pred[]{:T(512)S(6)} %eq.86, bf16[1,8,4,14,1024]{4,3,2,1,0:T(8,128)(2,1)S(1)} %get-tuple-element.24, bf16[1,4,1024,768]{3,2,1,0:T(8,128)(2,1)} %param.13), kind=kOutput, calls=%fused_computation.60 | convolution fusion | flops 708132864 | bytes 14188545 | tf_op jit(solution)/shard_map/sjcd,jdh->sjch/dot_general | solution.py:106
  67.2 4.6 %fusion.55 = bf16[1,8,4,14,768]{4,3,1,2,0:T(8,128)(2,1)S(1)} fusion(bf16[4,1024,768]{2,1,0:T(8,128)(2,1)} %collective-permute-done.3, pred[]{:T(512)S(6)} %eq.86, bf16[1,8,4,14,1024]{4,3,2,1,0:T(8,128)(2,1)S(1)} %get-tuple-element.24, bf16[1,4,1024,768]{3,2,1,0:T(8,128)(2,1)} %param.12), kind=kOutput, calls=%fused_computation.61 | convolution fusion | flops 708132864 | bytes 14188545 | tf_op jit(solution)/shard_map/sjcd,jdh->sjch/dot_general | solution.py:103
  73.1 4.6 %fusion.18 = f32[4,768,8,14]{1,3,2,0:T(8,128)S(1)} fusion(bf16[4,1024,768]{2,1,0:T(8,128)(2,1)} %collective-permute-done.3, pred[]{:T(512)S(6)} %eq.86, bf16[1,8,4,14,1024]{4,3,2,1,0:T(8,128)(2,1)S(1)} %get-tuple-element.25, bf16[1,4,1024,768]{3,2,1,0:T(8,128)(2,1)} %param.12), kind=kOutput, calls=%fused_computation.20 | convolution fusion | flops 707788800 | bytes 14876673 | tf_op jit(solution)/shard_map/sjcd,jdh->sjch/dot_general | solution.py:103
  77.7 26.3 %collective-permute-done.8 = bf16[2,8,4,14,768]{4,1,3,2,0:T(8,128)(2,1)S(1)} collective-permute-done((bf16[2,8,4,14,768]{4,1,3,2,0:T(8,128)(2,1)S(1)}, bf16[2,8,4,14,768]{4,1,3,2,0:T(8,128)(2,1)S(1)}, u32[]{:S(2)}, u32[]{:S(2)}) %collective-permute-start.8) | collective-permute-done | bytes 1376288 | tf_op jit(solution)/shard_map/ppermute | solution.py:115
  104.1 5.0 %fusion.31 = bf16[8,4,14,768]{3,2,0,1:T(8,128)(2,1)S(1)} fusion(f32[4,768,8,14]{1,3,2,0:T(8,128)S(1)} %fusion.18, bf16[1,8,4,14,768]{4,1,3,2,0:T(8,128)(2,1)S(1)} %get-tuple-element.29, bf16[1,8,4,14,768]{4,1,3,2,0:T(8,128)(2,1)S(1)} %get-tuple-element.28, bf16[1,8,4,14,1024]{4,3,2,1,0:T(8,128)(2,1)S(1)} %get-tuple-element.25, ...), kind=kOutput, calls=%fused_computation.44 | convolution fusion | flops 711229440 | bytes 16941056 | tf_op jit(solution)/shard_map/sjcd,jdh->sjch/dot_general | solution.py:106
  110.0 15.4 %collective-permute-done.9 = bf16[8,4,14,768]{3,0,2,1:T(8,128)(2,1)S(1)} collective-permute-done((bf16[8,4,14,768]{3,0,2,1:T(8,128)(2,1)S(1)}, bf16[8,4,14,768]{3,0,2,1:T(8,128)(2,1)S(1)}, u32[]{:S(2)}, u32[]{:S(2)}) %collective-permute-start.9) | collective-permute-done | bytes 688160 | tf_op jit(solution)/shard_map/ppermute | solution.py:125
  126.7 4.7 %convert_bitcast_fusion.1 = bf16[2,2,4,4,14,1024]{5,4,1,2,0,3:T(8,128)(2,1)S(1)} fusion(bf16[4,768,1024]{2,1,0:T(8,128)(2,1)} %collective-permute-done.2, pred[]{:T(512)S(6)} %eq.86, bf16[2,4,2,4,14,768]{5,4,2,1,3,0:T(8,128)(2,1)S(1)} %bitcast.312, bf16[1,4,768,1024]{3,2,1,0:T(8,128)(2,1)} %param.14), kind=kOutput, calls=%fused_computation.31 | convolution fusion | flops 1413349376 | bytes 15794177 | tf_op jit(solution)/shard_map/fipjch,jhd->fpijcd/dot_general | solution.py:133
  133.3 4.3 %all-to-all-start.1 = ((bf16[16,56,1024]{2,1,0:T(8,128)(2,1)}), bf16[16,56,1024]{2,1,0:T(8,128)(2,1)S(1)}, u32[]{:S(2)}, u32[]{:S(2)}) async-start(bf16[16,56,1024]{2,1,0:T(8,128)(2,1)} %reshape.223), calls=%async_computation.1 | async-start | bytes 3670016 | tf_op jit(solution)/shard_map/all_to_all | solution.py:136
  138.4 41.2 %all-to-all-done.1 = bf16[16,56,1024]{2,1,0:T(8,128)(2,1)S(1)} async-done(((bf16[16,56,1024]{2,1,0:T(8,128)(2,1)}), bf16[16,56,1024]{2,1,0:T(8,128)(2,1)S(1)}, u32[]{:S(2)}, u32[]{:S(2)}) %all-to-all-start.1) | async-done | bytes 1835040 | tf_op jit(solution)/shard_map/all_to_all | solution.py:136
  183.6 12.4 %collective-permute-done.10 = bf16[64,2048]{1,0:T(8,128)(2,1)S(1)} collective-permute-done((bf16[64,2048]{1,0:T(8,128)(2,1)S(1)}, bf16[64,2048]{1,0:T(8,128)(2,1)S(1)}, u32[]{:S(2)}, u32[]{:S(2)}) %collective-permute-start.10) | collective-permute-done | bytes 262176 | tf_op jit(solution)/shard_map/ppermute | solution.py:51
  197.5 29.2 %all_to_all.26 = bf16[8,112,1024]{2,1,0:T(8,128)(2,1)} all-to-all(bf16[8,112,1024]{2,1,0:T(8,128)(2,1)S(1)} %bitcast.301), channel_id=1, replica_groups=mesh['section'=2,'fsdp'=2,'zhalf'=2,'inner'=4] {'fsdp','inner'}, dimensions={0} | all-to-all | bytes 3670016 | tf_op jit(solution)/shard_map/all_to_all | solution.py:97
  229.5 6.4 %fusion.49 = bf16[1,8,4,14,768]{4,3,1,2,0:T(8,128)(2,1)S(1)} fusion(bf16[4,1024,768]{2,1,0:T(8,128)(2,1)} %collective-permute-done.3, pred[]{:T(512)S(6)} %eq.196, bf16[1,8,4,14,1024]{4,3,2,1,0:T(8,128)(2,1)S(1)} %get-tuple-element.22, bf16[1,4,1024,768]{3,2,1,0:T(8,128)(2,1)} %param.12), kind=kOutput, calls=%fused_computation.59 | convolution fusion | flops 708132864 | bytes 14188545 | tf_op jit(solution)/shard_map/sjcd,jdh->sjch/dot_general | solution.py:103
  236.0 6.5 %fusion.46 = bf16[1,8,4,14,768]{4,3,1,2,0:T(8,128)(2,1)S(1)} fusion(bf16[4,1024,768]{2,1,0:T(8,128)(2,1)} %collective-permute-done.7, pred[]{:T(512)S(6)} %eq.196, bf16[1,8,4,14,1024]{4,3,2,1,0:T(8,128)(2,1)S(1)} %get-tuple-element.22, bf16[1,4,1024,768]{3,2,1,0:T(8,128)(2,1)} %param.13), kind=kOutput, calls=%fused_computation.58 | convolution fusion | flops 708132864 | bytes 14188545 | tf_op jit(solution)/shard_map/sjcd,jdh->sjch/dot_general | solution.py:106
  243.7 6.4 %fusion.10 = f32[4,768,8,14]{1,3,2,0:T(8,128)S(1)} fusion(bf16[4,1024,768]{2,1,0:T(8,128)(2,1)} %collective-permute-done.3, pred[]{:T(512)S(6)} %eq.196, bf16[1,8,4,14,1024]{4,3,2,1,0:T(8,128)(2,1)S(1)} %get-tuple-element.23, bf16[1,4,1024,768]{3,2,1,0:T(8,128)(2,1)} %param.12), kind=kOutput, calls=%fused_computation.12 | convolution fusion | flops 707788800 | bytes 14876673 | tf_op jit(solution)/shard_map/sjcd,jdh->sjch/dot_general | solution.py:103
  250.2 20.1 %collective-permute-done.11 = bf16[2,8,4,14,768]{4,1,3,2,0:T(8,128)(2,1)S(1)} collective-permute-done((bf16[2,8,4,14,768]{4,1,3,2,0:T(8,128)(2,1)S(1)}, bf16[2,8,4,14,768]{4,1,3,2,0:T(8,128)(2,1)S(1)}, u32[]{:S(2)}, u32[]{:S(2)}) %collective-permute-start.11) | collective-permute-done | bytes 1376288 | tf_op jit(solution)/shard_map/ppermute | solution.py:115
  270.3 6.9 %fusion.29 = bf16[8,4,14,768]{3,2,0,1:T(8,128)(2,1)S(1)} fusion(f32[4,768,8,14]{1,3,2,0:T(8,128)S(1)} %fusion.10, bf16[1,8,4,14,768]{4,1,3,2,0:T(8,128)(2,1)S(1)} %get-tuple-element.27, bf16[1,8,4,14,768]{4,1,3,2,0:T(8,128)(2,1)S(1)} %get-tuple-element.26, bf16[1,8,4,14,1024]{4,3,2,1,0:T(8,128)(2,1)S(1)} %get-tuple-element.23, ...), kind=kOutput, calls=%fused_computation.40 | convolution fusion | flops 711229440 | bytes 16941056 | tf_op jit(solution)/shard_map/sjcd,jdh->sjch/dot_general | solution.py:106
  278.0 10.4 %collective-permute-done.12 = bf16[8,4,14,768]{3,0,2,1:T(8,128)(2,1)S(1)} collective-permute-done((bf16[8,4,14,768]{3,0,2,1:T(8,128)(2,1)S(1)}, bf16[8,4,14,768]{3,0,2,1:T(8,128)(2,1)S(1)}, u32[]{:S(2)}, u32[]{:S(2)}) %collective-permute-start.12) | collective-permute-done | bytes 688160 | tf_op jit(solution)/shard_map/ppermute | solution.py:125
  289.6 6.6 %convert_bitcast_fusion = bf16[2,2,4,4,14,1024]{5,4,1,2,0,3:T(8,128)(2,1)S(1)} fusion(bf16[4,768,1024]{2,1,0:T(8,128)(2,1)} %collective-permute-done.2, pred[]{:T(512)S(6)} %eq.196, bf16[2,4,2,4,14,768]{5,4,2,1,3,0:T(8,128)(2,1)S(1)} %bitcast.313, bf16[1,4,768,1024]{3,2,1,0:T(8,128)(2,1)} %param.14), kind=kOutput, calls=%fused_computation.30 | convolution fusion | flops 1413349376 | bytes 15794177 | tf_op jit(solution)/shard_map/fipjch,jhd->fpijcd/dot_general | solution.py:133
  297.9 4.2 %all-to-all-start.3 = ((bf16[16,56,1024]{2,1,0:T(8,128)(2,1)}), bf16[16,56,1024]{2,1,0:T(8,128)(2,1)S(1)}, u32[]{:S(2)}, u32[]{:S(2)}) async-start(bf16[16,56,1024]{2,1,0:T(8,128)(2,1)} %reshape.224), calls=%async_computation.3 | async-start | bytes 3670016 | tf_op jit(solution)/shard_map/all_to_all | solution.py:136
  302.9 33.2 %all-to-all-done.3 = bf16[16,56,1024]{2,1,0:T(8,128)(2,1)S(1)} async-done(((bf16[16,56,1024]{2,1,0:T(8,128)(2,1)}), bf16[16,56,1024]{2,1,0:T(8,128)(2,1)S(1)}, u32[]{:S(2)}, u32[]{:S(2)}) %all-to-all-start.3) | async-done | bytes 1835040 | tf_op jit(solution)/shard_map/all_to_all | solution.py:136
  343.6 6.7 %all-to-all-done.4 = f32[32,1,2]{2,1,0:T(1,128)S(1)} async-done(((f32[32,1,2]{2,1,0:T(1,128)}), f32[32,1,2]{2,1,0:T(1,128)S(1)}, u32[]{:S(2)}, u32[]{:S(2)}) %all-to-all-start.4) | async-done | bytes 288 | tf_op jit(solution)/shard_map/all_to_all | solution.py:198
  (145 shorter events, 51.0 us)
Async XLA Ops:
  1.4 10.1 %collective-permute-start.5 = (s32[128,6]{1,0:T(8,128)S(1)}, s32[128,6]{1,0:T(8,128)S(1)}, u32[]{:S(2)}, u32[]{:S(2)}) collective-permute-start(s32[128,6]{1,0:T(8,128)S(1)} %bitcast.318), channel_id=1, source_target_pairs={{0,4},{4,0},{1,5},{5,1},{2,6},{6,2},{3,7},{7,3},{8,12},{12,8},{9,1... | collective-permute-start | bytes 9224 | tf_op jit(solution)/shard_map/ppermute | solution.py:51
  5.5 12.3 %collective-permute-start.6 = (s32[128,6]{1,0:T(8,128)S(1)}, s32[128,6]{1,0:T(8,128)S(1)}, u32[]{:S(2)}, u32[]{:S(2)}) collective-permute-start(s32[128,6]{1,0:T(8,128)S(1)} %bitcast.319), channel_id=1, source_target_pairs={{0,20},{20,0},{4,16},{16,4},{1,21},{21,1},{5,17},{17,5},{2,22},{22... | collective-permute-start | bytes 9224 | tf_op jit(solution)/shard_map/ppermute | solution.py:176
  5.5 12.7 %collective-permute-start = (s32[128,6]{1,0:T(8,128)S(1)}, s32[128,6]{1,0:T(8,128)S(1)}, u32[]{:S(2)}, u32[]{:S(2)}) collective-permute-start(s32[128,6]{1,0:T(8,128)S(1)} %bitcast.320), channel_id=1, source_target_pairs={{0,16},{16,0},{1,17},{17,1},{2,18},{18,2},{3,19},{19,3},{4,20},{20... | collective-permute-start | bytes 9224 | tf_op jit(solution)/shard_map/ppermute | solution.py:14
  6.8 16.3 %copy-start.8 = (f32[1,2048]{1,0:T(1,128)S(1)}, f32[1,2048]{1,0:T(1,128)}, u32[]{:S(2)}) copy-start(f32[1,2048]{1,0:T(1,128)} %param.10) | copy-start | bytes 24580
  6.9 16.1 %collective-permute-start.4 = (bf16[64,2048]{1,0:T(8,128)(2,1)S(1)}, bf16[64,2048]{1,0:T(8,128)(2,1)S(1)}, u32[]{:S(2)}, u32[]{:S(2)}) collective-permute-start(bf16[64,2048]{1,0:T(8,128)(2,1)S(1)} %get-tuple-element.21), channel_id=1, source_target_pairs={{0,4},{4,0},{1,5},{5,1},{2,6},{6,2},{3,7},{7,3},{8,12},{12,8},{9,1... | collective-permute-start | bytes 786440 | tf_op jit(solution)/shard_map/ppermute | solution.py:51
  11.4 11.7 %collective-permute-start.1 = (f32[2048,33]{0,1:T(8,128)S(1)}, f32[2048,33]{0,1:T(8,128)S(1)}, u32[]{:S(2)}, u32[]{:S(2)}) collective-permute-start(f32[2048,33]{0,1:T(8,128)S(1)} %pad_maximum_fusion.6), channel_id=1, source_target_pairs={{0,16},{16,0},{1,17},{17,1},{2,18},{18,2},{3,19},{19,3},{4,20},{20... | collective-permute-start | bytes 811016 | tf_op jit(solution)/shard_map/ppermute | solution.py:14
  11.6 51.0 %collective-permute-start.7 = (bf16[4,1024,768]{2,1,0:T(8,128)(2,1)}, bf16[4,1024,768]{2,1,0:T(8,128)(2,1)}, u32[]{:S(2)}, u32[]{:S(2)}) collective-permute-start(bf16[4,1024,768]{2,1,0:T(8,128)(2,1)} %bitcast.328), channel_id=1, source_target_pairs={{0,16},{16,0},{1,17},{17,1},{2,18},{18,2},{3,19},{19,3},{4,20},{20... | collective-permute-start | bytes 18874376 | tf_op jit(solution)/shard_map/ppermute | solution.py:14
  17.9 49.3 %collective-permute-start.3 = (bf16[4,1024,768]{2,1,0:T(8,128)(2,1)}, bf16[4,1024,768]{2,1,0:T(8,128)(2,1)}, u32[]{:S(2)}, u32[]{:S(2)}) collective-permute-start(bf16[4,1024,768]{2,1,0:T(8,128)(2,1)} %bitcast.327), channel_id=1, source_target_pairs={{0,16},{16,0},{1,17},{17,1},{2,18},{18,2},{3,19},{19,3},{4,20},{20... | collective-permute-start | bytes 18874376 | tf_op jit(solution)/shard_map/ppermute | solution.py:14
  18.3 4.9 %copy-start.2 = (s32[64,6]{1,0:T(8,128)}, s32[64,6]{1,0:T(8,128)S(1)}, u32[]{:S(2)}) copy-start(s32[64,6]{1,0:T(8,128)S(1)} %get-tuple-element.39) | copy-start | bytes 4612
  25.8 34.0 %all-to-all-start = ((bf16[8,112,1024]{2,1,0:T(8,128)(2,1)}), bf16[8,112,1024]{2,1,0:T(8,128)(2,1)}, u32[]{:S(2)}, u32[]{:S(2)}) async-start(bf16[8,112,1024]{2,1,0:T(8,128)(2,1)} %bitcast.20), calls=%async_computation | async-start | bytes 3670016 | tf_op jit(solution)/shard_map/all_to_all | solution.py:97
  30.3 96.4 %collective-permute-start.2 = (bf16[4,768,1024]{2,1,0:T(8,128)(2,1)}, bf16[4,768,1024]{2,1,0:T(8,128)(2,1)}, u32[]{:S(2)}, u32[]{:S(2)}) collective-permute-start(bf16[4,768,1024]{2,1,0:T(8,128)(2,1)} %bitcast.329), channel_id=1, source_target_pairs={{0,16},{16,0},{1,17},{17,1},{2,18},{18,2},{3,19},{19,3},{4,20},{20... | collective-permute-start | bytes 18874376 | tf_op jit(solution)/shard_map/ppermute | solution.py:14
  72.5 31.5 %collective-permute-start.8 = (bf16[2,8,4,14,768]{4,1,3,2,0:T(8,128)(2,1)S(1)}, bf16[2,8,4,14,768]{4,1,3,2,0:T(8,128)(2,1)S(1)}, u32[]{:S(2)}, u32[]{:S(2)}) collective-permute-start(bf16[2,8,4,14,768]{4,1,3,2,0:T(8,128)(2,1)S(1)} %copy.131), channel_id=1, source_target_pairs={{0,8},{8,0},{1,9},{9,1},{2,10},{10,2},{3,11},{11,3},{4,12},{12,4},... | collective-permute-start | bytes 4128776 | tf_op jit(solution)/shard_map/ppermute | solution.py:115
  109.3 16.1 %collective-permute-start.9 = (bf16[8,4,14,768]{3,0,2,1:T(8,128)(2,1)S(1)}, bf16[8,4,14,768]{3,0,2,1:T(8,128)(2,1)S(1)}, u32[]{:S(2)}, u32[]{:S(2)}) collective-permute-start(bf16[8,4,14,768]{3,0,2,1:T(8,128)(2,1)S(1)} %copy.134), channel_id=1, source_target_pairs={{0,8},{8,0},{1,9},{9,1},{2,10},{10,2},{3,11},{11,3},{4,12},{12,4},... | collective-permute-start | bytes 2064392 | tf_op jit(solution)/shard_map/ppermute | solution.py:125
  133.3 4.4 %copy-start.6 = (bf16[1,2048,32]{1,2,0:T(8,128)(2,1)S(1)}, bf16[1,2048,32]{1,2,0:T(8,128)(2,1)}, u32[]{:S(2)}) copy-start(bf16[1,2048,32]{1,2,0:T(8,128)(2,1)} %param.11) | copy-start | bytes 393220
  133.3 4.4 %copy-start.10 = (f32[2048,33]{0,1:T(8,128)S(1)}, f32[2048,33]{0,1:T(8,128)}, u32[]{:S(2)}) copy-start(f32[2048,33]{0,1:T(8,128)} %copy-done.9) | copy-start | bytes 811012
  133.3 46.3 %all-to-all-start.1 = ((bf16[16,56,1024]{2,1,0:T(8,128)(2,1)}), bf16[16,56,1024]{2,1,0:T(8,128)(2,1)S(1)}, u32[]{:S(2)}, u32[]{:S(2)}) async-start(bf16[16,56,1024]{2,1,0:T(8,128)(2,1)} %reshape.223), calls=%async_computation.1 | async-start | bytes 3670016 | tf_op jit(solution)/shard_map/all_to_all | solution.py:136
  181.8 15.6 %copy-start = (bf16[64,2048]{1,0:T(8,128)(2,1)}, bf16[64,2048]{1,0:T(8,128)(2,1)S(1)}, u32[]{:S(2)}) copy-start(bf16[64,2048]{1,0:T(8,128)(2,1)S(1)} %get-tuple-element.15) | copy-start | bytes 786436
  181.8 14.3 %collective-permute-start.10 = (bf16[64,2048]{1,0:T(8,128)(2,1)S(1)}, bf16[64,2048]{1,0:T(8,128)(2,1)S(1)}, u32[]{:S(2)}, u32[]{:S(2)}) collective-permute-start(bf16[64,2048]{1,0:T(8,128)(2,1)S(1)} %get-tuple-element.15), channel_id=1, source_target_pairs={{0,4},{4,0},{1,5},{5,1},{2,6},{6,2},{3,7},{7,3},{8,12},{12,8},{9,1... | collective-permute-start | bytes 786440 | tf_op jit(solution)/shard_map/ppermute | solution.py:51
  243.1 27.1 %collective-permute-start.11 = (bf16[2,8,4,14,768]{4,1,3,2,0:T(8,128)(2,1)S(1)}, bf16[2,8,4,14,768]{4,1,3,2,0:T(8,128)(2,1)S(1)}, u32[]{:S(2)}, u32[]{:S(2)}) collective-permute-start(bf16[2,8,4,14,768]{4,1,3,2,0:T(8,128)(2,1)S(1)} %copy.150), channel_id=1, source_target_pairs={{0,8},{8,0},{1,9},{9,1},{2,10},{10,2},{3,11},{11,3},{4,12},{12,4},... | collective-permute-start | bytes 4128776 | tf_op jit(solution)/shard_map/ppermute | solution.py:115
  277.4 11.0 %collective-permute-start.12 = (bf16[8,4,14,768]{3,0,2,1:T(8,128)(2,1)S(1)}, bf16[8,4,14,768]{3,0,2,1:T(8,128)(2,1)S(1)}, u32[]{:S(2)}, u32[]{:S(2)}) collective-permute-start(bf16[8,4,14,768]{3,0,2,1:T(8,128)(2,1)S(1)} %copy.153), channel_id=1, source_target_pairs={{0,8},{8,0},{1,9},{9,1},{2,10},{10,2},{3,11},{11,3},{4,12},{12,4},... | collective-permute-start | bytes 2064392 | tf_op jit(solution)/shard_map/ppermute | solution.py:125
  297.9 4.4 %copy-start.11 = (f32[2048,33]{0,1:T(8,128)S(1)}, f32[2048,33]{0,1:T(8,128)}, u32[]{:S(2)}) copy-start(f32[2048,33]{0,1:T(8,128)} %copy-done.9) | copy-start | bytes 811012
  297.9 38.1 %all-to-all-start.3 = ((bf16[16,56,1024]{2,1,0:T(8,128)(2,1)}), bf16[16,56,1024]{2,1,0:T(8,128)(2,1)S(1)}, u32[]{:S(2)}, u32[]{:S(2)}) async-start(bf16[16,56,1024]{2,1,0:T(8,128)(2,1)} %reshape.224), calls=%async_computation.3 | async-start | bytes 3670016 | tf_op jit(solution)/shard_map/all_to_all | solution.py:136
  340.2 10.2 %all-to-all-start.4 = ((f32[32,1,2]{2,1,0:T(1,128)}), f32[32,1,2]{2,1,0:T(1,128)S(1)}, u32[]{:S(2)}, u32[]{:S(2)}) async-start(f32[32,1,2]{2,1,0:T(1,128)} %broadcast_in_dim.28), calls=%async_computation.4 | async-start | bytes 32768 | tf_op jit(solution)/shard_map/all_to_all | solution.py:198
  343.3 7.7 %collective-permute-start.13 = (bf16[64,1024]{1,0:T(8,128)(2,1)S(1)}, bf16[64,1024]{1,0:T(8,128)(2,1)S(1)}, u32[]{:S(2)}, u32[]{:S(2)}) collective-permute-start(bf16[64,1024]{1,0:T(8,128)(2,1)S(1)} %get-tuple-element.37), channel_id=1, source_target_pairs={{0,16},{16,0},{1,17},{17,1},{2,18},{18,2},{3,19},{19,3},{4,20},{20... | collective-permute-start | bytes 393224 | tf_op jit(solution)/shard_map/ppermute | solution.py:14
  (6 other events, 23.3 us)
